TPU v7x, 32 devices: a whole 2x2x4 slice. The times are simulated.
32 devices in a mesh: cuts: 2 (over x), mode: 16 (over z, y, core).
Axes of the slice: x: 2, y: 2, z: 4, core: 2. Of those that a mesh axis runs over, the one named last changes fastest.
Arguments:
- stem_blocks: bfloat16 [2, 4096, 2, 256], P('cuts', 'mode'), may hold values from -6 to 6
- w1_table: bfloat16 [8, 2, 256, 256], replicated, may hold values from -0.25 to 0.25
- w2_table: bfloat16 [8, 2, 256, 256], replicated, may hold values from -0.125 to 0.125
- slice_ids: int32 [2, 2, 2], P('cuts'), may hold values from 0 to 7, as said below
- mode_perm: int32 [256], replicated, may hold values from 0 to 255, each once
Outputs:
- amplitudes: float32 [256, 16, 2, 256], P('mode', 'cuts')
Inputs may be any that keep to these rules, and one draw needn't show every extreme that they name: For each stem block b, the 2 values slice_ids[:,b,0] are distinct, and so are the 2 values slice_ids[:,b,1]. `mode_perm`: each column appears once.
All inputs are finite; a program needn't handle non-finite values.
Results may differ from a plain program's by a relative error of at most 0.0029.
Values may be sent and summed in bfloat16 or wider, within the bound.
No kernel may reach another device: no remote copies, remote signals or barrier semaphores. Data moves between devices by JAX's collectives and lax.ppermute only.
A program may use at most 64 MiB of HBM per device.

v0:
```python
import jax
import jax.numpy as jnp
from jax import lax
from jax.sharding import PartitionSpec as P


def broadcast(block, axis, source):
    block = jnp.where(lax.axis_index(axis) == source, block, jnp.zeros_like(block))
    return lax.psum(block, axis)


def widen_first(entry):
    real_part, imag_part = (entry[0], entry[1])
    upper = jnp.concatenate([real_part, imag_part], axis=1)
    lower = jnp.concatenate([-imag_part, real_part], axis=1)
    return jnp.concatenate([upper, lower], axis=0)


def widen_second(entry):
    real_part, imag_part = (entry[0], entry[1])
    first_row = jnp.concatenate([real_part, imag_part], axis=1)
    second_row = jnp.concatenate([-imag_part, real_part], axis=1)
    return jnp.stack([first_row, second_row], axis=0)


def second_step(exchanged, weight_two, contract_cols, free_cols):
    block_count, mode_count, piece_rows, _ = exchanged.shape
    pieces = exchanged.reshape(block_count, mode_count, piece_rows, 2, contract_cols, free_cols)
    wide_out = weight_two.shape[3]
    shaped = weight_two.reshape(block_count, 2, mode_count, contract_cols, wide_out)
    return jnp.einsum("nhqpcs,nphco->qso", pieces, shaped, preferred_element_type=jnp.float32)


def on_device(stem_blocks, w1_table, w2_table, slice_ids, mode_perm):
    mode_count = lax.axis_size("mode")
    row_count = stem_blocks.shape[1]
    stem_width = stem_blocks.shape[3]
    mid_width = w1_table.shape[3]
    inner_width = w2_table.shape[2]
    out_width = w2_table.shape[3]
    piece_rows = row_count // mode_count
    contract_cols = inner_width // mode_count
    free_cols = mid_width // contract_cols
    block_count = slice_ids.shape[1]
    first_all = jax.vmap(widen_first)(jnp.take(w1_table, mode_perm, axis=3))
    second_all = jax.vmap(widen_second)(w2_table)
    own_slices = slice_ids[0]
    begin = jnp.zeros((piece_rows, free_cols, 2 * out_width), jnp.float32)

    def one_block(block_index, running):
        stem_part = broadcast(stem_blocks[0], "cuts", block_index)
        slice_pair = own_slices[block_index]
        weight_one = lax.dynamic_index_in_dim(first_all, slice_pair[0], 0, keepdims=False)
        product = jnp.dot(
            stem_part.reshape(row_count, 2 * stem_width),
            weight_one,
            preferred_element_type=jnp.float32,
        ).astype(jnp.bfloat16)
        exchanged = lax.all_to_all(
            product[None, None], "mode", split_axis=2, concat_axis=1, tiled=True
        )
        weight_two = lax.dynamic_index_in_dim(second_all, slice_pair[1], 0, keepdims=True)
        return running + second_step(exchanged, weight_two, contract_cols, free_cols)

    amplitude = lax.fori_loop(0, block_count, one_block, begin)
    summed = lax.psum_scatter(amplitude, "cuts", scatter_dimension=1, tiled=True)
    return summed.reshape(piece_rows, summed.shape[1], 2, out_width)


def solution(mesh):
    placed = (P("cuts", "mode", None, None), P(), P(), P("cuts", None, None), P())
    return jax.shard_map(
        on_device,
        mesh=mesh,
        in_specs=placed,
        out_specs=P("mode", "cuts", None, None),
        check_vma=False,
    )
```

profile of v0, /device:TPU:0, one launch (start us, length us, event | category | flops | bytes accessed | tf_op | source)
XLA Modules:
  0.0 173.1 jit_solution(13787529332660151836)
XLA Ops:
  7.4 3.2 %slice_bitcast_fusion.2 = (bf16[8,256,256]{2,1,0:T(8,128)(2,1)}, bf16[8,256,256]{2,1,0:T(8,128)(2,1)}) fusion(bf16[8,2,256,256]{3,2,1,0:T(8,128)(2,1)} %param.9), kind=kLoop, calls=%fused_computation.19 | loop fusion | bytes 4194304 | tf_op jit(solution)/shard_map/vmap()/squeeze | solution.py:20
  12.6 3.1 %copy.29 = bf16[8,2,256,256]{2,0,3,1:T(8,128)(2,1)} copy(bf16[8,2,256,256]{3,2,1,0:T(8,128)(2,1)S(1)} %copy-done.6) | data formatting | bytes 4194304 | tf_op args[1]
  15.7 2.4 %gather_fusion = bf16[256,8,2,256]{3,1,2,0:T(8,128)(2,1)S(1)} fusion(bf16[8,2,256,256]{2,0,3,1:T(8,128)(2,1)} %copy.29, s32[1024]{0:T(1024)S(1)} %pad_clamp_fusion), kind=kCustom, calls=%fused_computation | custom fusion | bytes 4195328 | tf_op jit(solution)/shard_map/jit(_take)/gather | solution.py:45
  20.2 13.0 %maximum_maximum_fusion = bf16[8,512,512]{1,0,2:T(8,128)(2,1)} fusion(bf16[8,256,256]{1,0,2:T(8,128)(2,1)} %get-tuple-element.171, bf16[8,256,256]{1,0,2:T(8,128)(2,1)S(1)} %fusion.7, bf16[8,256,256]{1,0,2:T(8,128)(2,1)S(1)} %get-tuple-element.170), kind=kLoop, calls=%fused_computation.12 | loop fusion | flops 16777216 | bytes 7340032 | tf_op jit(solution)/shard_map/vmap()/concatenate | solution.py:16
  33.3 7.7 %copy.34 = bf16[8,512,512]{2,1,0:T(8,128)(2,1)} copy(bf16[8,512,512]{1,0,2:T(8,128)(2,1)} %maximum_maximum_fusion) | data formatting | bytes 8388608
  41.0 1.9 %maximum_bitcast_fusion.1 = (bf16[1,8,256,512]{3,2,0,1:T(8,128)(2,1)S(1)}, bf16[1,8,256,512]{3,2,0,1:T(8,128)(2,1)S(1)}) fusion(bf16[8,256,256]{2,1,0:T(8,128)(2,1)S(1)} %copy-done.5, bf16[8,256,256]{2,1,0:T(8,128)(2,1)} %get-tuple-element.169, bf16[8,256,256]{2,1,0:T(8,128)(2,1)S(1)} %copy-done.4), kind=kLoop, calls=%fused_computation.14 | loop fusion | flops 8388608 | bytes 7340032 | tf_op jit(solution)/shard_map/vmap()/stack | solution.py:23
  42.9 2.3 %maximum_bitcast_fusion = bf16[8,2,256,512]{3,2,1,0:T(8,128)(2,1)} fusion(bf16[1,8,256,512]{3,2,0,1:T(8,128)(2,1)S(1)} %get-tuple-element.173, bf16[1,8,256,512]{3,2,0,1:T(8,128)(2,1)S(1)} %get-tuple-element.172), kind=kLoop, calls=%fused_computation.13 | loop fusion | flops 2097152 | bytes 8388608 | tf_op jit(solution)/shard_map/vmap()/transpose | solution.py:46
  45.3 104.0 %while.14 = (s32[]{:T(128)}, f32[16,16,512]{2,1,0:T(8,128)S(1)}, bf16[1,256,2,256]{3,2,1,0:T(2,128)(2,1)S(1)}, s32[2,2]{1,0:T(2,128)S(1)}, bf16[8,512,512]{2,1,0...) while((s32[]{:T(128)}, f32[16,16,512]{2,1,0:T(8,128)S(1)}, ...), condition=%wide.region_2.3_spmd.clone, body=%wide.region_0.0_spmd.clone.sunk | while | flops 269090816 | bytes 11534731 | solution.py:65
  48.9 25.5 %all-reduce.2.cloned.1.call-done = bf16[256,512]{1,0:T(8,128)(2,1)} async-done(((bf16[256,512]{1,0:T(8,128)(2,1)}), bf16[256,512]{1,0:T(8,128)(2,1)}) %all-reduce.2.cloned.1.call-update) | async-done | bytes 262160 | tf_op jit(solution)/shard_map/while/body/eval_jaxpr/psum | solution.py:9
  74.4 1.4 fusion.23
  76.7 2.2 %reduce.6 = bf16[256,512]{1,0:T(8,128)(2,1)S(1)} reduce(bf16[256,1,1,512]{3,2,1,0:T(2,128)(2,1)S(1)} %bitcast.79, bf16[]{:T(256)} %broadcast.40), dimensions={1,2}, to_apply=%bitcast.54.reduce_sub_computation | reduce | bytes 524290 | tf_op jit(solution)/shard_map/while
  79.8 5.6 %all-to-all-start = ((bf16[16,2,4096]{2,1,0:T(2,128)(2,1)}), bf16[16,2,4096]{2,1,0:T(2,128)(2,1)S(1)}, u32[]{:S(2)}, u32[]{:S(2)}) async-start(bf16[16,2,4096]{2,1,0:T(2,128)(2,1)} %reshape.66), calls=%async_computation | async-start | bytes 524288 | tf_op jit(solution)/shard_map/while/body/eval_jaxpr/all_to_all | solution.py:59
  88.6 6.9 %all-to-all-done = bf16[16,2,4096]{2,1,0:T(2,128)(2,1)S(1)} async-done(((bf16[16,2,4096]{2,1,0:T(2,128)(2,1)}), bf16[16,2,4096]{2,1,0:T(2,128)(2,1)S(1)}, u32[]{:S(2)}, u32[]{:S(2)}) %all-to-all-start) | async-done | bytes 262176 | tf_op jit(solution)/shard_map/while/body/eval_jaxpr/all_to_all | solution.py:59
  95.8 1.5 bitcast_reduce_fusion.2
  97.3 1.7 reshape.68
  103.5 20.2 %all-reduce.2.cloned.1.call-done = bf16[256,512]{1,0:T(8,128)(2,1)} async-done(((bf16[256,512]{1,0:T(8,128)(2,1)}), bf16[256,512]{1,0:T(8,128)(2,1)}) %all-reduce.2.cloned.1.call-update) | async-done | bytes 262160 | tf_op jit(solution)/shard_map/while/body/eval_jaxpr/psum | solution.py:9
  123.7 1.4 fusion.23
  126.1 2.2 %reduce.6 = bf16[256,512]{1,0:T(8,128)(2,1)S(1)} reduce(bf16[256,1,1,512]{3,2,1,0:T(2,128)(2,1)S(1)} %bitcast.79, bf16[]{:T(256)} %broadcast.40), dimensions={1,2}, to_apply=%bitcast.54.reduce_sub_computation | reduce | bytes 524290 | tf_op jit(solution)/shard_map/while
  129.2 5.6 %all-to-all-start = ((bf16[16,2,4096]{2,1,0:T(2,128)(2,1)}), bf16[16,2,4096]{2,1,0:T(2,128)(2,1)S(1)}, u32[]{:S(2)}, u32[]{:S(2)}) async-start(bf16[16,2,4096]{2,1,0:T(2,128)(2,1)} %reshape.66), calls=%async_computation | async-start | bytes 524288 | tf_op jit(solution)/shard_map/while/body/eval_jaxpr/all_to_all | solution.py:59
  138.0 6.9 %all-to-all-done = bf16[16,2,4096]{2,1,0:T(2,128)(2,1)S(1)} async-done(((bf16[16,2,4096]{2,1,0:T(2,128)(2,1)}), bf16[16,2,4096]{2,1,0:T(2,128)(2,1)S(1)}, u32[]{:S(2)}, u32[]{:S(2)}) %all-to-all-start) | async-done | bytes 262176 | tf_op jit(solution)/shard_map/while/body/eval_jaxpr/all_to_all | solution.py:59
  145.1 1.5 bitcast_reduce_fusion.2
  146.6 1.7 reshape.68
  150.1 13.7 %reduce-scatter.2.cloned.1.call-done = f32[16,8,512]{2,1,0:T(8,128)} async-done(((f32[16,16,512]{2,1,0:T(8,128)}), f32[16,8,512]{2,1,0:T(8,128)}) %reduce-scatter.2.cloned.1.call-update) | async-done | bytes 262160 | tf_op jit(solution)/shard_map/reduce_scatter | solution.py:66
  163.8 1.8 %reshape.44 = f32[16,8,2,256]{3,2,1,0:T(2,128)} reshape(f32[16,8,512]{2,1,0:T(8,128)} %reduce-scatter.2.cloned.1.call-done) | data formatting | bytes 524288 | tf_op jit(solution)/shard_map/reshape | solution.py:67
  (54 shorter events, 16.4 us)
Async XLA Ops:
  7.4 3.2 %copy-start.3 = (bf16[8,2,256,256]{3,2,1,0:T(8,128)(2,1)S(1)}, bf16[8,2,256,256]{3,2,1,0:T(8,128)(2,1)}, u32[]{:S(2)}) copy-start(bf16[8,2,256,256]{3,2,1,0:T(8,128)(2,1)} %param.9) | copy-start | bytes 6291460
  7.4 4.3 %copy-start.7 = (s32[256]{0:T(256)S(1)}, s32[256]{0:T(256)}, u32[]{:S(2)}) copy-start(s32[256]{0:T(256)} %param.11) | copy-start | bytes 3076
  10.6 2.0 %copy-start.6 = (bf16[8,2,256,256]{3,2,1,0:T(8,128)(2,1)S(1)}, bf16[8,2,256,256]{3,2,1,0:T(8,128)(2,1)}, u32[]{:S(2)}) copy-start(bf16[8,2,256,256]{3,2,1,0:T(8,128)(2,1)} %param.8) | copy-start | bytes 6291460
  33.3 7.7 %copy-start.4 = (bf16[8,256,256]{2,1,0:T(8,128)(2,1)S(1)}, bf16[8,256,256]{2,1,0:T(8,128)(2,1)}, u32[]{:S(2)}) copy-start(bf16[8,256,256]{2,1,0:T(8,128)(2,1)} %fusion.6) | copy-start | bytes 3145732
  33.3 7.7 %copy-start.5 = (bf16[8,256,256]{2,1,0:T(8,128)(2,1)S(1)}, bf16[8,256,256]{2,1,0:T(8,128)(2,1)}, u32[]{:S(2)}) copy-start(bf16[8,256,256]{2,1,0:T(8,128)(2,1)} %get-tuple-element.168) | copy-start | bytes 3145732
  42.9 2.4 %copy-start.1 = (bf16[1,256,2,256]{3,2,1,0:T(2,128)(2,1)S(1)}, bf16[1,256,2,256]{3,2,1,0:T(2,128)(2,1)}, u32[]{:S(2)}) copy-start(bf16[1,256,2,256]{3,2,1,0:T(2,128)(2,1)} %param.7) | copy-start | bytes 786436
  42.9 2.4 %copy-start.8 = (s32[1,2,2]{2,1,0:T(2,128)S(1)}, s32[1,2,2]{2,1,0:T(2,128)}, u32[]{:S(2)}) copy-start(s32[1,2,2]{2,1,0:T(2,128)} %param.10) | copy-start | bytes 52
  45.3 29.1 %all-reduce.2.cloned.1.call-start = ((), (), s32[]{:S(2)}) async-start(), calls=%async_computation.3 | async-start | bytes 524288 | tf_op jit(solution)/shard_map/while/body/eval_jaxpr/psum | solution.py:9
  79.8 15.7 %all-to-all-start = ((bf16[16,2,4096]{2,1,0:T(2,128)(2,1)}), bf16[16,2,4096]{2,1,0:T(2,128)(2,1)S(1)}, u32[]{:S(2)}, u32[]{:S(2)}) async-start(bf16[16,2,4096]{2,1,0:T(2,128)(2,1)} %reshape.66), calls=%async_computation | async-start | bytes 524288 | tf_op jit(solution)/shard_map/while/body/eval_jaxpr/all_to_all | solution.py:59
  99.0 1.0 copy-start.2
  99.9 23.8 %all-reduce.2.cloned.1.call-start = ((), (), s32[]{:S(2)}) async-start(), calls=%async_computation.3 | async-start | bytes 524288 | tf_op jit(solution)/shard_map/while/body/eval_jaxpr/psum | solution.py:9
  129.2 15.7 %all-to-all-start = ((bf16[16,2,4096]{2,1,0:T(2,128)(2,1)}), bf16[16,2,4096]{2,1,0:T(2,128)(2,1)S(1)}, u32[]{:S(2)}, u32[]{:S(2)}) async-start(bf16[16,2,4096]{2,1,0:T(2,128)(2,1)} %reshape.66), calls=%async_computation | async-start | bytes 524288 | tf_op jit(solution)/shard_map/while/body/eval_jaxpr/all_to_all | solution.py:59
  148.3 1.0 copy-start.2
  149.3 0.8 copy-start
  149.3 14.5 %reduce-scatter.2.cloned.1.call-start = ((), (), s32[]{:S(2)}) async-start(), calls=%async_computation.2 | async-start | bytes 786432 | tf_op jit(solution)/shard_map/reduce_scatter | solution.py:66
Sparse Core Ops, SparseCore 0:
  48.5 25.8 all-reduce.1
  103.1 20.5 all-reduce.1
Sparse Core Ops, SparseCore 1:
  152.0 11.8 reduce-scatter.1
where the time goes:
time: 174 us; the launch traced here: 173 us
  waiting for transfers between devices  73.3 us (42%)
  local copies, waits for them, and re-layouts  37 us (21%)
  other arithmetic  24.2 us (14%)
  between operations  14.9 us (9%)
  starting transfers between devices  11.3 us (6%)
  loops' own time  8.19 us (5%)
  matrix products  4.28 us (2%)
    psum x2, waiting for transfers between devices, broadcast(): return lax.psum(block, axis)  45.7 us
    all_to_all x2, waiting for transfers between devices, one_block(): lax.all_to_all(product[None, None], 'mode', split_axis=2, concat_axis=1,...  13.8 us
    reduce_scatter x1, waiting for transfers between devices, on_device(): lax.psum_scatter(amplitude, 'cuts', scatter_dimension=1, tiled=True)  13.7 us
    concatenate x1, other arithmetic, widen_first(): return jnp.concatenate([upper, lower], axis=0)  13 us
    unnamed x18, local copies, waits for them, and re-layouts  12.5 us
    all_to_all x2, starting transfers between devices, one_block(): lax.all_to_all(product[None, None], 'mode', split_axis=2, concat_axis=1,...  11.2 us
    another operation x1, loops' own time, on_device(): amplitude = lax.fori_loop(0, block_count, one_block, begin)  8.19 us
    while x12, local copies, waits for them, and re-layouts  5.23 us
  transfers between devices with their start and end apart: 5, of which 5 were waited for; matrix products, arithmetic and copies ran while one was open for 2% of the time, Pallas kernels for 0%

commit v1 on v0

v1 whole, which is shorter than its diff:
```python
import jax
import jax.numpy as jnp
from jax import lax
from jax.sharding import PartitionSpec as P


def gather_over_cuts(own, n_cuts):
    pieces = [own]
    current = own
    ring = [(j, (j + 1) % n_cuts) for j in range(n_cuts)]
    for _ in range(1, n_cuts):
        current = lax.ppermute(current, "cuts", ring)
        pieces.append(current)
    stacked = jnp.stack(pieces)
    me = lax.axis_index("cuts")
    order = (me - jnp.arange(n_cuts, dtype=jnp.int32)) % n_cuts
    return jnp.take(stacked, order, axis=0)


def blocks_part(stem_rows, first_all, w2_table, first_ids, second_ids, sizes):
    n_mode, t_local, n_cuts, a_count, q_local = sizes
    chunk = stem_rows.shape[0]
    wide_in = stem_rows.shape[2]
    col_width = first_all.shape[2]
    slice_count, _, inner, out_width = w2_table.shape
    first_w = jnp.take(first_all, first_ids, axis=0)
    first_w = jnp.transpose(first_w, (0, 2, 1, 3)).reshape(
        chunk, wide_in, n_cuts * col_width
    )
    product = jnp.einsum(
        "bri,bio->bro", stem_rows, first_w, preferred_element_type=jnp.float32
    ).astype(jnp.bfloat16)
    split = product.reshape(chunk, n_mode, t_local, n_cuts, 2, a_count, q_local)
    real_p, imag_p = split[:, :, :, :, 0], split[:, :, :, :, 1]
    lhs = jnp.stack(
        [
            jnp.stack([real_p, -imag_p]),
            jnp.stack([imag_p, real_p]),
        ]
    )
    lhs = jnp.transpose(lhs, (4, 7, 0, 2, 5, 1, 3, 6)).reshape(
        t_local * q_local * 2, chunk * n_cuts * 2 * inner
    )
    second_w = jnp.take(
        w2_table.reshape(slice_count, 2 * inner, out_width), second_ids, axis=0
    ).reshape(chunk * n_cuts * 2 * inner, out_width)
    return jnp.dot(lhs, second_w, preferred_element_type=jnp.float32)


def on_device(stem_blocks, w1_table, w2_table, slice_ids, mode_perm):
    n_mode = lax.axis_size("mode")
    n_cuts = lax.axis_size("cuts")
    rows = stem_blocks.shape[1]
    width = stem_blocks.shape[3]
    mid = w1_table.shape[3]
    inner = w2_table.shape[2]
    out_width = w2_table.shape[3]
    block_count = slice_ids.shape[1]
    t_local = rows // n_mode
    a_count = inner // n_mode
    q_count = mid // a_count
    q_local = q_count // n_cuts
    me = lax.axis_index("cuts")
    sizes = (n_mode, t_local, n_cuts, a_count, q_local)

    pieces = stem_blocks[0].reshape(1, n_mode, t_local, 2 * width)
    payload = jnp.broadcast_to(pieces, (n_cuts, n_mode, t_local, 2 * width))
    payload = payload.reshape(n_cuts * n_mode, t_local, 2 * width)
    stem_rows = lax.all_to_all(payload, ("cuts", "mode"), 0, 0, tiled=True)
    stem_rows = stem_rows.reshape(block_count, n_mode * t_local, 2 * width)

    all_ids = gather_over_cuts(slice_ids[0], n_cuts)
    first_ids = all_ids[:, :, 0].T
    second_ids = all_ids[:, :, 1].T

    perm_grid = mode_perm.reshape(a_count, q_count)
    wanted = lax.dynamic_slice_in_dim(perm_grid, me * q_local, q_local, axis=1).reshape(-1)
    picker = (jnp.arange(mid, dtype=jnp.int32)[:, None] == wanted[None, :]).astype(w1_table.dtype)
    first_cols = jnp.einsum(
        "spkj,jn->spkn", w1_table, picker, preferred_element_type=jnp.float32
    ).astype(w1_table.dtype)
    real_part, imag_part = first_cols[:, 0], first_cols[:, 1]
    upper = jnp.concatenate([real_part, imag_part], axis=2)
    lower = jnp.concatenate([-imag_part, real_part], axis=2)
    first_all = jnp.concatenate([upper, lower], axis=1)

    if block_count * n_cuts <= 8:
        amplitude = blocks_part(
            stem_rows, first_all, w2_table, first_ids, second_ids.reshape(-1), sizes
        )
    else:
        def one_block(index, running):
            stem_one = lax.dynamic_slice_in_dim(stem_rows, index, 1, axis=0)
            first_one = lax.dynamic_slice_in_dim(first_ids, index, 1, axis=0)
            second_one = lax.dynamic_slice_in_dim(second_ids, index, 1, axis=0)
            return running + blocks_part(
                stem_one, first_all, w2_table, first_one, second_one.reshape(-1), sizes
            )

        begin = jnp.zeros((t_local * q_local * 2, out_width), jnp.float32)
        amplitude = lax.fori_loop(0, block_count, one_block, begin)
    return amplitude.reshape(t_local, q_local, 2, out_width)


def solution(mesh):
    placed = (P("cuts", "mode", None, None), P(), P(), P("cuts", None, None), P())
    return jax.shard_map(
        on_device,
        mesh=mesh,
        in_specs=placed,
        out_specs=P("mode", "cuts", None, None),
        check_vma=False,
    )
```

time: 174 us -> 82.3 us (0.47)
  waiting for transfers between devices: 73.3 us -> 2.05 us
  between operations: 14.9 us -> 0.15 us
  local copies, waits for them, and re-layouts: 37 us -> 50.1 us
  other arithmetic: 24.2 us -> 15.3 us
  loops' own time: 8.19 us -> 0 us
  starting transfers between devices: 11.3 us -> 8.05 us
    psum x2 -> x0, waiting for transfers between devices: 45.7 us -> none  [broadcast(): return lax.psum(block, axis)]
    transpose x0 -> x2, local copies, waits for them, and re-layouts: none -> 18.6 us  [the longest x1 18.5 us: blocks_part(): jnp.transpose(lhs, (4, 7, 0, 2, 5, 1, 3, 6))]
    dot_general x0 -> x2, local copies, waits for them, and re-layouts: none -> 16 us  [blocks_part(): return jnp.dot(lhs, second_w, preferred_element_type=jnp.float32)]
    reduce_scatter x1 -> x0, waiting for transfers between devices: 13.7 us -> none  [on_device(): lax.psum_scatter(amplitude, 'cuts', scatter_dimension=1, tiled=True)]
    unnamed x18 -> x6, local copies, waits for them, and re-layouts: 12.5 us -> 0.08 us
    all_to_all x2 -> x1, waiting for transfers between devices: 13.8 us -> 2.05 us  [on_device(): stem_rows = lax.all_to_all(payload, ('cuts', 'mode'), 0, 0, tiled=True)]
    concatenate x1, other arithmetic: 13 us -> 1.51 us  [on_device(): first_all = jnp.concatenate([upper, lower], axis=1)]
    another operation x1 -> x0, loops' own time: 8.19 us -> none  [on_device(): amplitude = lax.fori_loop(0, block_count, one_block, begin)]
  transfers between devices with their start and end apart: 5 -> 2, of which waited for: 5 -> 1; matrix products, arithmetic and copies ran while one was open for 2% -> 19% of each run, Pallas kernels for 0% -> 0%
where the time goes in v1:
time: 82.3 us; the launch traced here: 81.6 us
  local copies, waits for them, and re-layouts  50.1 us (61%)
  other arithmetic  15.3 us (19%)
  starting transfers between devices  8.05 us (10%)
  matrix products  5.89 us (7%)
  waiting for transfers between devices  2.05 us (2%)
    transpose x1, local copies, waits for them, and re-layouts, blocks_part(): jnp.transpose(lhs, (4, 7, 0, 2, 5, 1, 3, 6))  18.5 us
    dot_general x2, local copies, waits for them, and re-layouts, blocks_part(): return jnp.dot(lhs, second_w, preferred_element_type=jnp.float32)  16 us
    transpose x1, other arithmetic, blocks_part(): jnp.transpose(lhs, (4, 7, 0, 2, 5, 1, 3, 6))  7.29 us
    all_to_all x1, starting transfers between devices, on_device(): stem_rows = lax.all_to_all(payload, ('cuts', 'mode'), 0, 0, tiled=True)  5.12 us
    reshape x1, local copies, waits for them, and re-layouts, blocks_part(): split = product.reshape(chunk, n_mode, t_local, n_cuts, 2, a_count, q_local)  4.13 us
    squeeze x1, local copies, waits for them, and re-layouts, blocks_part(): real_p, imag_p = (split[:, :, :, :, 0], split[:, :, :, :, 1])  3.37 us
    gather x1, local copies, waits for them, and re-layouts, blocks_part(): first_w = jnp.take(first_all, first_ids, axis=0)  3.19 us
    ppermute x1, starting transfers between devices, gather_over_cuts(): current = lax.ppermute(current, 'cuts', ring)  2.94 us
  transfers between devices with their start and end apart: 2, of which 1 were waited for; matrix products, arithmetic and copies ran while one was open for 19% of the time, Pallas kernels for 0%

profile of v1, /device:TPU:0, one launch (start us, length us, event | category | flops | bytes accessed | tf_op | source)
XLA Modules:
  0.0 81.6 jit_solution(10778673487798444668)
XLA Ops:
  0.0 2.9 %collective-permute-start = (s32[2,2]{1,0:T(2,128)}, s32[2,2]{1,0:T(2,128)S(1)}, u32[]{:S(2)}, u32[]{:S(2)}) collective-permute-start(s32[2,2]{1,0:T(2,128)} %bitcast.70), channel_id=1, source_target_pairs={{0,16},{16,0},{1,17},{17,1},{2,18},{18,2},{3,19},{19,3},{4,20},{20... | collective-permute-start | bytes 56 | tf_op jit(solution)/shard_map/ppermute | solution.py:12
  2.9 1.1 %broadcast_in_dim.40 = bf16[16,16,512]{2,1,0:T(8,128)(2,1)S(1)} reshape(bf16[1,256,2,256]{3,2,1,0:T(2,128)(2,1)} %param.5) | data formatting | bytes 524288 | tf_op jit(solution)/shard_map/broadcast_in_dim | solution.py:67
  4.1 0.9 %broadcast_in_dim.41 = bf16[2,16,16,512]{3,2,1,0:T(8,128)(2,1)} broadcast(bf16[16,16,512]{2,1,0:T(8,128)(2,1)S(1)} %broadcast_in_dim.40), dimensions={1,2,3} | broadcast | bytes 786432 | tf_op jit(solution)/shard_map/broadcast_in_dim | solution.py:67
  4.9 5.1 %all-to-all-start = ((bf16[32,16,512]{2,1,0:T(8,128)(2,1)}), bf16[32,16,512]{2,1,0:T(8,128)(2,1)}, u32[]{:S(2)}, u32[]{:S(2)}) async-start(bf16[32,16,512]{2,1,0:T(8,128)(2,1)} %bitcast.12), calls=%async_computation | async-start | bytes 1048576 | tf_op jit(solution)/shard_map/all_to_all | solution.py:69
  10.0 0.8 reshape.165
  11.0 2.4 %fusion = bf16[8,2,256,128]{2,3,1,0:T(8,128)(2,1)S(1)} fusion(bf16[8,2,256,256]{3,2,1,0:T(8,128)(2,1)} %param.6, s32[128]{0:T(128)S(1)} %eq.18), kind=kOutput, calls=%fused_computation.10 | convolution fusion | flops 268992512 | bytes 3146240 | tf_op jit(solution)/shard_map/spkj,jn->spkn/dot_general | solution.py:79
  13.6 1.5 %maximum_maximum_fusion = bf16[8,512,256]{1,2,0:T(8,128)(2,1)} fusion(bf16[8,256,128]{1,2,0:T(8,128)(2,1)S(1)} %get-tuple-element.12, bf16[8,256,128]{1,2,0:T(8,128)(2,1)S(1)} %fusion.9, bf16[8,256,128]{1,2,0:T(8,128)(2,1)S(1)} %get-tuple-element.11), kind=kLoop, calls=%fused_computation.8 | loop fusion | flops 8388608 | bytes 3670016 | tf_op jit(solution)/shard_map/concatenate | solution.py:85
  15.1 0.6 gather_fusion
  15.7 0.2 slice_reduce_fusion
  16.5 3.2 %gather_fusion.1 = bf16[4,512,256]{1,2,0:T(8,128)(2,1)} fusion(bf16[8,512,256]{1,2,0:T(8,128)(2,1)} %maximum_maximum_fusion, s32[1024]{0:T(1024)S(1)} %pad_clamp_fusion.1), kind=kCustom, calls=%fused_computation.1 | custom fusion | bytes 2097168 | tf_op jit(solution)/shard_map/jit(_take)/gather | solution.py:26
  19.7 0.6 gather_fusion.2
  20.4 2.4 %broadcast_select_fusion.1 = bf16[2,2,512,256]{2,3,1,0:T(8,128)(2,1)} fusion(bf16[2,2,512,256]{2,3,1,0:T(8,128)(2,1)} %bitcast.67, pred[2,2]{1,0:T(4,128)(4,1)S(1)} %copy.14), kind=kLoop, calls=%fused_computation.14 | loop fusion | flops 524288 | bytes 2097156 | tf_op jit(solution)/shard_map/jit(_take)/select_n | solution.py:26
  22.7 1.1 %broadcast_select_fusion = bf16[4,512,256]{2,1,0:T(8,128)(2,1)} fusion(bf16[4,512,256]{2,1,0:T(8,128)(2,1)S(1)} %gather_fusion.2, pred[4]{0:T(512)(128)(4,1)S(1)} %compare_and_fusion), kind=kLoop, calls=%fused_computation.13 | loop fusion | flops 524288 | bytes 2097156 | tf_op jit(solution)/shard_map/jit(_take)/select_n | solution.py:44
  23.9 2.0 %all-to-all-done = bf16[32,16,512]{2,1,0:T(8,128)(2,1)} async-done(((bf16[32,16,512]{2,1,0:T(8,128)(2,1)}), bf16[32,16,512]{2,1,0:T(8,128)(2,1)}, u32[]{:S(2)}, u32[]{:S(2)}) %all-to-all-start) | async-done | bytes 524320 | tf_op jit(solution)/shard_map/all_to_all | solution.py:69
  25.9 1.8 %fusion.1 = bf16[2,256,512]{1,2,0:T(8,128)(2,1)S(1)} fusion(bf16[2,512,512]{1,2,0:T(8,128)(2,1)} %bitcast.68, bf16[2,256,512]{2,1,0:T(8,128)(2,1)} %bitcast.13), kind=kOutput, calls=%fused_computation.12 | convolution fusion | flops 268697600 | bytes 2097152 | tf_op jit(solution)/shard_map/bri,bio->bro/dot_general | solution.py:30
  27.8 4.1 %reshape.169 = bf16[2,16,16,2,2,16,8]{2,1,6,5,4,3,0:T(8,128)(2,1)} reshape(bf16[2,256,512]{1,2,0:T(8,128)(2,1)S(1)} %fusion.1) | data formatting | bytes 1048576 | tf_op jit(solution)/shard_map/reshape | solution.py:33
  31.9 3.4 %slice_bitcast_fusion = (bf16[1,2,16,16,2,16,8]{3,2,6,5,4,1,0:T(8,128)(2,1)S(1)}, bf16[1,2,16,16,2,16,8]{3,2,6,5,4,1,0:T(8,128)(2,1)S(1)}) fusion(bf16[2,16,16,2,2,16,8]{2,1,6,5,4,3,0:T(8,128)(2,1)} %reshape.169), kind=kLoop, calls=%fused_computation.6 | loop fusion | bytes 1048576 | tf_op jit(solution)/shard_map/squeeze | solution.py:34
  35.3 0.3 fusion.10
  35.6 2.6 %maximum_bitcast_fusion.1 = (bf16[1,2,2,16,16,2,16,8]{4,3,7,6,5,2,1,0:T(8,128)(2,1)S(1)}, bf16[1,2,2,16,16,2,16,8]{4,3,7,6,5,2,1,0:T(8,128)(2,1)}) fusion(bf16[1,2,16,16,2,16,8]{3,2,6,5,4,1,0:T(8,128)(2,1)S(1)} %fusion.10, bf16[1,2,16,16,2,16,8]{3,2,6,5,4,1,0:T(8,128)(2,1)S(1)} %get-tuple-element.8, bf16[1,2,16,16,2,16,8]{3,2,6,5,4,1,0:T(8,128)(2,1)S(1)} %get-tuple-element.7), kind=kLoop, calls=%fused_computation.4 | loop fusion | flops 524288 | bytes 1835008 | tf_op jit(solution)/shard_map/stack | solution.py:35
  38.2 7.3 %maximum_bitcast_fusion = bf16[16,8,2,2,2,2,16,16]{0,6,1,7,4,3,5,2:T(8,128)(2,1)} fusion(bf16[1,2,2,16,16,2,16,8]{4,3,7,6,5,2,1,0:T(8,128)(2,1)} %get-tuple-element.10, bf16[1,2,2,16,16,2,16,8]{4,3,7,6,5,2,1,0:T(8,128)(2,1)S(1)} %get-tuple-element.9), kind=kLoop, calls=%fused_computation.3 | loop fusion | flops 524288 | bytes 2097152 | tf_op jit(solution)/shard_map/transpose | solution.py:41
  45.5 18.5 %copy.18 = bf16[16,8,2,2,2,2,16,16]{7,6,5,4,3,1,2,0:T(8,128)(2,1)} copy(bf16[16,8,2,2,2,2,16,16]{0,6,1,7,4,3,5,2:T(8,128)(2,1)} %maximum_bitcast_fusion) | data formatting | bytes 2097152 | tf_op jit(solution)/shard_map/transpose | solution.py:41
  63.9 15.1 %dot_general.13 = bf16[16,8,2,2048]{3,1,2,0:T(8,128)(2,1)S(1)} reshape(bf16[16,8,2,2,2,2,16,16]{7,6,5,4,3,1,2,0:T(8,128)(2,1)} %copy.18) | data formatting | bytes 2097152 | tf_op jit(solution)/shard_map/dot_general | solution.py:47
  79.1 1.7 %fusion.11 = f32[16,8,2,256]{3,1,2,0:T(8,128)S(1)} fusion(bf16[16,8,2,2048]{3,1,2,0:T(8,128)(2,1)S(1)} %dot_general.13, bf16[2048,256,1,1]{1,0,3,2:T(8,128)(2,1)} %bitcast.66), kind=kOutput, calls=%fused_computation.48 | convolution fusion | flops 268435456 | bytes 2359296 | tf_op jit(solution)/shard_map/dot_general | solution.py:47
  80.7 0.8 %copy.21 = f32[16,8,2,256]{3,2,1,0:T(2,128)} copy(f32[16,8,2,256]{3,1,2,0:T(8,128)S(1)} %fusion.11) | data formatting | bytes 524288 | tf_op jit(solution)/shard_map/dot_general | solution.py:47
  (28 shorter events, 1.1 us)
Async XLA Ops:
  0.0 19.7 %copy-start = (bf16[8,2,256,256]{3,2,1,0:T(8,128)(2,1)S(1)}, bf16[8,2,256,256]{3,2,1,0:T(8,128)(2,1)}, u32[]{:S(2)}) copy-start(bf16[8,2,256,256]{3,2,1,0:T(8,128)(2,1)} %param.7) | copy-start | bytes 6291460
  0.0 15.1 %collective-permute-start = (s32[2,2]{1,0:T(2,128)}, s32[2,2]{1,0:T(2,128)S(1)}, u32[]{:S(2)}, u32[]{:S(2)}) collective-permute-start(s32[2,2]{1,0:T(2,128)} %bitcast.70), channel_id=1, source_target_pairs={{0,16},{16,0},{1,17},{17,1},{2,18},{18,2},{3,19},{19,3},{4,20},{20... | collective-permute-start | bytes 56 | tf_op jit(solution)/shard_map/ppermute | solution.py:12
  4.9 21.0 %all-to-all-start = ((bf16[32,16,512]{2,1,0:T(8,128)(2,1)}), bf16[32,16,512]{2,1,0:T(8,128)(2,1)}, u32[]{:S(2)}, u32[]{:S(2)}) async-start(bf16[32,16,512]{2,1,0:T(8,128)(2,1)} %bitcast.12), calls=%async_computation | async-start | bytes 1048576 | tf_op jit(solution)/shard_map/all_to_all | solution.py:69
  13.4 1.7 %copy-start.2 = (s32[1,2,2]{2,1,0:T(2,128)S(1)}, s32[1,2,2]{2,1,0:T(2,128)}, u32[]{:S(2)}) copy-start(s32[1,2,2]{2,1,0:T(2,128)} %param.8) | copy-start | bytes 52
  31.9 3.5 %copy-start.1 = (bf16[2,16,16,2,2,16,8]{2,1,6,5,4,3,0:T(8,128)(2,1)S(1)}, bf16[2,16,16,2,2,16,8]{2,1,6,5,4,3,0:T(8,128)(2,1)}, u32[]{:S(2)}) copy-start(bf16[2,16,16,2,2,16,8]{2,1,6,5,4,3,0:T(8,128)(2,1)} %reshape.169) | copy-start | bytes 1572868

commit v2 on v1

--- a/solution.py
+++ b/solution.py
@@ -47,6 +47,42 @@
     return jnp.dot(lhs, second_w, preferred_element_type=jnp.float32)
 
 
+def stacked_part(stem_rows, first_cols, w2_table, first_ids, second_ids, sizes):
+    n_mode, t_local, n_cuts, a_count, q_local = sizes
+    block_count = stem_rows.shape[0]
+    slice_count, _, width, _ = first_cols.shape
+    _, _, inner, out_width = w2_table.shape
+    group = n_cuts * 2 * a_count
+    split_cols = first_cols.reshape(slice_count, 2, width, a_count, q_local)
+    real_part, imag_part = split_cols[:, 0], split_cols[:, 1]
+    first_w = jnp.stack(
+        [jnp.stack([real_part, imag_part]), jnp.stack([-imag_part, real_part])]
+    )
+    first_w = jnp.take(first_w, first_ids.reshape(-1), axis=2)
+    first_w = first_w.reshape(2, 2, block_count, n_cuts, width, a_count, q_local)
+    first_w = jnp.transpose(first_w, (2, 0, 4, 6, 3, 1, 5)).reshape(
+        block_count, 2 * width, q_local * group
+    )
+    product = jnp.einsum(
+        "bri,bio->bro", stem_rows, first_w, preferred_element_type=jnp.float32
+    ).astype(jnp.bfloat16)
+    lhs = product.reshape(block_count * n_mode, t_local, q_local, group)
+    lhs = jnp.transpose(lhs, (2, 1, 0, 3)).reshape(
+        q_local * t_local, block_count * n_mode * group
+    )
+    second = jnp.take(w2_table, second_ids.reshape(-1), axis=0)
+    second = second.reshape(block_count, n_cuts, 2, n_mode, a_count, out_width)
+    real_two, imag_two = second[:, :, 0], second[:, :, 1]
+    second_w = jnp.stack(
+        [jnp.stack([real_two, imag_two]), jnp.stack([-imag_two, real_two])]
+    )
+    second_w = jnp.transpose(second_w, (2, 4, 3, 0, 5, 1, 6)).reshape(
+        block_count * n_mode * group, 2 * out_width
+    )
+    amplitude = jnp.dot(lhs, second_w, preferred_element_type=jnp.float32)
+    amplitude = amplitude.reshape(q_local, t_local, 2, out_width)
+    return jnp.transpose(amplitude, (1, 0, 2, 3))
+
 def on_device(stem_blocks, w1_table, w2_table, slice_ids, mode_perm):
     n_mode = lax.axis_size("mode")
     n_cuts = lax.axis_size("cuts")
@@ -85,9 +121,7 @@
     first_all = jnp.concatenate([upper, lower], axis=1)
 
     if block_count * n_cuts <= 8:
-        amplitude = blocks_part(
-            stem_rows, first_all, w2_table, first_ids, second_ids.reshape(-1), sizes
-        )
+        return stacked_part(stem_rows, first_cols, w2_table, first_ids, second_ids, sizes)
     else:
         def one_block(index, running):
             stem_one = lax.dynamic_slice_in_dim(stem_rows, index, 1, axis=0)

time: 82.3 us -> 47.7 us (0.58)
  local copies, waits for them, and re-layouts: 50.1 us -> 28.2 us
  other arithmetic: 15.3 us -> 5.23 us
  waiting for transfers between devices: 2.05 us -> 0.01 us
    transpose x1 -> x4, local copies, waits for them, and re-layouts: 18.5 us -> 5.9 us  [the longest x1 3.24 us: stacked_part(): jnp.transpose(second_w, (2, 4, 3, 0, 5, 1, 6))]
    dot_general x2, local copies, waits for them, and re-layouts: 16 us -> 6.13 us  [stacked_part(): amplitude = jnp.dot(lhs, second_w, preferred_element_type=jnp.float32)]
    transpose x1 -> x2, other arithmetic: 7.29 us -> 2.94 us  [the longest x1 2.74 us: stacked_part(): jnp.transpose(first_w, (2, 0, 4, 6, 3, 1, 5))]
    squeeze x2 -> x0, local copies, waits for them, and re-layouts: 3.44 us -> none  [the longest x1 3.37 us: blocks_part(): real_p, imag_p = (split[:, :, :, :, 0], split[:, :, :, :, 1])]
    select_n x4 -> x3, other arithmetic: 3.49 us -> 0.18 us  [the longest x2 0.17 us: stacked_part(): second = jnp.take(w2_table, second_ids.reshape(-1), axis=0)]
    convert_element_type x0 -> x1, local copies, waits for them, and re-layouts: none -> 2.06 us  [stacked_part(): product = jnp.einsum('bri,bio->bro', stem_rows, first_w, preferred_elemen...]
    all_to_all x1, waiting for transfers between devices: 2.05 us -> 0.01 us  [on_device(): stem_rows = lax.all_to_all(payload, ('cuts', 'mode'), 0, 0, tiled=True)]
    unnamed x6 -> x9, local copies, waits for them, and re-layouts: 0.08 us -> 1.85 us
  transfers between devices with their start and end apart: 2 -> 2, of which waited for: 1 -> 0; matrix products, arithmetic and copies ran while one was open for 19% -> 55% of each run, Pallas kernels for 0% -> 0%
where the time goes in v2:
time: 47.7 us; the launch traced here: 47.2 us
  local copies, waits for them, and re-layouts  28.2 us (59%)
  starting transfers between devices  8 us (17%)
  matrix products  5.55 us (12%)
  other arithmetic  5.23 us (11%)
    dot_general x2, local copies, waits for them, and re-layouts, stacked_part(): amplitude = jnp.dot(lhs, second_w, preferred_element_type=jnp.float32)  6.13 us
    all_to_all x1, starting transfers between devices, on_device(): stem_rows = lax.all_to_all(payload, ('cuts', 'mode'), 0, 0, tiled=True)  5.06 us
    transpose x1, local copies, waits for them, and re-layouts, stacked_part(): jnp.transpose(second_w, (2, 4, 3, 0, 5, 1, 6))  3.24 us
    ppermute x1, starting transfers between devices, gather_over_cuts(): current = lax.ppermute(current, 'cuts', ring)  2.94 us
    transpose x1, other arithmetic, stacked_part(): jnp.transpose(first_w, (2, 0, 4, 6, 3, 1, 5))  2.74 us
    reshape x1, local copies, waits for them, and re-layouts, stacked_part(): jnp.transpose(first_w, (2, 0, 4, 6, 3, 1, 5))  2.52 us
    dot_general x1, matrix products, stacked_part(): amplitude = jnp.dot(lhs, second_w, preferred_element_type=jnp.float32)  2.42 us
    dot_general x1, matrix products, stacked_part(): jnp.einsum('bri,bio->bro', stem_rows, first_w, preferred_element_type=jnp...  2.31 us
  transfers between devices with their start and end apart: 2, of which 0 were waited for; matrix products, arithmetic and copies ran while one was open for 55% of the time, Pallas kernels for 0%

profile of v2, /device:TPU:0, one launch (start us, length us, event | category | flops | bytes accessed | tf_op | source)
XLA Modules:
  0.0 47.2 jit_solution(4252173542771565453)
XLA Ops:
  0.0 2.9 %collective-permute-start = (s32[2,2]{1,0:T(2,128)}, s32[2,2]{1,0:T(2,128)S(1)}, u32[]{:S(2)}, u32[]{:S(2)}) collective-permute-start(s32[2,2]{1,0:T(2,128)} %bitcast.85), channel_id=1, source_target_pairs={{0,16},{16,0},{1,17},{17,1},{2,18},{18,2},{3,19},{19,3},{4,20},{20... | collective-permute-start | bytes 56 | tf_op jit(solution)/shard_map/ppermute | solution.py:12
  2.9 1.1 %broadcast_in_dim.37 = bf16[16,16,512]{2,1,0:T(8,128)(2,1)S(1)} reshape(bf16[1,256,2,256]{3,2,1,0:T(2,128)(2,1)} %param.5) | data formatting | bytes 524288 | tf_op jit(solution)/shard_map/broadcast_in_dim | solution.py:103
  4.1 0.8 %broadcast_in_dim.38 = bf16[2,16,16,512]{3,2,1,0:T(8,128)(2,1)} broadcast(bf16[16,16,512]{2,1,0:T(8,128)(2,1)S(1)} %broadcast_in_dim.37), dimensions={1,2,3} | broadcast | bytes 786432 | tf_op jit(solution)/shard_map/broadcast_in_dim | solution.py:103
  4.9 5.1 %all-to-all-start = ((bf16[32,16,512]{2,1,0:T(8,128)(2,1)}), bf16[32,16,512]{2,1,0:T(8,128)(2,1)}, u32[]{:S(2)}, u32[]{:S(2)}) async-start(bf16[32,16,512]{2,1,0:T(8,128)(2,1)} %bitcast.17), calls=%async_computation | async-start | bytes 1048576 | tf_op jit(solution)/shard_map/all_to_all | solution.py:105
  10.3 0.8 %fusion = bf16[8,2,256,16,8]{2,4,3,1,0:T(8,128)(2,1)S(1)} fusion(bf16[8,2,256,256]{3,2,1,0:T(8,128)(2,1)S(1)} %copy-done, s32[128]{0:T(128)S(1)} %eq.18), kind=kOutput, calls=%fused_computation.7 | convolution fusion | flops 268992512 | bytes 3146240 | tf_op jit(solution)/shard_map/spkj,jn->spkn/dot_general | solution.py:115
  11.3 0.2 maximum_bitcast_fusion.1
  11.5 1.5 %pad_maximum_fusion = bf16[2,2,8,256,16,8]{3,5,4,2,1,0:T(8,128)(2,1)} fusion(bf16[1,2,8,256,16,8]{3,5,4,2,1,0:T(8,128)(2,1)S(1)} %get-tuple-element.12, bf16[1,2,8,256,16,8]{3,5,4,2,1,0:T(8,128)(2,1)S(1)} %get-tuple-element.11), kind=kLoop, calls=%fused_computation.3 | loop fusion | flops 1048576 | bytes 4194304 | tf_op jit(solution)/shard_map/stack | solution.py:58
  13.0 0.6 %gather_fusion = s32[2,2,2]{2,1,0:T(2,128)S(1)} fusion(s32[2,2,2]{2,1,0:T(2,128)S(1)} %pad_add_fusion, s32[1024]{0:T(1024)S(1)} %pad_clamp_fusion.2), kind=kCustom, calls=%fused_computation | custom fusion | bytes 72 | tf_op jit(solution)/shard_map/jit(_take)/gather | solution.py:17
  13.6 0.2 slice_reduce_fusion.1
  14.2 2.2 %gather_fusion.1 = bf16[4,2,2,256,16,8]{3,5,4,2,1,0:T(8,128)(2,1)S(1)} fusion(bf16[2,2,8,256,16,8]{3,5,4,2,1,0:T(8,128)(2,1)} %pad_maximum_fusion, s32[1024]{0:T(1024)S(1)} %pad_clamp_fusion.1), kind=kCustom, calls=%fused_computation.1 | custom fusion | bytes 2097168 | tf_op jit(solution)/shard_map/jit(_take)/gather | solution.py:61
  16.4 2.7 %fusion.2 = bf16[2,2,256,8,2,2,16]{2,1,6,5,4,3,0:T(2,128)(2,1)} fusion(pred[2,2]{1,0:T(4,128)(4,1)S(1)} %copy.26, bf16[2,2,2,2,256,16,8]{4,6,5,1,0,3,2:T(8,128)(2,1)S(1)} %bitcast.77), kind=kLoop, calls=%fused_computation.11 | loop fusion | flops 524288 | bytes 2097156 | tf_op jit(solution)/shard_map/transpose | solution.py:63
  19.1 2.5 %reshape.185 = bf16[2,512,512]{1,2,0:T(8,128)(2,1)} reshape(bf16[2,2,256,8,2,2,16]{2,1,6,5,4,3,0:T(2,128)(2,1)} %fusion.2) | data formatting | bytes 2097152 | tf_op jit(solution)/shard_map/reshape | solution.py:63
  22.0 2.2 %gather_fusion.2 = bf16[4,2,256,256]{3,2,1,0:T(8,128)(2,1)S(1)} fusion(bf16[8,2,256,256]{3,2,1,0:T(8,128)(2,1)} %param.7, s32[1024]{0:T(1024)S(1)} %pad_clamp_fusion), kind=kCustom, calls=%fused_computation.2 | custom fusion | bytes 2097168 | tf_op jit(solution)/shard_map/jit(_take)/gather | solution.py:73
  24.8 0.2 maximum_bitcast_fusion
  25.0 3.2 %copy.35 = bf16[2,16,2,2,16,2,256]{6,5,4,3,2,1,0:T(2,128)(2,1)S(1)} copy(bf16[2,16,2,2,16,2,256]{6,4,1,2,0,5,3:T(8,128)(2,1)S(1)} %maximum_bitcast_fusion) | data formatting | bytes 4194304 | tf_op jit(solution)/shard_map/transpose | solution.py:79
  28.2 1.8 %copy.41 = bf16[256,8,2,256]{3,1,2,0:T(8,128)(2,1)} copy(bf16[256,8,2,256]{3,2,1,0:T(2,128)(2,1)S(1)} %bitcast.78) | data formatting | bytes 4194304
  30.0 4.1 %copy.36 = bf16[512,2048]{1,0:T(8,128)(2,1)} copy(bf16[512,2048]{0,1:T(8,128)(2,1)} %bitcast.79) | data formatting | bytes 4194304 | tf_op jit(solution)/shard_map/dot_general | solution.py:82
  34.1 2.3 %fusion.1 = bf16[2,256,512]{1,2,0:T(8,128)(2,1)} fusion(bf16[2,512,512]{1,2,0:T(8,128)(2,1)S(1)} %copy-done.1, bf16[2,256,512]{2,1,0:T(8,128)(2,1)} %bitcast.18), kind=kOutput, calls=%fused_computation.9 | convolution fusion | flops 268697600 | bytes 2097152 | tf_op jit(solution)/shard_map/bri,bio->bro/dot_general | solution.py:66
  36.4 2.1 %copy.30 = bf16[2,256,512]{2,1,0:T(8,128)(2,1)} copy(bf16[2,256,512]{1,2,0:T(8,128)(2,1)} %fusion.1) | data formatting | bytes 1048576 | tf_op jit(solution)/shard_map/convert_element_type | solution.py:68
  38.5 1.6 %reshape.188 = bf16[32,16,8,64]{3,2,1,0:T(8,128)(2,1)S(1)} reshape(bf16[2,256,512]{2,1,0:T(8,128)(2,1)} %copy.30) | data formatting | bytes 1048576 | tf_op jit(solution)/shard_map/reshape | solution.py:69
  40.2 1.7 %copy.31 = bf16[8,16,32,64]{3,2,1,0:T(8,128)(2,1)} copy(bf16[8,16,32,64]{3,0,1,2:T(8,128)(2,1)S(1)} %bitcast.81) | data formatting | bytes 1048576 | tf_op jit(solution)/shard_map/transpose | solution.py:70
  41.8 2.0 %reshape.216 = bf16[8,16,2048,1]{2,1,0,3:T(8,128)(2,1)S(1)} reshape(bf16[8,16,32,64]{3,2,1,0:T(8,128)(2,1)} %copy.31) | data formatting | bytes 1048576 | tf_op jit(solution)/shard_map/dot_general | solution.py:82
  43.9 2.4 %convolution_bitcast_fusion = f32[16,8,2,256]{3,0,2,1:T(8,128)S(1)} fusion(bf16[2,256,2048,1]{2,1,0,3:T(8,128)(2,1)} %bitcast.82, bf16[8,16,2048,1]{2,1,0,3:T(8,128)(2,1)S(1)} %reshape.216), kind=kOutput, calls=%fused_computation.10 | convolution fusion | flops 268435456 | bytes 2883584 | tf_op jit(solution)/shard_map/dot_general | solution.py:82
  46.3 0.9 %copy.37 = f32[16,8,2,256]{3,2,1,0:T(2,128)} copy(f32[16,8,2,256]{3,0,2,1:T(8,128)S(1)} %convolution_bitcast_fusion) | data formatting | bytes 524288 | tf_op jit(solution)/shard_map/transpose | solution.py:84
  (36 shorter events, 1.7 us)
Async XLA Ops:
  0.0 10.2 %copy-start = (bf16[8,2,256,256]{3,2,1,0:T(8,128)(2,1)S(1)}, bf16[8,2,256,256]{3,2,1,0:T(8,128)(2,1)}, u32[]{:S(2)}) copy-start(bf16[8,2,256,256]{3,2,1,0:T(8,128)(2,1)} %param.6) | copy-start | bytes 6291460
  0.0 10.0 %copy-start.2 = (s32[256]{0:T(256)S(1)}, s32[256]{0:T(256)}, u32[]{:S(2)}) copy-start(s32[256]{0:T(256)} %param.9) | copy-start | bytes 3076
  0.0 13.0 %collective-permute-start = (s32[2,2]{1,0:T(2,128)}, s32[2,2]{1,0:T(2,128)S(1)}, u32[]{:S(2)}, u32[]{:S(2)}) collective-permute-start(s32[2,2]{1,0:T(2,128)} %bitcast.85), channel_id=1, source_target_pairs={{0,16},{16,0},{1,17},{17,1},{2,18},{18,2},{3,19},{19,3},{4,20},{20... | collective-permute-start | bytes 56 | tf_op jit(solution)/shard_map/ppermute | solution.py:12
  4.9 29.2 %all-to-all-start = ((bf16[32,16,512]{2,1,0:T(8,128)(2,1)}), bf16[32,16,512]{2,1,0:T(8,128)(2,1)}, u32[]{:S(2)}, u32[]{:S(2)}) async-start(bf16[32,16,512]{2,1,0:T(8,128)(2,1)} %bitcast.17), calls=%async_computation | async-start | bytes 1048576 | tf_op jit(solution)/shard_map/all_to_all | solution.py:105
  11.4 1.5 %copy-start.3 = (s32[1,2,2]{2,1,0:T(2,128)S(1)}, s32[1,2,2]{2,1,0:T(2,128)}, u32[]{:S(2)}) copy-start(s32[1,2,2]{2,1,0:T(2,128)} %param.8) | copy-start | bytes 52
  30.0 4.1 %copy-start.1 = (bf16[2,512,512]{1,2,0:T(8,128)(2,1)S(1)}, bf16[2,512,512]{1,2,0:T(8,128)(2,1)}, u32[]{:S(2)}) copy-start(bf16[2,512,512]{1,2,0:T(8,128)(2,1)} %reshape.185) | copy-start | bytes 3145732

commit v3 on v2

--- a/solution.py
+++ b/solution.py
@@ -47,39 +47,41 @@
     return jnp.dot(lhs, second_w, preferred_element_type=jnp.float32)
 
 
-def stacked_part(stem_rows, first_cols, w2_table, first_ids, second_ids, sizes):
+def stacked_part(stem_rows, first_t, w2_table, first_ids, second_ids, sizes):
     n_mode, t_local, n_cuts, a_count, q_local = sizes
     block_count = stem_rows.shape[0]
-    slice_count, _, width, _ = first_cols.shape
+    width = first_t.shape[3]
     _, _, inner, out_width = w2_table.shape
     group = n_cuts * 2 * a_count
-    split_cols = first_cols.reshape(slice_count, 2, width, a_count, q_local)
-    real_part, imag_part = split_cols[:, 0], split_cols[:, 1]
+    picked = jnp.take(first_t, first_ids.reshape(-1), axis=0)
+    picked = picked.reshape(block_count, n_cuts, 2, q_local, a_count, width)
+    real_part, imag_part = picked[:, :, 0], picked[:, :, 1]
     first_w = jnp.stack(
         [jnp.stack([real_part, imag_part]), jnp.stack([-imag_part, real_part])]
     )
-    first_w = jnp.take(first_w, first_ids.reshape(-1), axis=2)
-    first_w = first_w.reshape(2, 2, block_count, n_cuts, width, a_count, q_local)
-    first_w = jnp.transpose(first_w, (2, 0, 4, 6, 3, 1, 5)).reshape(
-        block_count, 2 * width, q_local * group
+    first_w = jnp.transpose(first_w, (2, 4, 3, 1, 5, 0, 6)).reshape(
+        block_count, q_local * group, 2 * width
     )
     product = jnp.einsum(
-        "bri,bio->bro", stem_rows, first_w, preferred_element_type=jnp.float32
+        "brk,bnk->brn", stem_rows, first_w, preferred_element_type=jnp.float32
     ).astype(jnp.bfloat16)
-    lhs = product.reshape(block_count * n_mode, t_local, q_local, group)
-    lhs = jnp.transpose(lhs, (2, 1, 0, 3)).reshape(
+    lhs = product.reshape(block_count, n_mode, t_local, q_local, group)
+    lhs = jnp.transpose(lhs, (3, 2, 0, 1, 4)).reshape(
         q_local * t_local, block_count * n_mode * group
     )
     second = jnp.take(w2_table, second_ids.reshape(-1), axis=0)
-    second = second.reshape(block_count, n_cuts, 2, n_mode, a_count, out_width)
+    second = jnp.swapaxes(second, 2, 3)
+    second = second.reshape(block_count, n_cuts, 2, out_width, n_mode, a_count)
     real_two, imag_two = second[:, :, 0], second[:, :, 1]
     second_w = jnp.stack(
-        [jnp.stack([real_two, imag_two]), jnp.stack([-imag_two, real_two])]
+        [jnp.stack([real_two, -imag_two]), jnp.stack([imag_two, real_two])]
     )
-    second_w = jnp.transpose(second_w, (2, 4, 3, 0, 5, 1, 6)).reshape(
-        block_count * n_mode * group, 2 * out_width
+    second_w = jnp.transpose(second_w, (0, 4, 2, 5, 3, 1, 6)).reshape(
+        2 * out_width, block_count * n_mode * group
     )
-    amplitude = jnp.dot(lhs, second_w, preferred_element_type=jnp.float32)
+    amplitude = jnp.einsum(
+        "mk,nk->mn", lhs, second_w, preferred_element_type=jnp.float32
+    )
     amplitude = amplitude.reshape(q_local, t_local, 2, out_width)
     return jnp.transpose(amplitude, (1, 0, 2, 3))
 
@@ -121,7 +123,12 @@
     first_all = jnp.concatenate([upper, lower], axis=1)
 
     if block_count * n_cuts <= 8:
-        return stacked_part(stem_rows, first_cols, w2_table, first_ids, second_ids, sizes)
+        wanted_t = lax.dynamic_slice_in_dim(perm_grid, me * q_local, q_local, axis=1).T.reshape(-1)
+        picker_t = (wanted_t[:, None] == jnp.arange(mid, dtype=jnp.int32)[None, :]).astype(w1_table.dtype)
+        first_t = jnp.einsum(
+            "nj,spkj->spnk", picker_t, w1_table, preferred_element_type=jnp.float32
+        ).astype(w1_table.dtype)
+        return stacked_part(stem_rows, first_t, w2_table, first_ids, second_ids, sizes)
     else:
         def one_block(index, running):
             stem_one = lax.dynamic_slice_in_dim(stem_rows, index, 1, axis=0)

time: 47.7 us -> 37.5 us (0.79)
  local copies, waits for them, and re-layouts: 28.2 us -> 19.7 us
  other arithmetic: 5.23 us -> 3.3 us
    dot_general x2 -> x1, local copies, waits for them, and re-layouts: 6.13 us -> 2.05 us  [stacked_part(): jnp.einsum('mk,nk->mn', lhs, second_w, preferred_element_type=jnp.float32)]
    transpose x2, other arithmetic: 2.94 us -> 0.29 us  [the longest x1 0.19 us: stacked_part(): jnp.transpose(second_w, (0, 4, 2, 5, 3, 1, 6))]
    unnamed x9 -> x8, local copies, waits for them, and re-layouts: 1.85 us -> 0.02 us
    another operation x2 -> x1, other arithmetic: 1.71 us -> 0.09 us  [stacked_part(): jnp.stack([jnp.stack([real_part, imag_part]), jnp.stack([-imag_part, real...]
    another operation x1, other arithmetic: 0.18 us -> 1.38 us  [stacked_part(): jnp.stack([jnp.stack([real_two, -imag_two]), jnp.stack([imag_two, real_tw...]
    select_n x1 -> x2, other arithmetic: 0.01 us -> 1.16 us  [stacked_part(): picked = jnp.take(first_t, first_ids.reshape(-1), axis=0)]
    convert_element_type x1, local copies, waits for them, and re-layouts: 2.06 us -> 1.02 us  [stacked_part(): product = jnp.einsum('brk,bnk->brn', stem_rows, first_w, preferred_elemen...]
    reshape x3, local copies, waits for them, and re-layouts: 4.24 us -> 3.23 us  [the longest x1 1.64 us: stacked_part(): lhs = product.reshape(block_count, n_mode, t_local, q_local, group)]
  transfers between devices with their start and end apart: 2 -> 2, of which waited for: 0 -> 1; matrix products, arithmetic and copies ran while one was open for 55% -> 47% of each run, Pallas kernels for 0% -> 0%
where the time goes in v3:
time: 37.5 us; the launch traced here: 37 us
  local copies, waits for them, and re-layouts  19.7 us (53%)
  starting transfers between devices  8 us (21%)
  matrix products  5.69 us (15%)
  other arithmetic  3.3 us (9%)
    all_to_all x1, starting transfers between devices, on_device(): stem_rows = lax.all_to_all(payload, ('cuts', 'mode'), 0, 0, tiled=True)  5.06 us
    ppermute x1, starting transfers between devices, gather_over_cuts(): current = lax.ppermute(current, 'cuts', ring)  2.94 us
    gather x1, local copies, waits for them, and re-layouts, stacked_part(): second = jnp.take(w2_table, second_ids.reshape(-1), axis=0)  2.21 us
    dot_general x1, local copies, waits for them, and re-layouts, stacked_part(): jnp.einsum('mk,nk->mn', lhs, second_w, preferred_element_type=jnp.float32)  2.05 us
    dot_general x1, matrix products, stacked_part(): jnp.einsum('mk,nk->mn', lhs, second_w, preferred_element_type=jnp.float32)  2.03 us
    broadcast_in_dim x2, local copies, waits for them, and re-layouts, on_device(): payload = jnp.broadcast_to(pieces, (n_cuts, n_mode, t_local, 2 * width))  1.97 us
    dot_general x1, matrix products, on_device(): jnp.einsum('nj,spkj->spnk', picker_t, w1_table, preferred_element_type=jn...  1.83 us
    dot_general x1, matrix products, stacked_part(): jnp.einsum('brk,bnk->brn', stem_rows, first_w, preferred_element_type=jnp...  1.82 us
  transfers between devices with their start and end apart: 2, of which 1 were waited for; matrix products, arithmetic and copies ran while one was open for 47% of the time, Pallas kernels for 0%

profile of v3, /device:TPU:0, one launch (start us, length us, event | category | flops | bytes accessed | tf_op | source)
XLA Modules:
  0.0 37.0 jit_solution(16951512116122450524)
XLA Ops:
  0.0 2.9 %collective-permute-start = (s32[2,2]{1,0:T(2,128)}, s32[2,2]{1,0:T(2,128)S(1)}, u32[]{:S(2)}, u32[]{:S(2)}) collective-permute-start(s32[2,2]{1,0:T(2,128)} %bitcast.76), channel_id=1, source_target_pairs={{0,16},{16,0},{1,17},{17,1},{2,18},{18,2},{3,19},{19,3},{4,20},{20... | collective-permute-start | bytes 56 | tf_op jit(solution)/shard_map/ppermute | solution.py:12
  2.9 1.1 %broadcast_in_dim.37 = bf16[16,16,512]{2,1,0:T(8,128)(2,1)S(1)} reshape(bf16[1,256,2,256]{3,2,1,0:T(2,128)(2,1)} %param.5) | data formatting | bytes 524288 | tf_op jit(solution)/shard_map/broadcast_in_dim | solution.py:105
  4.1 0.9 %broadcast_in_dim.38 = bf16[2,16,16,512]{3,2,1,0:T(8,128)(2,1)} broadcast(bf16[16,16,512]{2,1,0:T(8,128)(2,1)S(1)} %broadcast_in_dim.37), dimensions={1,2,3} | broadcast | bytes 786432 | tf_op jit(solution)/shard_map/broadcast_in_dim | solution.py:105
  4.9 5.1 %all-to-all-start = ((bf16[32,16,512]{2,1,0:T(8,128)(2,1)}), bf16[32,16,512]{2,1,0:T(8,128)(2,1)}, u32[]{:S(2)}, u32[]{:S(2)}) async-start(bf16[32,16,512]{2,1,0:T(8,128)(2,1)} %bitcast.15), calls=%async_computation | async-start | bytes 1048576 | tf_op jit(solution)/shard_map/all_to_all | solution.py:107
  10.4 1.8 %fusion = bf16[8,2,128,256]{3,2,1,0:T(8,128)(2,1)} fusion(bf16[8,2,256,256]{3,2,1,0:T(8,128)(2,1)S(1)} %copy-done, s32[128]{0:T(128)S(1)} %eq.17), kind=kOutput, calls=%fused_computation.5 | convolution fusion | flops 268992512 | bytes 3146240 | tf_op jit(solution)/shard_map/nj,spkj->spnk/dot_general | solution.py:128
  12.2 0.6 %gather_fusion = s32[2,2,2]{2,1,0:T(2,128)S(1)} fusion(s32[2,2,2]{2,1,0:T(2,128)S(1)} %pad_add_fusion, s32[1024]{0:T(1024)S(1)} %pad_clamp_fusion.2), kind=kCustom, calls=%fused_computation | custom fusion | bytes 72 | tf_op jit(solution)/shard_map/jit(_take)/gather | solution.py:17
  12.9 0.2 slice_reduce_fusion.1
  13.4 2.2 %gather_fusion.2 = bf16[4,2,256,256]{3,2,1,0:T(8,128)(2,1)S(1)} fusion(bf16[8,2,256,256]{3,2,1,0:T(8,128)(2,1)} %param.7, s32[1024]{0:T(1024)S(1)} %pad_clamp_fusion), kind=kCustom, calls=%fused_computation.2 | custom fusion | bytes 2097168 | tf_op jit(solution)/shard_map/jit(_take)/gather | solution.py:72
  15.8 0.9 %slice_bitcast_fusion = (bf16[1,2,2,256,16,16]{3,5,4,2,1,0:T(8,128)(2,1)S(1)}, bf16[1,2,2,256,16,16]{3,5,4,2,1,0:T(8,128)(2,1)}) fusion(bf16[2,2,2,256,16,16]{3,5,4,2,1,0:T(8,128)(2,1)S(1)} %bitcast.70), kind=kLoop, calls=%fused_computation.13 | loop fusion | bytes 2097152 | tf_op jit(solution)/shard_map/squeeze | solution.py:75
  16.9 1.4 %maximum_bitcast_fusion.2 = (bf16[1,2,2,2,256,16,16]{4,6,5,3,2,1,0:T(8,128)(2,1)S(1)}, bf16[1,2,2,2,256,16,16]{4,6,5,3,2,1,0:T(8,128)(2,1)S(1)}) fusion(bf16[1,2,2,256,16,16]{3,5,4,2,1,0:T(8,128)(2,1)S(1)} %fusion.12, bf16[1,2,2,256,16,16]{3,5,4,2,1,0:T(8,128)(2,1)} %get-tuple-element.8, bf16[1,2,2,256,16,16]{3,5,4,2,1,0:T(8,128)(2,1)S(1)} %get-tuple-element.7), kind=kLoop, calls=%fused_computation.10 | loop fusion | flops 1048576 | bytes 3670016 | tf_op jit(solution)/shard_map/stack | solution.py:76
  18.3 0.2 maximum_bitcast_fusion
  18.5 1.7 %copy.36 = bf16[2,256,2,16,2,2,16]{1,6,5,4,3,2,0:T(8,128)(2,1)} copy(bf16[2,256,2,16,2,2,16]{1,6,3,4,2,5,0:T(8,128)(2,1)S(1)} %maximum_bitcast_fusion) | data formatting | bytes 4194304 | tf_op jit(solution)/shard_map/transpose | solution.py:79
  20.3 1.4 %gather_fusion.1 = bf16[4,2,128,256]{3,2,1,0:T(8,128)(2,1)} fusion(bf16[8,2,128,256]{3,2,1,0:T(8,128)(2,1)S(1)} %copy-done.1, s32[1024]{0:T(1024)S(1)} %pad_clamp_fusion.1), kind=kCustom, calls=%fused_computation.1 | custom fusion | bytes 1048592 | tf_op jit(solution)/shard_map/jit(_take)/gather | solution.py:56
  21.7 1.2 %broadcast_select_fusion.1 = bf16[2,2,2,8,16,256]{5,4,3,2,1,0:T(8,128)(2,1)S(1)} fusion(bf16[2,2,2,8,16,256]{5,4,3,2,1,0:T(8,128)(2,1)} %bitcast.73, pred[2,2]{1,0:T(4,128)(4,1)S(1)} %copy.27), kind=kLoop, calls=%fused_computation.18 | loop fusion | flops 262144 | bytes 1048580 | tf_op jit(solution)/shard_map/jit(_take)/select_n | solution.py:56
  23.1 1.1 %copy.31 = bf16[2,8,2,2,16,2,256]{6,5,4,3,2,1,0:T(2,128)(2,1)S(1)} copy(bf16[2,8,2,2,16,2,256]{6,4,1,2,0,3,5:T(8,128)(2,1)S(1)} %maximum_bitcast_fusion.1) | data formatting | bytes 2097152 | tf_op jit(solution)/shard_map/transpose | solution.py:62
  24.2 1.5 %reshape.182 = bf16[2,512,512]{2,1,0:T(8,128)(2,1)} reshape(bf16[2,8,2,2,16,2,256]{6,5,4,3,2,1,0:T(2,128)(2,1)S(1)} %copy.31) | data formatting | bytes 2097152 | tf_op jit(solution)/shard_map/reshape | solution.py:62
  25.7 0.2 all-to-all-done
  25.9 1.8 %fusion.1 = bf16[2,256,512]{1,2,0:T(8,128)(2,1)S(1)} fusion(bf16[2,512,512]{2,1,0:T(8,128)(2,1)} %reshape.182, bf16[2,256,512]{2,1,0:T(8,128)(2,1)} %bitcast.16), kind=kOutput, calls=%fused_computation.7 | convolution fusion | flops 268697600 | bytes 2097152 | tf_op jit(solution)/shard_map/brk,bnk->brn/dot_general | solution.py:65
  27.7 1.0 %copy.32 = bf16[2,256,512]{2,1,0:T(8,128)(2,1)} copy(bf16[2,256,512]{1,2,0:T(8,128)(2,1)S(1)} %fusion.1) | data formatting | bytes 1048576 | tf_op jit(solution)/shard_map/convert_element_type | solution.py:67
  28.7 1.6 %reshape.185 = bf16[2,16,16,8,64]{4,3,2,1,0:T(8,128)(2,1)S(1)} reshape(bf16[2,256,512]{2,1,0:T(8,128)(2,1)} %copy.32) | data formatting | bytes 1048576 | tf_op jit(solution)/shard_map/reshape | solution.py:68
  30.4 1.7 %copy.33 = bf16[8,16,2,16,64]{4,3,2,1,0:T(8,128)(2,1)} copy(bf16[8,16,2,16,64]{4,0,1,3,2:T(8,128)(2,1)S(1)} %bitcast.71) | data formatting | bytes 1048576 | tf_op jit(solution)/shard_map/transpose | solution.py:69
  32.0 2.0 %reshape.214 = bf16[8,16,2048,1]{2,1,0,3:T(8,128)(2,1)S(1)} reshape(bf16[8,16,2,16,64]{4,3,2,1,0:T(8,128)(2,1)} %copy.33) | data formatting | bytes 1048576 | tf_op jit(solution)/shard_map/mk,nk->mn/dot_general | solution.py:82
  34.1 2.0 %convolution_bitcast_fusion = f32[16,8,2,256]{3,0,2,1:T(8,128)S(1)} fusion(bf16[2,256,2048,1]{1,2,0,3:T(8,128)(2,1)} %bitcast.72, bf16[8,16,2048,1]{2,1,0,3:T(8,128)(2,1)S(1)} %reshape.214), kind=kOutput, calls=%fused_computation.8 | convolution fusion | flops 268435456 | bytes 2883584 | tf_op jit(solution)/shard_map/mk,nk->mn/dot_general | solution.py:82
  36.1 0.9 %copy.38 = f32[16,8,2,256]{3,2,1,0:T(2,128)} copy(f32[16,8,2,256]{3,0,2,1:T(8,128)S(1)} %convolution_bitcast_fusion) | data formatting | bytes 524288 | tf_op jit(solution)/shard_map/transpose | solution.py:86
  (36 shorter events, 1.5 us)
Async XLA Ops:
  0.0 10.4 %copy-start = (bf16[8,2,256,256]{3,2,1,0:T(8,128)(2,1)S(1)}, bf16[8,2,256,256]{3,2,1,0:T(8,128)(2,1)}, u32[]{:S(2)}) copy-start(bf16[8,2,256,256]{3,2,1,0:T(8,128)(2,1)} %param.6) | copy-start | bytes 6291460
  0.0 10.0 %copy-start.2 = (s32[256]{0:T(256)S(1)}, s32[256]{0:T(256)}, u32[]{:S(2)}) copy-start(s32[256]{0:T(256)} %param.9) | copy-start | bytes 3076
  0.0 12.2 %collective-permute-start = (s32[2,2]{1,0:T(2,128)}, s32[2,2]{1,0:T(2,128)S(1)}, u32[]{:S(2)}, u32[]{:S(2)}) collective-permute-start(s32[2,2]{1,0:T(2,128)} %bitcast.76), channel_id=1, source_target_pairs={{0,16},{16,0},{1,17},{17,1},{2,18},{18,2},{3,19},{19,3},{4,20},{20... | collective-permute-start | bytes 56 | tf_op jit(solution)/shard_map/ppermute | solution.py:12
  4.9 7.3 %copy-start.3 = (s32[1,2,2]{2,1,0:T(2,128)S(1)}, s32[1,2,2]{2,1,0:T(2,128)}, u32[]{:S(2)}) copy-start(s32[1,2,2]{2,1,0:T(2,128)} %param.8) | copy-start | bytes 52
  4.9 20.9 %all-to-all-start = ((bf16[32,16,512]{2,1,0:T(8,128)(2,1)}), bf16[32,16,512]{2,1,0:T(8,128)(2,1)}, u32[]{:S(2)}, u32[]{:S(2)}) async-start(bf16[32,16,512]{2,1,0:T(8,128)(2,1)} %bitcast.15), calls=%async_computation | async-start | bytes 1048576 | tf_op jit(solution)/shard_map/all_to_all | solution.py:107
  18.5 1.8 %copy-start.1 = (bf16[8,2,128,256]{3,2,1,0:T(8,128)(2,1)S(1)}, bf16[8,2,128,256]{3,2,1,0:T(8,128)(2,1)}, u32[]{:S(2)}) copy-start(bf16[8,2,128,256]{3,2,1,0:T(8,128)(2,1)} %fusion) | copy-start | bytes 3145732

commit v4 on v3

--- a/solution.py
+++ b/solution.py
@@ -1,6 +1,8 @@
 import jax
 import jax.numpy as jnp
 from jax import lax
+from jax.experimental import pallas as pl
+from jax.experimental.pallas import tpu as pltpu
 from jax.sharding import PartitionSpec as P
 
 
@@ -47,6 +49,48 @@
     return jnp.dot(lhs, second_w, preferred_element_type=jnp.float32)
 
 
+def regroup_kernel(stem_ref, weight_ref, out_ref):
+    block_count, rows, _ = stem_ref.shape
+    q_local = weight_ref.shape[1] // 64
+    t_local = 16
+    n_mode = rows // t_local
+    lane = lax.broadcasted_iota(jnp.int32, (t_local, 128), 1)
+    low = lane < 64
+    for b in range(block_count):
+        product = lax.dot_general(
+            stem_ref[b], weight_ref[b], (((1,), (1,)), ((), ())),
+            preferred_element_type=jnp.float32,
+        ).astype(jnp.bfloat16)
+        for pair in range(n_mode // 2):
+            upper = product[(2 * pair) * t_local:(2 * pair + 1) * t_local]
+            lower = product[(2 * pair + 1) * t_local:(2 * pair + 2) * t_local]
+            col = (b * n_mode // 2 + pair) * 128
+            for qp in range(q_local // 2):
+                first = upper[:, qp * 128:(qp + 1) * 128]
+                second = lower[:, qp * 128:(qp + 1) * 128]
+                even = jnp.where(low, first, pltpu.roll(second, 64, 1))
+                odd = jnp.where(low, pltpu.roll(first, 64, 1), second)
+                out_ref[(2 * qp) * t_local:(2 * qp + 1) * t_local, col:col + 128] = even
+                out_ref[(2 * qp + 1) * t_local:(2 * qp + 2) * t_local, col:col + 128] = odd
+
+
+def regroup(stem_rows, first_w, q_local, t_local):
+    block_count, rows, _ = stem_rows.shape
+    n_mode = rows // t_local
+    out_shape = jax.ShapeDtypeStruct((q_local * t_local, block_count * n_mode * 64), jnp.bfloat16)
+    return pl.pallas_call(
+        regroup_kernel,
+        out_shape=out_shape,
+        in_specs=[pl.BlockSpec(memory_space=pltpu.VMEM)] * 2,
+        out_specs=pl.BlockSpec(memory_space=pltpu.VMEM),
+        cost_estimate=pl.CostEstimate(
+            flops=2 * stem_rows.shape[0] * rows * first_w.shape[1] * first_w.shape[2],
+            transcendentals=0,
+            bytes_accessed=2 * (stem_rows.size + first_w.size) + 2 * rows * block_count * first_w.shape[1],
+        ),
+    )(stem_rows, first_w)
+
+
 def stacked_part(stem_rows, first_t, w2_table, first_ids, second_ids, sizes):
     n_mode, t_local, n_cuts, a_count, q_local = sizes
     block_count = stem_rows.shape[0]
@@ -62,13 +106,16 @@
     first_w = jnp.transpose(first_w, (2, 4, 3, 1, 5, 0, 6)).reshape(
         block_count, q_local * group, 2 * width
     )
-    product = jnp.einsum(
-        "brk,bnk->brn", stem_rows, first_w, preferred_element_type=jnp.float32
-    ).astype(jnp.bfloat16)
-    lhs = product.reshape(block_count, n_mode, t_local, q_local, group)
-    lhs = jnp.transpose(lhs, (3, 2, 0, 1, 4)).reshape(
-        q_local * t_local, block_count * n_mode * group
-    )
+    if group == 64 and t_local == 16 and n_mode % 2 == 0 and q_local % 2 == 0:
+        lhs = regroup(stem_rows, first_w, q_local, t_local)
+    else:
+        product = jnp.einsum(
+            "brk,bnk->brn", stem_rows, first_w, preferred_element_type=jnp.float32
+        ).astype(jnp.bfloat16)
+        lhs = product.reshape(block_count, n_mode, t_local, q_local, group)
+        lhs = jnp.transpose(lhs, (3, 2, 0, 1, 4)).reshape(
+            q_local * t_local, block_count * n_mode * group
+        )
     second = jnp.take(w2_table, second_ids.reshape(-1), axis=0)
     second = jnp.swapaxes(second, 2, 3)
     second = second.reshape(block_count, n_cuts, 2, out_width, n_mode, a_count)

time: 37.5 us -> 32.1 us (0.86)
  local copies, waits for them, and re-layouts: 19.7 us -> 12.5 us
  waiting for transfers between devices: 0.17 us -> 3.2 us
  Pallas kernels: 0 us -> 2.74 us
  matrix products: 5.69 us -> 3.02 us
  other arithmetic: 3.3 us -> 2.1 us
    all_to_all x1, waiting for transfers between devices: 0.17 us -> 3.19 us  [on_device(): stem_rows = lax.all_to_all(payload, ('cuts', 'mode'), 0, 0, tiled=True)]
    pallas_call x0 -> x1, Pallas kernels: none -> 2.74 us  [regroup(): pl.pallas_call(regroup_kernel, out_shape=out_shape, in_specs=[pl.BlockSpe...]
    dot_general x1 -> x0, local copies, waits for them, and re-layouts: 2.05 us -> none  [stacked_part(): jnp.einsum('mk,nk->mn', lhs, second_w, preferred_element_type=jnp.float32)]
    dot_general x1 -> x0, matrix products: 1.82 us -> none  [stacked_part(): jnp.einsum('brk,bnk->brn', stem_rows, first_w, preferred_element_type=jnp...]
    transpose x1 -> x0, local copies, waits for them, and re-layouts: 1.68 us -> none  [stacked_part(): jnp.transpose(lhs, (3, 2, 0, 1, 4))]
    reshape x1 -> x0, local copies, waits for them, and re-layouts: 1.64 us -> none  [stacked_part(): lhs = product.reshape(block_count, n_mode, t_local, q_local, group)]
    another operation x1, other arithmetic: 1.38 us -> 0.18 us  [stacked_part(): jnp.stack([jnp.stack([real_two, -imag_two]), jnp.stack([imag_two, real_tw...]
    dot_general x1, matrix products: 1.83 us -> 0.81 us  [on_device(): jnp.einsum('nj,spkj->spnk', picker_t, w1_table, preferred_element_type=jn...]
  transfers between devices with their start and end apart: 2 -> 2, of which waited for: 1 -> 1; matrix products, arithmetic and copies ran while one was open for 47% -> 46% of each run, Pallas kernels for 0% -> 0%
where the time goes in v4:
time: 32.1 us; the launch traced here: 31.7 us
  local copies, waits for them, and re-layouts  12.5 us (39%)
  starting transfers between devices  8 us (25%)
  waiting for transfers between devices  3.2 us (10%)
  matrix products  3.02 us (9%)
  Pallas kernels  2.74 us (9%)
  other arithmetic  2.1 us (7%)
    all_to_all x1, starting transfers between devices, on_device(): stem_rows = lax.all_to_all(payload, ('cuts', 'mode'), 0, 0, tiled=True)  5.06 us
    all_to_all x1, waiting for transfers between devices, on_device(): stem_rows = lax.all_to_all(payload, ('cuts', 'mode'), 0, 0, tiled=True)  3.19 us
    ppermute x1, starting transfers between devices, gather_over_cuts(): current = lax.ppermute(current, 'cuts', ring)  2.94 us
    pallas_call x1, Pallas kernels, regroup(): pl.pallas_call(regroup_kernel, out_shape=out_shape, in_specs=[pl.BlockSpe...  2.74 us
    gather x1, local copies, waits for them, and re-layouts, stacked_part(): second = jnp.take(w2_table, second_ids.reshape(-1), axis=0)  2.21 us
    dot_general x1, matrix products, stacked_part(): jnp.einsum('mk,nk->mn', lhs, second_w, preferred_element_type=jnp.float32)  2.2 us
    broadcast_in_dim x2, local copies, waits for them, and re-layouts, on_device(): payload = jnp.broadcast_to(pieces, (n_cuts, n_mode, t_local, 2 * width))  1.98 us
    transpose x1, local copies, waits for them, and re-layouts, stacked_part(): jnp.transpose(second_w, (0, 4, 2, 5, 3, 1, 6))  1.67 us
  transfers between devices with their start and end apart: 2, of which 1 were waited for; matrix products, arithmetic and copies ran while one was open for 46% of the time, Pallas kernels for 0%

profile of v4, /device:TPU:0, one launch (start us, length us, event | category | flops | bytes accessed | tf_op | source)
XLA Modules:
  0.0 31.7 jit_solution(837957742739560665)
XLA Ops:
  0.0 2.9 %collective-permute-start = (s32[2,2]{1,0:T(2,128)}, s32[2,2]{1,0:T(2,128)S(1)}, u32[]{:S(2)}, u32[]{:S(2)}) collective-permute-start(s32[2,2]{1,0:T(2,128)} %bitcast.70), channel_id=1, source_target_pairs={{0,16},{16,0},{1,17},{17,1},{2,18},{18,2},{3,19},{19,3},{4,20},{20... | collective-permute-start | bytes 56 | tf_op jit(solution)/shard_map/ppermute | solution.py:14
  2.9 1.1 %broadcast_in_dim.34 = bf16[16,16,512]{2,1,0:T(8,128)(2,1)S(1)} reshape(bf16[1,256,2,256]{3,2,1,0:T(2,128)(2,1)} %param.5) | data formatting | bytes 524288 | tf_op jit(solution)/shard_map/broadcast_in_dim | solution.py:152
  4.1 0.9 %broadcast_in_dim.35 = bf16[2,16,16,512]{3,2,1,0:T(8,128)(2,1)} broadcast(bf16[16,16,512]{2,1,0:T(8,128)(2,1)S(1)} %broadcast_in_dim.34), dimensions={1,2,3} | broadcast | bytes 786432 | tf_op jit(solution)/shard_map/broadcast_in_dim | solution.py:152
  4.9 5.1 %all-to-all-start = ((bf16[32,16,512]{2,1,0:T(8,128)(2,1)}), bf16[32,16,512]{2,1,0:T(8,128)(2,1)}, u32[]{:S(2)}, u32[]{:S(2)}) async-start(bf16[32,16,512]{2,1,0:T(8,128)(2,1)} %bitcast), calls=%async_computation | async-start | bytes 1048576 | tf_op jit(solution)/shard_map/all_to_all | solution.py:154
  10.4 0.8 %fusion = bf16[8,2,128,256]{3,2,1,0:T(8,128)(2,1)S(1)} fusion(bf16[8,2,256,256]{3,2,1,0:T(8,128)(2,1)S(1)} %copy-done, s32[128]{0:T(128)S(1)} %eq.17), kind=kOutput, calls=%fused_computation.5 | convolution fusion | flops 268992512 | bytes 3146240 | tf_op jit(solution)/shard_map/nj,spkj->spnk/dot_general | solution.py:175
  11.2 0.6 %gather_fusion = s32[2,2,2]{2,1,0:T(2,128)S(1)} fusion(s32[2,2,2]{2,1,0:T(2,128)S(1)} %pad_add_fusion, s32[1024]{0:T(1024)S(1)} %pad_clamp_fusion.2), kind=kCustom, calls=%fused_computation | custom fusion | bytes 72 | tf_op jit(solution)/shard_map/jit(_take)/gather | solution.py:19
  11.9 0.2 slice_reduce_fusion
  12.1 0.1 copy.17
  12.3 0.1 copy.15
  12.4 1.4 %gather_fusion.1 = bf16[4,2,128,256]{3,2,1,0:T(8,128)(2,1)} fusion(bf16[8,2,128,256]{3,2,1,0:T(8,128)(2,1)S(1)} %fusion, s32[1024]{0:T(1024)S(1)} %pad_clamp_fusion.1), kind=kCustom, calls=%fused_computation.1 | custom fusion | bytes 1048592 | tf_op jit(solution)/shard_map/jit(_take)/gather | solution.py:100
  13.8 1.2 %copy_select_fusion = bf16[2,2,2,8,16,256]{5,4,3,1,0,2:T(8,128)(2,1)S(1)} fusion(bf16[2,2,2,8,16,256]{5,4,3,2,1,0:T(8,128)(2,1)} %bitcast.66, pred[2,2]{1,0:T(4,128)(4,1)S(1)} %copy.15), kind=kLoop, calls=%fused_computation.15 | loop fusion | flops 262144 | bytes 1048580 | tf_op jit(solution)/shard_map/jit(_take)/select_n | solution.py:100
  15.4 0.1 maximum_bitcast_fusion.1
  15.5 1.1 %copy.19 = bf16[2,8,2,2,16,2,256]{6,5,4,3,2,1,0:T(2,128)(2,1)S(1)} copy(bf16[2,8,2,2,16,2,256]{6,4,1,2,0,3,5:T(8,128)(2,1)S(1)} %maximum_bitcast_fusion.1) | data formatting | bytes 2097152 | tf_op jit(solution)/shard_map/transpose | solution.py:106
  16.6 1.5 %reshape.179.weight_ref = bf16[2,512,512]{2,1,0:T(8,128)(2,1)} reshape(bf16[2,8,2,2,16,2,256]{6,5,4,3,2,1,0:T(2,128)(2,1)S(1)} %copy.19) | data formatting | bytes 2097152 | tf_op jit(solution)/shard_map/reshape | solution.py:106
  18.1 2.2 %gather_fusion.2 = bf16[4,2,256,256]{3,2,1,0:T(8,128)(2,1)S(1)} fusion(bf16[8,2,256,256]{3,2,1,0:T(8,128)(2,1)} %param.7, s32[1024]{0:T(1024)S(1)} %pad_clamp_fusion), kind=kCustom, calls=%fused_computation.2 | custom fusion | bytes 2097168 | tf_op jit(solution)/shard_map/jit(_take)/gather | solution.py:119
  20.3 0.2 broadcast_select_fusion
  20.5 0.1 slice_bitcast_fusion
  20.6 0.2 maximum_bitcast_fusion.2
  20.8 0.2 maximum_bitcast_fusion
  21.0 1.7 %copy.22 = bf16[2,256,2,16,2,2,16]{1,6,5,4,3,2,0:T(8,128)(2,1)} copy(bf16[2,256,2,16,2,2,16]{1,6,3,4,2,5,0:T(8,128)(2,1)S(1)} %maximum_bitcast_fusion) | data formatting | bytes 4194304 | tf_op jit(solution)/shard_map/transpose | solution.py:126
  22.7 3.2 %all-to-all-done = bf16[32,16,512]{2,1,0:T(8,128)(2,1)} async-done(((bf16[32,16,512]{2,1,0:T(8,128)(2,1)}), bf16[32,16,512]{2,1,0:T(8,128)(2,1)}, u32[]{:S(2)}, u32[]{:S(2)}) %all-to-all-start) | async-done | bytes 524320 | tf_op jit(solution)/shard_map/all_to_all | solution.py:154
  25.9 2.7 %shard_map.55 = bf16[128,2048]{1,0:T(8,128)(2,1)} custom-call(bf16[2,256,512]{2,1,0:T(8,128)(2,1)} %bitcast.1.stem_ref, bf16[2,512,512]{2,1,0:T(8,128)(2,1)} %reshape.179.weight_ref), custom_call_target="tpu_custom_call" | custom-call | flops 268435456 | bytes 2097152 | tf_op jit(solution)/shard_map/pallas_call | solution.py:81
  28.6 2.2 %convolution_bitcast_fusion = f32[16,8,2,256]{3,0,2,1:T(8,128)S(1)} fusion(bf16[8,16,2048,1]{2,1,3,0:T(8,128)(2,1)} %bitcast.67, bf16[2,256,2048,1]{1,2,0,3:T(8,128)(2,1)} %bitcast.65), kind=kOutput, calls=%fused_computation.6 | convolution fusion | flops 268435456 | bytes 2883584 | tf_op jit(solution)/shard_map/mk,nk->mn/dot_general | solution.py:129
  30.8 0.9 %copy.24 = f32[16,8,2,256]{3,2,1,0:T(2,128)} copy(f32[16,8,2,256]{3,0,2,1:T(8,128)S(1)} %convolution_bitcast_fusion) | data formatting | bytes 524288 | tf_op jit(solution)/shard_map/transpose | solution.py:133
  (30 shorter events, 1.0 us)
Async XLA Ops:
  0.0 10.4 %copy-start = (bf16[8,2,256,256]{3,2,1,0:T(8,128)(2,1)S(1)}, bf16[8,2,256,256]{3,2,1,0:T(8,128)(2,1)}, u32[]{:S(2)}) copy-start(bf16[8,2,256,256]{3,2,1,0:T(8,128)(2,1)} %param.6) | copy-start | bytes 6291460
  0.0 10.0 %copy-start.1 = (s32[256]{0:T(256)S(1)}, s32[256]{0:T(256)}, u32[]{:S(2)}) copy-start(s32[256]{0:T(256)} %param.9) | copy-start | bytes 3076
  0.0 11.2 %collective-permute-start = (s32[2,2]{1,0:T(2,128)}, s32[2,2]{1,0:T(2,128)S(1)}, u32[]{:S(2)}, u32[]{:S(2)}) collective-permute-start(s32[2,2]{1,0:T(2,128)} %bitcast.70), channel_id=1, source_target_pairs={{0,16},{16,0},{1,17},{17,1},{2,18},{18,2},{3,19},{19,3},{4,20},{20... | collective-permute-start | bytes 56 | tf_op jit(solution)/shard_map/ppermute | solution.py:14
  4.9 6.3 %copy-start.2 = (s32[1,2,2]{2,1,0:T(2,128)S(1)}, s32[1,2,2]{2,1,0:T(2,128)}, u32[]{:S(2)}) copy-start(s32[1,2,2]{2,1,0:T(2,128)} %param.8) | copy-start | bytes 52
  4.9 20.9 %all-to-all-start = ((bf16[32,16,512]{2,1,0:T(8,128)(2,1)}), bf16[32,16,512]{2,1,0:T(8,128)(2,1)}, u32[]{:S(2)}, u32[]{:S(2)}) async-start(bf16[32,16,512]{2,1,0:T(8,128)(2,1)} %bitcast), calls=%async_computation | async-start | bytes 1048576 | tf_op jit(solution)/shard_map/all_to_all | solution.py:154

commit v5 on v4

--- a/solution.py
+++ b/solution.py
@@ -49,7 +49,7 @@
     return jnp.dot(lhs, second_w, preferred_element_type=jnp.float32)
 
 
-def regroup_kernel(stem_ref, weight_ref, out_ref):
+def regroup_kernel(stem_ref, weight_ref, second_ref, out_ref, lhs_ref):
     block_count, rows, _ = stem_ref.shape
     q_local = weight_ref.shape[1] // 64
     t_local = 16
@@ -70,26 +70,34 @@
                 second = lower[:, qp * 128:(qp + 1) * 128]
                 even = jnp.where(low, first, pltpu.roll(second, 64, 1))
                 odd = jnp.where(low, pltpu.roll(first, 64, 1), second)
-                out_ref[(2 * qp) * t_local:(2 * qp + 1) * t_local, col:col + 128] = even
-                out_ref[(2 * qp + 1) * t_local:(2 * qp + 2) * t_local, col:col + 128] = odd
-
-
-def regroup(stem_rows, first_w, q_local, t_local):
+                lhs_ref[(2 * qp) * t_local:(2 * qp + 1) * t_local, col:col + 128] = even
+                lhs_ref[(2 * qp + 1) * t_local:(2 * qp + 2) * t_local, col:col + 128] = odd
+    out_ref[...] = lax.dot_general(
+        lhs_ref[...], second_ref[...], (((1,), (1,)), ((), ())),
+        preferred_element_type=jnp.float32,
+    )
+
+
+def regroup(stem_rows, first_w, second_w, q_local, t_local):
     block_count, rows, _ = stem_rows.shape
     n_mode = rows // t_local
-    out_shape = jax.ShapeDtypeStruct((q_local * t_local, block_count * n_mode * 64), jnp.bfloat16)
+    lhs_shape = (q_local * t_local, block_count * n_mode * 64)
+    out_shape = jax.ShapeDtypeStruct((q_local * t_local, second_w.shape[0]), jnp.float32)
+    flops = 2 * block_count * rows * first_w.shape[1] * first_w.shape[2]
+    flops += 2 * lhs_shape[0] * lhs_shape[1] * second_w.shape[0]
     return pl.pallas_call(
         regroup_kernel,
         out_shape=out_shape,
-        in_specs=[pl.BlockSpec(memory_space=pltpu.VMEM)] * 2,
+        in_specs=[pl.BlockSpec(memory_space=pltpu.VMEM)] * 3,
         out_specs=pl.BlockSpec(memory_space=pltpu.VMEM),
+        scratch_shapes=[pltpu.VMEM(lhs_shape, jnp.bfloat16)],
         cost_estimate=pl.CostEstimate(
-            flops=2 * stem_rows.shape[0] * rows * first_w.shape[1] * first_w.shape[2],
+            flops=flops,
             transcendentals=0,
-            bytes_accessed=2 * (stem_rows.size + first_w.size) + 2 * rows * block_count * first_w.shape[1],
+            bytes_accessed=2 * (stem_rows.size + first_w.size + second_w.size)
+            + 4 * lhs_shape[0] * second_w.shape[0],
         ),
-    )(stem_rows, first_w)
-
+    )(stem_rows, first_w, second_w)
 
 def stacked_part(stem_rows, first_t, w2_table, first_ids, second_ids, sizes):
     n_mode, t_local, n_cuts, a_count, q_local = sizes
@@ -106,8 +114,18 @@
     first_w = jnp.transpose(first_w, (2, 4, 3, 1, 5, 0, 6)).reshape(
         block_count, q_local * group, 2 * width
     )
+    second = jnp.take(w2_table, second_ids.reshape(-1), axis=0)
+    second = jnp.swapaxes(second, 2, 3)
+    second = second.reshape(block_count, n_cuts, 2, out_width, n_mode, a_count)
+    real_two, imag_two = second[:, :, 0], second[:, :, 1]
+    second_w = jnp.stack(
+        [jnp.stack([real_two, -imag_two]), jnp.stack([imag_two, real_two])]
+    )
+    second_w = jnp.transpose(second_w, (0, 4, 2, 5, 3, 1, 6)).reshape(
+        2 * out_width, block_count * n_mode * group
+    )
     if group == 64 and t_local == 16 and n_mode % 2 == 0 and q_local % 2 == 0:
-        lhs = regroup(stem_rows, first_w, q_local, t_local)
+        amplitude = regroup(stem_rows, first_w, second_w, q_local, t_local)
     else:
         product = jnp.einsum(
             "brk,bnk->brn", stem_rows, first_w, preferred_element_type=jnp.float32
@@ -116,21 +134,12 @@
         lhs = jnp.transpose(lhs, (3, 2, 0, 1, 4)).reshape(
             q_local * t_local, block_count * n_mode * group
         )
-    second = jnp.take(w2_table, second_ids.reshape(-1), axis=0)
-    second = jnp.swapaxes(second, 2, 3)
-    second = second.reshape(block_count, n_cuts, 2, out_width, n_mode, a_count)
-    real_two, imag_two = second[:, :, 0], second[:, :, 1]
-    second_w = jnp.stack(
-        [jnp.stack([real_two, -imag_two]), jnp.stack([imag_two, real_two])]
-    )
-    second_w = jnp.transpose(second_w, (0, 4, 2, 5, 3, 1, 6)).reshape(
-        2 * out_width, block_count * n_mode * group
-    )
-    amplitude = jnp.einsum(
-        "mk,nk->mn", lhs, second_w, preferred_element_type=jnp.float32
-    )
+        amplitude = jnp.einsum(
+            "mk,nk->mn", lhs, second_w, preferred_element_type=jnp.float32
+        )
     amplitude = amplitude.reshape(q_local, t_local, 2, out_width)
     return jnp.transpose(amplitude, (1, 0, 2, 3))
+
 
 def on_device(stem_blocks, w1_table, w2_table, slice_ids, mode_perm):
     n_mode = lax.axis_size("mode")

time: 32.1 us -> 42.3 us (1.32)
  local copies, waits for them, and re-layouts: 12.5 us -> 23.3 us
  waiting for transfers between devices: 3.2 us -> 0.01 us
  other arithmetic: 2.1 us -> 4.63 us
  matrix products: 3.02 us -> 1.81 us
  Pallas kernels: 2.74 us -> 3.89 us
    reshape x0 -> x3, local copies, waits for them, and re-layouts: none -> 5.92 us  [the longest x1 4.04 us: stacked_part(): jnp.transpose(second_w, (0, 4, 2, 5, 3, 1, 6))]
    all_to_all x1, waiting for transfers between devices: 3.19 us -> 0.01 us  [on_device(): stem_rows = lax.all_to_all(payload, ('cuts', 'mode'), 0, 0, tiled=True)]
    transpose x1, local copies, waits for them, and re-layouts: 1.67 us -> 4.83 us  [stacked_part(): jnp.transpose(second_w, (0, 4, 2, 5, 3, 1, 6))]
    dot_general x1 -> x0, matrix products: 2.2 us -> none  [stacked_part(): jnp.einsum('mk,nk->mn', lhs, second_w, preferred_element_type=jnp.float32)]
    unnamed x6 -> x9, local copies, waits for them, and re-layouts: 0.01 us -> 1.85 us
    transpose x1, other arithmetic: 0.19 us -> 1.54 us  [stacked_part(): jnp.transpose(second_w, (0, 4, 2, 5, 3, 1, 6))]
    another operation x1, other arithmetic: 0.18 us -> 1.38 us  [stacked_part(): jnp.stack([jnp.stack([real_two, -imag_two]), jnp.stack([imag_two, real_tw...]
    pallas_call x1, Pallas kernels: 2.74 us -> 3.89 us  [regroup(): pl.pallas_call(regroup_kernel, out_shape=out_shape, in_specs=[pl.BlockSpe...]
  transfers between devices with their start and end apart: 2 -> 2, of which waited for: 1 -> 0; matrix products, arithmetic and copies ran while one was open for 46% -> 67% of each run, Pallas kernels for 0% -> 0%
where the time goes in v5:
time: 42.3 us; the launch traced here: 41.8 us
  local copies, waits for them, and re-layouts  23.3 us (55%)
  starting transfers between devices  8 us (19%)
  other arithmetic  4.63 us (11%)
  Pallas kernels  3.89 us (9%)
  matrix products  1.81 us (4%)
    all_to_all x1, starting transfers between devices, on_device(): stem_rows = lax.all_to_all(payload, ('cuts', 'mode'), 0, 0, tiled=True)  5.06 us
    transpose x1, local copies, waits for them, and re-layouts, stacked_part(): jnp.transpose(second_w, (0, 4, 2, 5, 3, 1, 6))  4.83 us
    reshape x1, local copies, waits for them, and re-layouts, stacked_part(): jnp.transpose(second_w, (0, 4, 2, 5, 3, 1, 6))  4.04 us
    pallas_call x1, Pallas kernels, regroup(): pl.pallas_call(regroup_kernel, out_shape=out_shape, in_specs=[pl.BlockSpe...  3.89 us
    ppermute x1, starting transfers between devices, gather_over_cuts(): current = lax.ppermute(current, 'cuts', ring)  2.94 us
    gather x1, local copies, waits for them, and re-layouts, stacked_part(): second = jnp.take(w2_table, second_ids.reshape(-1), axis=0)  2.21 us
    broadcast_in_dim x2, local copies, waits for them, and re-layouts, on_device(): payload = jnp.broadcast_to(pieces, (n_cuts, n_mode, t_local, 2 * width))  1.97 us
    reshape x2, local copies, waits for them, and re-layouts, stacked_part(): amplitude = amplitude.reshape(q_local, t_local, 2, out_width)  1.88 us
  transfers between devices with their start and end apart: 2, of which 0 were waited for; matrix products, arithmetic and copies ran while one was open for 67% of the time, Pallas kernels for 0%

profile of v5, /device:TPU:0, one launch (start us, length us, event | category | flops | bytes accessed | tf_op | source)
XLA Modules:
  0.0 41.8 jit_solution(4728135194616748690)
XLA Ops:
  0.0 2.9 %collective-permute-start = (s32[2,2]{1,0:T(2,128)}, s32[2,2]{1,0:T(2,128)S(1)}, u32[]{:S(2)}, u32[]{:S(2)}) collective-permute-start(s32[2,2]{1,0:T(2,128)} %bitcast.66), channel_id=1, source_target_pairs={{0,16},{16,0},{1,17},{17,1},{2,18},{18,2},{3,19},{19,3},{4,20},{20... | collective-permute-start | bytes 56 | tf_op jit(solution)/shard_map/ppermute | solution.py:14
  2.9 1.1 %broadcast_in_dim.34 = bf16[16,16,512]{2,1,0:T(8,128)(2,1)S(1)} reshape(bf16[1,256,2,256]{3,2,1,0:T(2,128)(2,1)} %param.5) | data formatting | bytes 524288 | tf_op jit(solution)/shard_map/broadcast_in_dim | solution.py:161
  4.1 0.9 %broadcast_in_dim.35 = bf16[2,16,16,512]{3,2,1,0:T(8,128)(2,1)} broadcast(bf16[16,16,512]{2,1,0:T(8,128)(2,1)S(1)} %broadcast_in_dim.34), dimensions={1,2,3} | broadcast | bytes 786432 | tf_op jit(solution)/shard_map/broadcast_in_dim | solution.py:161
  4.9 5.1 %all-to-all-start = ((bf16[32,16,512]{2,1,0:T(8,128)(2,1)}), bf16[32,16,512]{2,1,0:T(8,128)(2,1)}, u32[]{:S(2)}, u32[]{:S(2)}) async-start(bf16[32,16,512]{2,1,0:T(8,128)(2,1)} %bitcast), calls=%async_computation | async-start | bytes 1048576 | tf_op jit(solution)/shard_map/all_to_all | solution.py:163
  10.4 1.8 %fusion = bf16[8,2,128,256]{3,2,1,0:T(8,128)(2,1)} fusion(bf16[8,2,256,256]{3,2,1,0:T(8,128)(2,1)S(1)} %copy-done, s32[128]{0:T(128)S(1)} %eq.17), kind=kOutput, calls=%fused_computation.5 | convolution fusion | flops 268992512 | bytes 3146240 | tf_op jit(solution)/shard_map/nj,spkj->spnk/dot_general | solution.py:184
  12.2 0.6 %gather_fusion = s32[2,2,2]{2,1,0:T(2,128)S(1)} fusion(s32[2,2,2]{2,1,0:T(2,128)S(1)} %pad_add_fusion, s32[1024]{0:T(1024)S(1)} %pad_clamp_fusion.2), kind=kCustom, calls=%fused_computation | custom fusion | bytes 72 | tf_op jit(solution)/shard_map/jit(_take)/gather | solution.py:19
  12.8 0.2 slice_reduce_fusion
  13.3 2.2 %gather_fusion.2 = bf16[4,2,256,256]{3,2,1,0:T(8,128)(2,1)S(1)} fusion(bf16[8,2,256,256]{3,2,1,0:T(8,128)(2,1)} %param.7, s32[1024]{0:T(1024)S(1)} %pad_clamp_fusion), kind=kCustom, calls=%fused_computation.2 | custom fusion | bytes 2097168 | tf_op jit(solution)/shard_map/jit(_take)/gather | solution.py:117
  15.6 0.2 broadcast_select_fusion
  15.8 0.9 %slice_bitcast_fusion = (bf16[1,2,2,256,16,16]{3,5,4,2,1,0:T(8,128)(2,1)S(1)}, bf16[1,2,2,256,16,16]{3,5,4,2,1,0:T(8,128)(2,1)}) fusion(bf16[2,2,2,256,16,16]{3,5,4,2,1,0:T(8,128)(2,1)S(1)} %bitcast.62), kind=kLoop, calls=%fused_computation.10 | loop fusion | bytes 2097152 | tf_op jit(solution)/shard_map/squeeze | solution.py:120
  16.9 1.4 %maximum_bitcast_fusion.2 = (bf16[1,2,2,2,256,16,16]{4,6,5,3,2,1,0:T(8,128)(2,1)S(1)}, bf16[1,2,2,2,256,16,16]{4,6,5,3,2,1,0:T(8,128)(2,1)S(1)}) fusion(bf16[1,2,2,256,16,16]{3,5,4,2,1,0:T(8,128)(2,1)S(1)} %fusion.10, bf16[1,2,2,256,16,16]{3,5,4,2,1,0:T(8,128)(2,1)} %get-tuple-element.8, bf16[1,2,2,256,16,16]{3,5,4,2,1,0:T(8,128)(2,1)S(1)} %get-tuple-element.7), kind=kLoop, calls=%fused_computation.7 | loop fusion | flops 1048576 | bytes 3670016 | tf_op jit(solution)/shard_map/stack | solution.py:121
  18.2 1.5 %maximum_bitcast_fusion = bf16[2,256,2,16,2,2,16]{1,6,3,4,2,5,0:T(8,128)(2,1)} fusion(bf16[1,2,2,2,256,16,16]{4,6,5,3,2,1,0:T(8,128)(2,1)S(1)} %get-tuple-element.10, bf16[1,2,2,2,256,16,16]{4,6,5,3,2,1,0:T(8,128)(2,1)S(1)} %get-tuple-element.9), kind=kLoop, calls=%fused_computation.3 | loop fusion | flops 1048576 | bytes 4194304 | tf_op jit(solution)/shard_map/transpose | solution.py:124
  19.8 0.1 copy.15
  19.9 4.8 %copy.22 = bf16[2,256,2,16,2,2,16]{1,0,6,5,4,3,2:T(2,128)(2,1)S(1)} copy(bf16[2,256,2,16,2,2,16]{1,6,3,4,2,5,0:T(8,128)(2,1)} %maximum_bitcast_fusion) | data formatting | bytes 4194304 | tf_op jit(solution)/shard_map/transpose | solution.py:124
  24.7 1.8 %copy.26 = bf16[256,8,2,256]{3,1,2,0:T(8,128)(2,1)} copy(bf16[256,8,2,256]{3,2,1,0:T(2,128)(2,1)S(1)} %bitcast.59) | data formatting | bytes 4194304
  26.6 4.0 %copy.23.second_ref = bf16[512,2048]{1,0:T(8,128)(2,1)} copy(bf16[512,2048]{0,1:T(8,128)(2,1)} %bitcast.60) | data formatting | bytes 4194304 | tf_op jit(solution)/shard_map/reshape | solution.py:124
  30.6 1.4 %gather_fusion.1 = bf16[4,2,128,256]{3,2,1,0:T(8,128)(2,1)} fusion(bf16[8,2,128,256]{3,2,1,0:T(8,128)(2,1)S(1)} %copy-done.1, s32[1024]{0:T(1024)S(1)} %pad_clamp_fusion.1), kind=kCustom, calls=%fused_computation.1 | custom fusion | bytes 1048592 | tf_op jit(solution)/shard_map/jit(_take)/gather | solution.py:108
  32.0 1.2 %copy_select_fusion = bf16[2,2,2,8,16,256]{5,4,3,1,0,2:T(8,128)(2,1)S(1)} fusion(bf16[2,2,2,8,16,256]{5,4,3,2,1,0:T(8,128)(2,1)} %bitcast.63, pred[2,2]{1,0:T(4,128)(4,1)S(1)} %copy.15), kind=kLoop, calls=%fused_computation.14 | loop fusion | flops 262144 | bytes 1048580 | tf_op jit(solution)/shard_map/jit(_take)/select_n | solution.py:108
  33.3 0.1 maximum_bitcast_fusion.1
  33.4 1.1 %copy.19 = bf16[2,8,2,2,16,2,256]{6,5,4,3,2,1,0:T(2,128)(2,1)S(1)} copy(bf16[2,8,2,2,16,2,256]{6,4,1,2,0,3,5:T(8,128)(2,1)S(1)} %maximum_bitcast_fusion.1) | data formatting | bytes 2097152 | tf_op jit(solution)/shard_map/transpose | solution.py:114
  34.5 1.5 %reshape.180.weight_ref = bf16[2,512,512]{2,1,0:T(8,128)(2,1)} reshape(bf16[2,8,2,2,16,2,256]{6,5,4,3,2,1,0:T(2,128)(2,1)S(1)} %copy.19) | data formatting | bytes 2097152 | tf_op jit(solution)/shard_map/reshape | solution.py:114
  36.0 3.9 %shard_map.55 = f32[128,512]{1,0:T(8,128)} custom-call(bf16[2,256,512]{2,1,0:T(8,128)(2,1)} %bitcast.1.stem_ref, bf16[2,512,512]{2,1,0:T(8,128)(2,1)} %reshape.180.weight_ref, bf16[512,2048]{1,0:T(8,128)(2,1)} %copy.23.second_ref), custom_call_target="tpu_custom_call" | custom-call | flops 536870912 | bytes 3932160 | tf_op jit(solution)/shard_map/pallas_call | solution.py:88
  39.9 1.1 %reshape.185 = f32[8,16,2,256]{3,2,1,0:T(2,128)S(1)} reshape(f32[128,512]{1,0:T(8,128)} %shard_map.55) | data formatting | bytes 524288 | tf_op jit(solution)/shard_map/reshape | solution.py:140
  41.0 0.8 %copy.29 = f32[8,16,2,256]{3,2,0,1:T(2,128)} copy(f32[8,16,2,256]{3,2,1,0:T(2,128)S(1)} %reshape.185) | data formatting | bytes 524288 | tf_op jit(solution)/shard_map/reshape | solution.py:140
  (34 shorter events, 1.1 us)
Async XLA Ops:
  0.0 10.4 %copy-start = (bf16[8,2,256,256]{3,2,1,0:T(8,128)(2,1)S(1)}, bf16[8,2,256,256]{3,2,1,0:T(8,128)(2,1)}, u32[]{:S(2)}) copy-start(bf16[8,2,256,256]{3,2,1,0:T(8,128)(2,1)} %param.6) | copy-start | bytes 6291460
  0.0 10.0 %copy-start.2 = (s32[256]{0:T(256)S(1)}, s32[256]{0:T(256)}, u32[]{:S(2)}) copy-start(s32[256]{0:T(256)} %param.9) | copy-start | bytes 3076
  0.0 12.2 %collective-permute-start = (s32[2,2]{1,0:T(2,128)}, s32[2,2]{1,0:T(2,128)S(1)}, u32[]{:S(2)}, u32[]{:S(2)}) collective-permute-start(s32[2,2]{1,0:T(2,128)} %bitcast.66), channel_id=1, source_target_pairs={{0,16},{16,0},{1,17},{17,1},{2,18},{18,2},{3,19},{19,3},{4,20},{20... | collective-permute-start | bytes 56 | tf_op jit(solution)/shard_map/ppermute | solution.py:14
  4.9 7.3 %copy-start.3 = (s32[1,2,2]{2,1,0:T(2,128)S(1)}, s32[1,2,2]{2,1,0:T(2,128)}, u32[]{:S(2)}) copy-start(s32[1,2,2]{2,1,0:T(2,128)} %param.8) | copy-start | bytes 52
  4.9 31.1 %all-to-all-start = ((bf16[32,16,512]{2,1,0:T(8,128)(2,1)}), bf16[32,16,512]{2,1,0:T(8,128)(2,1)}, u32[]{:S(2)}, u32[]{:S(2)}) async-start(bf16[32,16,512]{2,1,0:T(8,128)(2,1)} %bitcast), calls=%async_computation | async-start | bytes 1048576 | tf_op jit(solution)/shard_map/all_to_all | solution.py:163
  26.6 4.0 %copy-start.1 = (bf16[8,2,128,256]{3,2,1,0:T(8,128)(2,1)S(1)}, bf16[8,2,128,256]{3,2,1,0:T(8,128)(2,1)}, u32[]{:S(2)}) copy-start(bf16[8,2,128,256]{3,2,1,0:T(8,128)(2,1)} %fusion) | copy-start | bytes 3145732

commit v6 on v5

--- a/solution.py
+++ b/solution.py
@@ -72,9 +72,8 @@
                 odd = jnp.where(low, pltpu.roll(first, 64, 1), second)
                 lhs_ref[(2 * qp) * t_local:(2 * qp + 1) * t_local, col:col + 128] = even
                 lhs_ref[(2 * qp + 1) * t_local:(2 * qp + 2) * t_local, col:col + 128] = odd
-    out_ref[...] = lax.dot_general(
-        lhs_ref[...], second_ref[...], (((1,), (1,)), ((), ())),
-        preferred_element_type=jnp.float32,
+    out_ref[...] = jnp.dot(
+        lhs_ref[...], second_ref[...], preferred_element_type=jnp.float32
     )
 
 
@@ -82,9 +81,9 @@
     block_count, rows, _ = stem_rows.shape
     n_mode = rows // t_local
     lhs_shape = (q_local * t_local, block_count * n_mode * 64)
-    out_shape = jax.ShapeDtypeStruct((q_local * t_local, second_w.shape[0]), jnp.float32)
+    out_shape = jax.ShapeDtypeStruct((q_local * t_local, second_w.shape[1]), jnp.float32)
     flops = 2 * block_count * rows * first_w.shape[1] * first_w.shape[2]
-    flops += 2 * lhs_shape[0] * lhs_shape[1] * second_w.shape[0]
+    flops += 2 * lhs_shape[0] * lhs_shape[1] * second_w.shape[1]
     return pl.pallas_call(
         regroup_kernel,
         out_shape=out_shape,
@@ -95,7 +94,7 @@
             flops=flops,
             transcendentals=0,
             bytes_accessed=2 * (stem_rows.size + first_w.size + second_w.size)
-            + 4 * lhs_shape[0] * second_w.shape[0],
+            + 4 * lhs_shape[0] * second_w.shape[1],
         ),
     )(stem_rows, first_w, second_w)
 
@@ -114,19 +113,28 @@
     first_w = jnp.transpose(first_w, (2, 4, 3, 1, 5, 0, 6)).reshape(
         block_count, q_local * group, 2 * width
     )
-    second = jnp.take(w2_table, second_ids.reshape(-1), axis=0)
-    second = jnp.swapaxes(second, 2, 3)
-    second = second.reshape(block_count, n_cuts, 2, out_width, n_mode, a_count)
-    real_two, imag_two = second[:, :, 0], second[:, :, 1]
-    second_w = jnp.stack(
-        [jnp.stack([real_two, -imag_two]), jnp.stack([imag_two, real_two])]
-    )
-    second_w = jnp.transpose(second_w, (0, 4, 2, 5, 3, 1, 6)).reshape(
-        2 * out_width, block_count * n_mode * group
-    )
     if group == 64 and t_local == 16 and n_mode % 2 == 0 and q_local % 2 == 0:
+        second = jnp.take(w2_table, second_ids.reshape(-1), axis=0)
+        second = second.reshape(block_count, n_cuts, 2, n_mode, a_count, out_width)
+        real_two, imag_two = second[:, :, 0], second[:, :, 1]
+        second_w = jnp.stack(
+            [jnp.stack([real_two, imag_two]), jnp.stack([-imag_two, real_two])]
+        )
+        second_w = jnp.transpose(second_w, (2, 4, 3, 0, 5, 1, 6)).reshape(
+            block_count * n_mode * group, 2 * out_width
+        )
         amplitude = regroup(stem_rows, first_w, second_w, q_local, t_local)
     else:
+        second = jnp.take(w2_table, second_ids.reshape(-1), axis=0)
+        second = jnp.swapaxes(second, 2, 3)
+        second = second.reshape(block_count, n_cuts, 2, out_width, n_mode, a_count)
+        real_two, imag_two = second[:, :, 0], second[:, :, 1]
+        second_w = jnp.stack(
+            [jnp.stack([real_two, -imag_two]), jnp.stack([imag_two, real_two])]
+        )
+        second_w = jnp.transpose(second_w, (0, 4, 2, 5, 3, 1, 6)).reshape(
+            2 * out_width, block_count * n_mode * group
+        )
         product = jnp.einsum(
             "brk,bnk->brn", stem_rows, first_w, preferred_element_type=jnp.float32
         ).astype(jnp.bfloat16)

time: 42.3 us -> 35 us (0.83)
  local copies, waits for them, and re-layouts: 23.3 us -> 17.8 us
  other arithmetic: 4.63 us -> 3.31 us
    reshape x1 -> x0, local copies, waits for them, and re-layouts: 4.04 us -> none  [stacked_part(): jnp.transpose(second_w, (0, 4, 2, 5, 3, 1, 6))]
    transpose x1, local copies, waits for them, and re-layouts: 4.83 us -> 3.24 us  [stacked_part(): jnp.transpose(second_w, (2, 4, 3, 0, 5, 1, 6))]
    transpose x1, other arithmetic: 1.54 us -> 0.19 us  [stacked_part(): jnp.transpose(second_w, (2, 4, 3, 0, 5, 1, 6))]
    squeeze x1 -> x0, local copies, waits for them, and re-layouts: 0.89 us -> none  [stacked_part(): real_two, imag_two = (second[:, :, 0], second[:, :, 1])]
    another operation x0 -> x1, local copies, waits for them, and re-layouts: none -> 0.89 us  [stacked_part(): jnp.stack([real_two, imag_two])]
    gather x1 -> x2, local copies, waits for them, and re-layouts: 2.21 us -> 2.28 us  [stacked_part(): second = jnp.take(w2_table, second_ids.reshape(-1), axis=0)]
  transfers between devices with their start and end apart: 2 -> 2, of which waited for: 0 -> 0; matrix products, arithmetic and copies ran while one was open for 67% -> 61% of each run, Pallas kernels for 0% -> 0%
where the time goes in v6:
time: 35 us; the launch traced here: 34.6 us
  local copies, waits for them, and re-layouts  17.8 us (51%)
  starting transfers between devices  8 us (23%)
  Pallas kernels  3.53 us (10%)
  other arithmetic  3.31 us (9%)
  matrix products  1.81 us (5%)
    all_to_all x1, starting transfers between devices, on_device(): stem_rows = lax.all_to_all(payload, ('cuts', 'mode'), 0, 0, tiled=True)  5.06 us
    pallas_call x1, Pallas kernels, regroup(): pl.pallas_call(regroup_kernel, out_shape=out_shape, in_specs=[pl.BlockSpe...  3.53 us
    transpose x1, local copies, waits for them, and re-layouts, stacked_part(): jnp.transpose(second_w, (2, 4, 3, 0, 5, 1, 6))  3.24 us
    ppermute x1, starting transfers between devices, gather_over_cuts(): current = lax.ppermute(current, 'cuts', ring)  2.94 us
    gather x2, local copies, waits for them, and re-layouts, stacked_part(): second = jnp.take(w2_table, second_ids.reshape(-1), axis=0)  2.28 us
    broadcast_in_dim x2, local copies, waits for them, and re-layouts, on_device(): payload = jnp.broadcast_to(pieces, (n_cuts, n_mode, t_local, 2 * width))  1.96 us
    reshape x2, local copies, waits for them, and re-layouts, stacked_part(): amplitude = amplitude.reshape(q_local, t_local, 2, out_width)  1.88 us
    unnamed x9, local copies, waits for them, and re-layouts  1.88 us
  transfers between devices with their start and end apart: 2, of which 0 were waited for; matrix products, arithmetic and copies ran while one was open for 61% of the time, Pallas kernels for 0%

profile of v6, /device:TPU:0, one launch (start us, length us, event | category | flops | bytes accessed | tf_op | source)
XLA Modules:
  0.0 34.6 jit_solution(12243554141576168895)
XLA Ops:
  0.0 2.9 %collective-permute-start = (s32[2,2]{1,0:T(2,128)}, s32[2,2]{1,0:T(2,128)S(1)}, u32[]{:S(2)}, u32[]{:S(2)}) collective-permute-start(s32[2,2]{1,0:T(2,128)} %bitcast.62), channel_id=1, source_target_pairs={{0,16},{16,0},{1,17},{17,1},{2,18},{18,2},{3,19},{19,3},{4,20},{20... | collective-permute-start | bytes 56 | tf_op jit(solution)/shard_map/ppermute | solution.py:14
  2.9 1.1 %broadcast_in_dim.34 = bf16[16,16,512]{2,1,0:T(8,128)(2,1)S(1)} reshape(bf16[1,256,2,256]{3,2,1,0:T(2,128)(2,1)} %param.5) | data formatting | bytes 524288 | tf_op jit(solution)/shard_map/broadcast_in_dim | solution.py:169
  4.1 0.8 %broadcast_in_dim.35 = bf16[2,16,16,512]{3,2,1,0:T(8,128)(2,1)} broadcast(bf16[16,16,512]{2,1,0:T(8,128)(2,1)S(1)} %broadcast_in_dim.34), dimensions={1,2,3} | broadcast | bytes 786432 | tf_op jit(solution)/shard_map/broadcast_in_dim | solution.py:169
  4.9 5.1 %all-to-all-start = ((bf16[32,16,512]{2,1,0:T(8,128)(2,1)}), bf16[32,16,512]{2,1,0:T(8,128)(2,1)}, u32[]{:S(2)}, u32[]{:S(2)}) async-start(bf16[32,16,512]{2,1,0:T(8,128)(2,1)} %bitcast), calls=%async_computation | async-start | bytes 1048576 | tf_op jit(solution)/shard_map/all_to_all | solution.py:171
  10.4 1.8 %fusion = bf16[8,2,128,256]{3,2,1,0:T(8,128)(2,1)} fusion(bf16[8,2,256,256]{3,2,1,0:T(8,128)(2,1)S(1)} %copy-done, s32[128]{0:T(128)S(1)} %eq.17), kind=kOutput, calls=%fused_computation.5 | convolution fusion | flops 268992512 | bytes 3146240 | tf_op jit(solution)/shard_map/nj,spkj->spnk/dot_general | solution.py:192
  12.2 0.6 %gather_fusion = s32[2,2,2]{2,1,0:T(2,128)S(1)} fusion(s32[2,2,2]{2,1,0:T(2,128)S(1)} %pad_add_fusion, s32[1024]{0:T(1024)S(1)} %pad_clamp_fusion.2), kind=kCustom, calls=%fused_computation | custom fusion | bytes 72 | tf_op jit(solution)/shard_map/jit(_take)/gather | solution.py:19
  12.8 0.2 slice_reduce_fusion
  13.1 0.1 copy.20
  13.4 2.2 %gather_fusion.2 = bf16[4,2,256,256]{3,2,1,0:T(8,128)(2,1)S(1)} fusion(bf16[8,2,256,256]{3,2,1,0:T(8,128)(2,1)} %param.7, s32[1024]{0:T(1024)S(1)} %pad_clamp_fusion), kind=kCustom, calls=%fused_computation.2 | custom fusion | bytes 2097168 | tf_op jit(solution)/shard_map/jit(_take)/gather | solution.py:117
  15.7 0.2 broadcast_select_fusion
  15.8 0.9 %slice_bitcast_fusion = (bf16[1,2,2,16,16,256]{5,4,3,2,1,0:T(8,128)(2,1)S(1)}, bf16[1,2,2,16,16,256]{5,4,3,2,1,0:T(8,128)(2,1)}) fusion(bf16[2,2,2,16,16,256]{5,4,3,1,0,2:T(8,128)(2,1)S(1)} %broadcast_select_fusion), kind=kLoop, calls=%fused_computation.10 | loop fusion | bytes 2097152 | tf_op jit(solution)/shard_map/stack;squeeze | solution.py:121
  16.9 1.4 %maximum_bitcast_fusion.2 = (bf16[1,2,2,2,16,16,256]{6,5,4,3,2,1,0:T(8,128)(2,1)S(1)}, bf16[1,2,2,2,16,16,256]{6,5,4,3,2,1,0:T(8,128)(2,1)S(1)}) fusion(bf16[1,2,2,16,16,256]{5,4,3,2,1,0:T(8,128)(2,1)S(1)} %get-tuple-element.7, bf16[1,2,2,16,16,256]{5,4,3,2,1,0:T(8,128)(2,1)} %get-tuple-element.8, bf16[1,2,2,16,16,256]{5,4,3,2,1,0:T(8,128)(2,1)S(1)} %fusion.10), kind=kLoop, calls=%fused_computation.7 | loop fusion | flops 1048576 | bytes 3670016 | tf_op jit(solution)/shard_map/stack | solution.py:120
  18.3 0.2 maximum_bitcast_fusion
  18.6 3.2 %copy.23 = bf16[2,16,2,2,16,2,256]{6,5,4,3,2,1,0:T(2,128)(2,1)S(1)} copy(bf16[2,16,2,2,16,2,256]{6,4,1,2,0,5,3:T(8,128)(2,1)S(1)} %maximum_bitcast_fusion) | data formatting | bytes 4194304 | tf_op jit(solution)/shard_map/transpose | solution.py:123
  21.8 1.9 %copy.26 = bf16[256,8,2,256]{3,1,2,0:T(8,128)(2,1)} copy(bf16[256,8,2,256]{3,2,1,0:T(2,128)(2,1)S(1)} %bitcast.57) | data formatting | bytes 4194304
  23.7 0.1 copy.15
  23.8 1.4 %gather_fusion.1 = bf16[4,2,128,256]{3,2,1,0:T(8,128)(2,1)} fusion(bf16[8,2,128,256]{3,2,1,0:T(8,128)(2,1)S(1)} %copy-done.1, s32[1024]{0:T(1024)S(1)} %pad_clamp_fusion.1), kind=kCustom, calls=%fused_computation.1 | custom fusion | bytes 1048592 | tf_op jit(solution)/shard_map/jit(_take)/gather | solution.py:107
  25.2 1.2 %copy_select_fusion = bf16[2,2,2,8,16,256]{5,4,3,1,0,2:T(8,128)(2,1)S(1)} fusion(bf16[2,2,2,8,16,256]{5,4,3,2,1,0:T(8,128)(2,1)} %bitcast.59, pred[2,2]{1,0:T(4,128)(4,1)S(1)} %copy.15), kind=kLoop, calls=%fused_computation.14 | loop fusion | flops 262144 | bytes 1048580 | tf_op jit(solution)/shard_map/jit(_take)/select_n | solution.py:107
  26.5 0.1 maximum_bitcast_fusion.1
  26.6 1.1 %copy.19 = bf16[2,8,2,2,16,2,256]{6,5,4,3,2,1,0:T(2,128)(2,1)S(1)} copy(bf16[2,8,2,2,16,2,256]{6,4,1,2,0,3,5:T(8,128)(2,1)S(1)} %maximum_bitcast_fusion.1) | data formatting | bytes 2097152 | tf_op jit(solution)/shard_map/transpose | solution.py:113
  27.7 1.5 %reshape.178.weight_ref = bf16[2,512,512]{2,1,0:T(8,128)(2,1)} reshape(bf16[2,8,2,2,16,2,256]{6,5,4,3,2,1,0:T(2,128)(2,1)S(1)} %copy.19) | data formatting | bytes 2097152 | tf_op jit(solution)/shard_map/reshape | solution.py:113
  29.2 3.5 %shard_map.55 = f32[128,512]{1,0:T(8,128)} custom-call(bf16[2,256,512]{2,1,0:T(8,128)(2,1)} %bitcast.1.stem_ref, bf16[2,512,512]{2,1,0:T(8,128)(2,1)} %reshape.178.weight_ref, bf16[2048,512]{1,0:T(8,128)(2,1)} %bitcast.56), custom_call_target="tpu_custom_call" | custom-call | flops 536870912 | bytes 3932160 | tf_op jit(solution)/shard_map/pallas_call | solution.py:87
  32.7 1.1 %reshape.181 = f32[8,16,2,256]{3,2,1,0:T(2,128)S(1)} reshape(f32[128,512]{1,0:T(8,128)} %shard_map.55) | data formatting | bytes 524288 | tf_op jit(solution)/shard_map/reshape | solution.py:148
  33.8 0.8 %copy.29 = f32[8,16,2,256]{3,2,0,1:T(2,128)} copy(f32[8,16,2,256]{3,2,1,0:T(2,128)S(1)} %reshape.181) | data formatting | bytes 524288 | tf_op jit(solution)/shard_map/reshape | solution.py:148
  (33 shorter events, 1.1 us)
Async XLA Ops:
  0.0 10.4 %copy-start = (bf16[8,2,256,256]{3,2,1,0:T(8,128)(2,1)S(1)}, bf16[8,2,256,256]{3,2,1,0:T(8,128)(2,1)}, u32[]{:S(2)}) copy-start(bf16[8,2,256,256]{3,2,1,0:T(8,128)(2,1)} %param.6) | copy-start | bytes 6291460
  0.0 10.0 %copy-start.2 = (s32[256]{0:T(256)S(1)}, s32[256]{0:T(256)}, u32[]{:S(2)}) copy-start(s32[256]{0:T(256)} %param.9) | copy-start | bytes 3076
  0.0 12.2 %collective-permute-start = (s32[2,2]{1,0:T(2,128)}, s32[2,2]{1,0:T(2,128)S(1)}, u32[]{:S(2)}, u32[]{:S(2)}) collective-permute-start(s32[2,2]{1,0:T(2,128)} %bitcast.62), channel_id=1, source_target_pairs={{0,16},{16,0},{1,17},{17,1},{2,18},{18,2},{3,19},{19,3},{4,20},{20... | collective-permute-start | bytes 56 | tf_op jit(solution)/shard_map/ppermute | solution.py:14
  4.9 7.3 %copy-start.3 = (s32[1,2,2]{2,1,0:T(2,128)S(1)}, s32[1,2,2]{2,1,0:T(2,128)}, u32[]{:S(2)}) copy-start(s32[1,2,2]{2,1,0:T(2,128)} %param.8) | copy-start | bytes 52
  4.9 24.3 %all-to-all-start = ((bf16[32,16,512]{2,1,0:T(8,128)(2,1)}), bf16[32,16,512]{2,1,0:T(8,128)(2,1)}, u32[]{:S(2)}, u32[]{:S(2)}) async-start(bf16[32,16,512]{2,1,0:T(8,128)(2,1)} %bitcast), calls=%async_computation | async-start | bytes 1048576 | tf_op jit(solution)/shard_map/all_to_all | solution.py:171
  21.8 2.0 %copy-start.1 = (bf16[8,2,128,256]{3,2,1,0:T(8,128)(2,1)S(1)}, bf16[8,2,128,256]{3,2,1,0:T(8,128)(2,1)}, u32[]{:S(2)}) copy-start(bf16[8,2,128,256]{3,2,1,0:T(8,128)(2,1)} %fusion) | copy-start | bytes 3145732

commit v7 on v6

--- a/solution.py
+++ b/solution.py
@@ -72,18 +72,20 @@
                 odd = jnp.where(low, pltpu.roll(first, 64, 1), second)
                 lhs_ref[(2 * qp) * t_local:(2 * qp + 1) * t_local, col:col + 128] = even
                 lhs_ref[(2 * qp + 1) * t_local:(2 * qp + 2) * t_local, col:col + 128] = odd
-    out_ref[...] = jnp.dot(
-        lhs_ref[...], second_ref[...], preferred_element_type=jnp.float32
-    )
+    lhs = lhs_ref[...]
+    for part in range(second_ref.shape[0]):
+        out_ref[part] = jnp.dot(lhs, second_ref[part], preferred_element_type=jnp.float32)
 
 
 def regroup(stem_rows, first_w, second_w, q_local, t_local):
     block_count, rows, _ = stem_rows.shape
     n_mode = rows // t_local
     lhs_shape = (q_local * t_local, block_count * n_mode * 64)
-    out_shape = jax.ShapeDtypeStruct((q_local * t_local, second_w.shape[1]), jnp.float32)
+    out_shape = jax.ShapeDtypeStruct(
+        (second_w.shape[0], q_local * t_local, second_w.shape[2]), jnp.float32
+    )
     flops = 2 * block_count * rows * first_w.shape[1] * first_w.shape[2]
-    flops += 2 * lhs_shape[0] * lhs_shape[1] * second_w.shape[1]
+    flops += 2 * lhs_shape[0] * lhs_shape[1] * second_w.shape[0] * second_w.shape[2]
     return pl.pallas_call(
         regroup_kernel,
         out_shape=out_shape,
@@ -94,7 +96,7 @@
             flops=flops,
             transcendentals=0,
             bytes_accessed=2 * (stem_rows.size + first_w.size + second_w.size)
-            + 4 * lhs_shape[0] * second_w.shape[1],
+            + 4 * lhs_shape[0] * second_w.shape[0] * second_w.shape[2],
         ),
     )(stem_rows, first_w, second_w)
 
@@ -120,10 +122,11 @@
         second_w = jnp.stack(
             [jnp.stack([real_two, imag_two]), jnp.stack([-imag_two, real_two])]
         )
-        second_w = jnp.transpose(second_w, (2, 4, 3, 0, 5, 1, 6)).reshape(
-            block_count * n_mode * group, 2 * out_width
+        second_w = jnp.transpose(second_w, (1, 2, 4, 3, 0, 5, 6)).reshape(
+            2, block_count * n_mode * group, out_width
         )
         amplitude = regroup(stem_rows, first_w, second_w, q_local, t_local)
+        amplitude = jnp.transpose(amplitude, (1, 0, 2))
     else:
         second = jnp.take(w2_table, second_ids.reshape(-1), axis=0)
         second = jnp.swapaxes(second, 2, 3)

time: 35 us -> 31.6 us (0.903)
  local copies, waits for them, and re-layouts: 17.8 us -> 11.8 us
  waiting for transfers between devices: 0.01 us -> 3.5 us
  matrix products: 1.81 us -> 0.83 us
    all_to_all x1, waiting for transfers between devices: 0.01 us -> 3.5 us  [on_device(): stem_rows = lax.all_to_all(payload, ('cuts', 'mode'), 0, 0, tiled=True)]
    transpose x1 -> x0, local copies, waits for them, and re-layouts: 3.24 us -> none  [stacked_part(): jnp.transpose(second_w, (2, 4, 3, 0, 5, 1, 6))]
    unnamed x9 -> x6, local copies, waits for them, and re-layouts: 1.88 us -> 0.01 us
    dot_general x1, matrix products: 1.81 us -> 0.83 us  [on_device(): jnp.einsum('nj,spkj->spnk', picker_t, w1_table, preferred_element_type=jn...]
    another operation x1, local copies, waits for them, and re-layouts: 0.89 us -> 0.09 us  [stacked_part(): jnp.stack([real_two, imag_two])]
    another operation x1 -> x2, other arithmetic: 1.4 us -> 1.72 us  [stacked_part(): jnp.stack([jnp.stack([real_two, imag_two]), jnp.stack([-imag_two, real_tw...]
    gather x2 -> x1, local copies, waits for them, and re-layouts: 2.28 us -> 2.2 us  [stacked_part(): second = jnp.take(w2_table, second_ids.reshape(-1), axis=0)]
    reshape x2 -> x1, local copies, waits for them, and re-layouts: 1.88 us -> 1.85 us  [stacked_part(): amplitude = amplitude.reshape(q_local, t_local, 2, out_width)]
  transfers between devices with their start and end apart: 2 -> 2, of which waited for: 0 -> 1; matrix products, arithmetic and copies ran while one was open for 61% -> 45% of each run, Pallas kernels for 0% -> 0%
where the time goes in v7:
time: 31.6 us; the launch traced here: 31.3 us
  local copies, waits for them, and re-layouts  11.8 us (37%)
  starting transfers between devices  8 us (25%)
  Pallas kernels  3.54 us (11%)
  waiting for transfers between devices  3.5 us (11%)
  other arithmetic  3.44 us (11%)
  matrix products  0.83 us (3%)
    all_to_all x1, starting transfers between devices, on_device(): stem_rows = lax.all_to_all(payload, ('cuts', 'mode'), 0, 0, tiled=True)  5.06 us
    pallas_call x1, Pallas kernels, regroup(): pl.pallas_call(regroup_kernel, out_shape=out_shape, in_specs=[pl.BlockSpe...  3.54 us
    all_to_all x1, waiting for transfers between devices, on_device(): stem_rows = lax.all_to_all(payload, ('cuts', 'mode'), 0, 0, tiled=True)  3.5 us
    ppermute x1, starting transfers between devices, gather_over_cuts(): current = lax.ppermute(current, 'cuts', ring)  2.94 us
    gather x1, local copies, waits for them, and re-layouts, stacked_part(): second = jnp.take(w2_table, second_ids.reshape(-1), axis=0)  2.2 us
    broadcast_in_dim x2, local copies, waits for them, and re-layouts, on_device(): payload = jnp.broadcast_to(pieces, (n_cuts, n_mode, t_local, 2 * width))  1.97 us
    reshape x1, local copies, waits for them, and re-layouts, stacked_part(): amplitude = amplitude.reshape(q_local, t_local, 2, out_width)  1.85 us
    another operation x2, other arithmetic, stacked_part(): jnp.stack([jnp.stack([real_two, imag_two]), jnp.stack([-imag_two, real_tw...  1.72 us
  transfers between devices with their start and end apart: 2, of which 1 were waited for; matrix products, arithmetic and copies ran while one was open for 45% of the time, Pallas kernels for 0%

profile of v7, /device:TPU:0, one launch (start us, length us, event | category | flops | bytes accessed | tf_op | source)
XLA Modules:
  0.0 31.3 jit_solution(15151232487293422652)
XLA Ops:
  0.0 2.9 %collective-permute-start = (s32[2,2]{1,0:T(2,128)}, s32[2,2]{1,0:T(2,128)S(1)}, u32[]{:S(2)}, u32[]{:S(2)}) collective-permute-start(s32[2,2]{1,0:T(2,128)} %bitcast.65), channel_id=1, source_target_pairs={{0,16},{16,0},{1,17},{17,1},{2,18},{18,2},{3,19},{19,3},{4,20},{20... | collective-permute-start | bytes 56 | tf_op jit(solution)/shard_map/ppermute | solution.py:14
  2.9 1.1 %broadcast_in_dim.34 = bf16[16,16,512]{2,1,0:T(8,128)(2,1)S(1)} reshape(bf16[1,256,2,256]{3,2,1,0:T(2,128)(2,1)} %param.5) | data formatting | bytes 524288 | tf_op jit(solution)/shard_map/broadcast_in_dim | solution.py:172
  4.1 0.9 %broadcast_in_dim.35 = bf16[2,16,16,512]{3,2,1,0:T(8,128)(2,1)} broadcast(bf16[16,16,512]{2,1,0:T(8,128)(2,1)S(1)} %broadcast_in_dim.34), dimensions={1,2,3} | broadcast | bytes 786432 | tf_op jit(solution)/shard_map/broadcast_in_dim | solution.py:172
  4.9 5.1 %all-to-all-start = ((bf16[32,16,512]{2,1,0:T(8,128)(2,1)}), bf16[32,16,512]{2,1,0:T(8,128)(2,1)}, u32[]{:S(2)}, u32[]{:S(2)}) async-start(bf16[32,16,512]{2,1,0:T(8,128)(2,1)} %bitcast), calls=%async_computation | async-start | bytes 1048576 | tf_op jit(solution)/shard_map/all_to_all | solution.py:174
  10.4 0.8 %fusion = bf16[8,2,128,256]{3,2,1,0:T(8,128)(2,1)S(1)} fusion(bf16[8,2,256,256]{3,2,1,0:T(8,128)(2,1)S(1)} %copy-done, s32[128]{0:T(128)S(1)} %eq.17), kind=kOutput, calls=%fused_computation.5 | convolution fusion | flops 268992512 | bytes 3146240 | tf_op jit(solution)/shard_map/nj,spkj->spnk/dot_general | solution.py:195
  11.2 0.6 %gather_fusion = s32[2,2,2]{2,1,0:T(2,128)S(1)} fusion(s32[2,2,2]{2,1,0:T(2,128)S(1)} %pad_add_fusion, s32[1024]{0:T(1024)S(1)} %pad_clamp_fusion.2), kind=kCustom, calls=%fused_computation | custom fusion | bytes 72 | tf_op jit(solution)/shard_map/jit(_take)/gather | solution.py:19
  11.9 0.2 slice_reduce_fusion
  12.1 0.1 copy.17
  12.3 0.1 copy.15
  12.4 1.4 %gather_fusion.1 = bf16[4,2,128,256]{3,2,1,0:T(8,128)(2,1)} fusion(bf16[8,2,128,256]{3,2,1,0:T(8,128)(2,1)S(1)} %fusion, s32[1024]{0:T(1024)S(1)} %pad_clamp_fusion.1), kind=kCustom, calls=%fused_computation.1 | custom fusion | bytes 1048592 | tf_op jit(solution)/shard_map/jit(_take)/gather | solution.py:109
  13.8 1.2 %copy_select_fusion.1 = bf16[2,2,2,8,16,256]{5,4,3,1,0,2:T(8,128)(2,1)S(1)} fusion(bf16[2,2,2,8,16,256]{5,4,3,2,1,0:T(8,128)(2,1)} %bitcast.61, pred[2,2]{1,0:T(4,128)(4,1)S(1)} %copy.15), kind=kLoop, calls=%fused_computation.14 | loop fusion | flops 262144 | bytes 1048580 | tf_op jit(solution)/shard_map/jit(_take)/select_n | solution.py:109
  15.0 0.1 copy.20
  15.1 0.1 copy.21
  15.4 0.1 maximum_bitcast_fusion
  15.5 1.1 %copy.19 = bf16[2,8,2,2,16,2,256]{6,5,4,3,2,1,0:T(2,128)(2,1)S(1)} copy(bf16[2,8,2,2,16,2,256]{6,4,1,2,0,3,5:T(8,128)(2,1)S(1)} %maximum_bitcast_fusion) | data formatting | bytes 2097152 | tf_op jit(solution)/shard_map/transpose | solution.py:115
  16.6 1.5 %reshape.178.weight_ref = bf16[2,512,512]{2,1,0:T(8,128)(2,1)} reshape(bf16[2,8,2,2,16,2,256]{6,5,4,3,2,1,0:T(2,128)(2,1)S(1)} %copy.19) | data formatting | bytes 2097152 | tf_op jit(solution)/shard_map/reshape | solution.py:115
  18.1 2.2 %gather_fusion.2 = bf16[4,2,256,256]{3,2,1,0:T(8,128)(2,1)S(1)} fusion(bf16[8,2,256,256]{3,2,1,0:T(8,128)(2,1)} %param.7, s32[1024]{0:T(1024)S(1)} %pad_clamp_fusion), kind=kCustom, calls=%fused_computation.2 | custom fusion | bytes 2097168 | tf_op jit(solution)/shard_map/jit(_take)/gather | solution.py:119
  20.3 0.2 copy_select_fusion
  20.5 0.1 slice_bitcast_fusion
  20.6 0.2 maximum_bitcast_fusion.1
  20.8 1.5 %pad_maximum_fusion = bf16[2,2,2,2,16,16,256]{6,5,0,3,4,2,1:T(8,128)(2,1)} fusion(bf16[1,2,2,2,16,16,256]{6,5,0,3,4,2,1:T(8,128)(2,1)S(1)} %get-tuple-element.10, bf16[1,2,2,2,16,16,256]{6,5,0,3,4,2,1:T(8,128)(2,1)S(1)} %get-tuple-element.9), kind=kLoop, calls=%fused_computation.3 | loop fusion | flops 1048576 | bytes 4194304 | tf_op jit(solution)/shard_map/stack | solution.py:122
  22.4 3.5 %all-to-all-done = bf16[32,16,512]{2,1,0:T(8,128)(2,1)} async-done(((bf16[32,16,512]{2,1,0:T(8,128)(2,1)}), bf16[32,16,512]{2,1,0:T(8,128)(2,1)}, u32[]{:S(2)}, u32[]{:S(2)}) %all-to-all-start) | async-done | bytes 524320 | tf_op jit(solution)/shard_map/all_to_all | solution.py:174
  25.9 3.5 %shard_map.55 = f32[2,128,256]{2,1,0:T(8,128)} custom-call(bf16[2,256,512]{2,1,0:T(8,128)(2,1)} %bitcast.1.stem_ref, bf16[2,512,512]{2,1,0:T(8,128)(2,1)} %reshape.178.weight_ref, bf16[2,2048,256]{2,1,0:T(8,128)(2,1)} %bitcast.59), custom_call_target="tpu_custom_call" | custom-call | flops 536870912 | bytes 3932160 | tf_op jit(solution)/shard_map/pallas_call | solution.py:89
  29.4 1.9 %copy.29 = f32[8,16,2,256]{3,2,0,1:T(2,128)} copy(f32[8,16,2,256]{3,1,0,2:T(8,128)} %bitcast.62) | data formatting | bytes 524288 | tf_op jit(solution)/shard_map/reshape | solution.py:151
  (27 shorter events, 0.8 us)
Async XLA Ops:
  0.0 10.4 %copy-start = (bf16[8,2,256,256]{3,2,1,0:T(8,128)(2,1)S(1)}, bf16[8,2,256,256]{3,2,1,0:T(8,128)(2,1)}, u32[]{:S(2)}) copy-start(bf16[8,2,256,256]{3,2,1,0:T(8,128)(2,1)} %param.6) | copy-start | bytes 6291460
  0.0 10.0 %copy-start.1 = (s32[256]{0:T(256)S(1)}, s32[256]{0:T(256)}, u32[]{:S(2)}) copy-start(s32[256]{0:T(256)} %param.9) | copy-start | bytes 3076
  0.0 11.2 %collective-permute-start = (s32[2,2]{1,0:T(2,128)}, s32[2,2]{1,0:T(2,128)S(1)}, u32[]{:S(2)}, u32[]{:S(2)}) collective-permute-start(s32[2,2]{1,0:T(2,128)} %bitcast.65), channel_id=1, source_target_pairs={{0,16},{16,0},{1,17},{17,1},{2,18},{18,2},{3,19},{19,3},{4,20},{20... | collective-permute-start | bytes 56 | tf_op jit(solution)/shard_map/ppermute | solution.py:14
  4.9 6.3 %copy-start.2 = (s32[1,2,2]{2,1,0:T(2,128)S(1)}, s32[1,2,2]{2,1,0:T(2,128)}, u32[]{:S(2)}) copy-start(s32[1,2,2]{2,1,0:T(2,128)} %param.8) | copy-start | bytes 52
  4.9 20.9 %all-to-all-start = ((bf16[32,16,512]{2,1,0:T(8,128)(2,1)}), bf16[32,16,512]{2,1,0:T(8,128)(2,1)}, u32[]{:S(2)}, u32[]{:S(2)}) async-start(bf16[32,16,512]{2,1,0:T(8,128)(2,1)} %bitcast), calls=%async_computation | async-start | bytes 1048576 | tf_op jit(solution)/shard_map/all_to_all | solution.py:174

commit v8 on v7

--- a/solution.py
+++ b/solution.py
@@ -74,7 +74,9 @@
                 lhs_ref[(2 * qp + 1) * t_local:(2 * qp + 2) * t_local, col:col + 128] = odd
     lhs = lhs_ref[...]
     for part in range(second_ref.shape[0]):
-        out_ref[part] = jnp.dot(lhs, second_ref[part], preferred_element_type=jnp.float32)
+        result = jnp.dot(lhs, second_ref[part], preferred_element_type=jnp.float32)
+        for q in range(q_local):
+            out_ref[:, q, part, :] = result[q * t_local:(q + 1) * t_local]
 
 
 def regroup(stem_rows, first_w, second_w, q_local, t_local):
@@ -82,7 +84,7 @@
     n_mode = rows // t_local
     lhs_shape = (q_local * t_local, block_count * n_mode * 64)
     out_shape = jax.ShapeDtypeStruct(
-        (second_w.shape[0], q_local * t_local, second_w.shape[2]), jnp.float32
+        (t_local, q_local, second_w.shape[0], second_w.shape[2]), jnp.float32
     )
     flops = 2 * block_count * rows * first_w.shape[1] * first_w.shape[2]
     flops += 2 * lhs_shape[0] * lhs_shape[1] * second_w.shape[0] * second_w.shape[2]
@@ -125,8 +127,7 @@
         second_w = jnp.transpose(second_w, (1, 2, 4, 3, 0, 5, 6)).reshape(
             2, block_count * n_mode * group, out_width
         )
-        amplitude = regroup(stem_rows, first_w, second_w, q_local, t_local)
-        amplitude = jnp.transpose(amplitude, (1, 0, 2))
+        return regroup(stem_rows, first_w, second_w, q_local, t_local)
     else:
         second = jnp.take(w2_table, second_ids.reshape(-1), axis=0)
         second = jnp.swapaxes(second, 2, 3)

time: 31.6 us -> 29.8 us (0.943)
  local copies, waits for them, and re-layouts: 11.8 us -> 9.94 us
    reshape x1 -> x0, local copies, waits for them, and re-layouts: 1.85 us -> none  [stacked_part(): amplitude = amplitude.reshape(q_local, t_local, 2, out_width)]
  transfers between devices with their start and end apart: 2 -> 2, of which waited for: 1 -> 1; matrix products, arithmetic and copies ran while one was open for 45% -> 48% of each run, Pallas kernels for 0% -> 0%
where the time goes in v8:
time: 29.8 us; the launch traced here: 29.5 us
  local copies, waits for them, and re-layouts  9.94 us (33%)
  starting transfers between devices  8 us (27%)
  Pallas kernels  3.59 us (12%)
  waiting for transfers between devices  3.5 us (12%)
  other arithmetic  3.44 us (12%)
  matrix products  0.83 us (3%)
    all_to_all x1, starting transfers between devices, on_device(): stem_rows = lax.all_to_all(payload, ('cuts', 'mode'), 0, 0, tiled=True)  5.06 us
    pallas_call x1, Pallas kernels, regroup(): pl.pallas_call(regroup_kernel, out_shape=out_shape, in_specs=[pl.BlockSpe...  3.59 us
    all_to_all x1, waiting for transfers between devices, on_device(): stem_rows = lax.all_to_all(payload, ('cuts', 'mode'), 0, 0, tiled=True)  3.5 us
    ppermute x1, starting transfers between devices, gather_over_cuts(): current = lax.ppermute(current, 'cuts', ring)  2.94 us
    gather x1, local copies, waits for them, and re-layouts, stacked_part(): second = jnp.take(w2_table, second_ids.reshape(-1), axis=0)  2.2 us
    broadcast_in_dim x2, local copies, waits for them, and re-layouts, on_device(): payload = jnp.broadcast_to(pieces, (n_cuts, n_mode, t_local, 2 * width))  1.97 us
    another operation x2, other arithmetic, stacked_part(): jnp.stack([jnp.stack([real_two, imag_two]), jnp.stack([-imag_two, real_tw...  1.72 us
    reshape x1, local copies, waits for them, and re-layouts, stacked_part(): jnp.transpose(first_w, (2, 4, 3, 1, 5, 0, 6))  1.51 us
  transfers between devices with their start and end apart: 2, of which 1 were waited for; matrix products, arithmetic and copies ran while one was open for 48% of the time, Pallas kernels for 0%

profile of v8, /device:TPU:0, one launch (start us, length us, event | category | flops | bytes accessed | tf_op | source)
XLA Modules:
  0.0 29.5 jit_solution(977509963275948328)
XLA Ops:
  0.0 2.9 %collective-permute-start = (s32[2,2]{1,0:T(2,128)}, s32[2,2]{1,0:T(2,128)S(1)}, u32[]{:S(2)}, u32[]{:S(2)}) collective-permute-start(s32[2,2]{1,0:T(2,128)} %bitcast.58), channel_id=1, source_target_pairs={{0,16},{16,0},{1,17},{17,1},{2,18},{18,2},{3,19},{19,3},{4,20},{20... | collective-permute-start | bytes 56 | tf_op jit(solution)/shard_map/ppermute | solution.py:14
  2.9 1.1 %broadcast_in_dim.34 = bf16[16,16,512]{2,1,0:T(8,128)(2,1)S(1)} reshape(bf16[1,256,2,256]{3,2,1,0:T(2,128)(2,1)} %param.5) | data formatting | bytes 524288 | tf_op jit(solution)/shard_map/broadcast_in_dim | solution.py:173
  4.1 0.9 %broadcast_in_dim.35 = bf16[2,16,16,512]{3,2,1,0:T(8,128)(2,1)} broadcast(bf16[16,16,512]{2,1,0:T(8,128)(2,1)S(1)} %broadcast_in_dim.34), dimensions={1,2,3} | broadcast | bytes 786432 | tf_op jit(solution)/shard_map/broadcast_in_dim | solution.py:173
  4.9 5.1 %all-to-all-start = ((bf16[32,16,512]{2,1,0:T(8,128)(2,1)}), bf16[32,16,512]{2,1,0:T(8,128)(2,1)}, u32[]{:S(2)}, u32[]{:S(2)}) async-start(bf16[32,16,512]{2,1,0:T(8,128)(2,1)} %bitcast), calls=%async_computation | async-start | bytes 1048576 | tf_op jit(solution)/shard_map/all_to_all | solution.py:175
  10.4 0.8 %fusion = bf16[8,2,128,256]{3,2,1,0:T(8,128)(2,1)S(1)} fusion(bf16[8,2,256,256]{3,2,1,0:T(8,128)(2,1)S(1)} %copy-done, s32[128]{0:T(128)S(1)} %eq.17), kind=kOutput, calls=%fused_computation.5 | convolution fusion | flops 268992512 | bytes 3146240 | tf_op jit(solution)/shard_map/nj,spkj->spnk/dot_general | solution.py:196
  11.2 0.6 %gather_fusion = s32[2,2,2]{2,1,0:T(2,128)S(1)} fusion(s32[2,2,2]{2,1,0:T(2,128)S(1)} %pad_add_fusion, s32[1024]{0:T(1024)S(1)} %pad_clamp_fusion.2), kind=kCustom, calls=%fused_computation | custom fusion | bytes 72 | tf_op jit(solution)/shard_map/jit(_take)/gather | solution.py:19
  11.9 0.2 slice_reduce_fusion
  12.1 0.1 copy.16
  12.3 0.1 copy.14
  12.4 1.4 %gather_fusion.1 = bf16[4,2,128,256]{3,2,1,0:T(8,128)(2,1)} fusion(bf16[8,2,128,256]{3,2,1,0:T(8,128)(2,1)S(1)} %fusion, s32[1024]{0:T(1024)S(1)} %pad_clamp_fusion.1), kind=kCustom, calls=%fused_computation.1 | custom fusion | bytes 1048592 | tf_op jit(solution)/shard_map/jit(_take)/gather | solution.py:111
  13.8 1.2 %copy_select_fusion.1 = bf16[2,2,2,8,16,256]{5,4,3,1,0,2:T(8,128)(2,1)S(1)} fusion(bf16[2,2,2,8,16,256]{5,4,3,2,1,0:T(8,128)(2,1)} %bitcast.55, pred[2,2]{1,0:T(4,128)(4,1)S(1)} %copy.14), kind=kLoop, calls=%fused_computation.14 | loop fusion | flops 262144 | bytes 1048580 | tf_op jit(solution)/shard_map/jit(_take)/select_n | solution.py:111
  15.0 0.1 copy.19
  15.1 0.1 copy.20
  15.3 0.1 maximum_bitcast_fusion.3
  15.4 0.1 maximum_bitcast_fusion
  15.5 1.1 %copy.18 = bf16[2,8,2,2,16,2,256]{6,5,4,3,2,1,0:T(2,128)(2,1)S(1)} copy(bf16[2,8,2,2,16,2,256]{6,4,1,2,0,3,5:T(8,128)(2,1)S(1)} %maximum_bitcast_fusion) | data formatting | bytes 2097152 | tf_op jit(solution)/shard_map/transpose | solution.py:117
  16.6 1.5 %reshape.175.weight_ref = bf16[2,512,512]{2,1,0:T(8,128)(2,1)} reshape(bf16[2,8,2,2,16,2,256]{6,5,4,3,2,1,0:T(2,128)(2,1)S(1)} %copy.18) | data formatting | bytes 2097152 | tf_op jit(solution)/shard_map/reshape | solution.py:117
  18.1 2.2 %gather_fusion.2 = bf16[4,2,256,256]{3,2,1,0:T(8,128)(2,1)S(1)} fusion(bf16[8,2,256,256]{3,2,1,0:T(8,128)(2,1)} %param.7, s32[1024]{0:T(1024)S(1)} %pad_clamp_fusion), kind=kCustom, calls=%fused_computation.2 | custom fusion | bytes 2097168 | tf_op jit(solution)/shard_map/jit(_take)/gather | solution.py:121
  20.3 0.2 copy_select_fusion
  20.5 0.1 slice_bitcast_fusion
  20.6 0.2 maximum_bitcast_fusion.1
  20.8 1.5 %pad_maximum_fusion = bf16[2,2,2,2,16,16,256]{6,5,0,3,4,2,1:T(8,128)(2,1)} fusion(bf16[1,2,2,2,16,16,256]{6,5,0,3,4,2,1:T(8,128)(2,1)S(1)} %get-tuple-element.10, bf16[1,2,2,2,16,16,256]{6,5,0,3,4,2,1:T(8,128)(2,1)S(1)} %get-tuple-element.9), kind=kLoop, calls=%fused_computation.3 | loop fusion | flops 1048576 | bytes 4194304 | tf_op jit(solution)/shard_map/stack | solution.py:124
  22.4 3.5 %all-to-all-done = bf16[32,16,512]{2,1,0:T(8,128)(2,1)} async-done(((bf16[32,16,512]{2,1,0:T(8,128)(2,1)}), bf16[32,16,512]{2,1,0:T(8,128)(2,1)}, u32[]{:S(2)}, u32[]{:S(2)}) %all-to-all-start) | async-done | bytes 524320 | tf_op jit(solution)/shard_map/all_to_all | solution.py:175
  25.9 3.6 %shard_map.55 = f32[16,8,2,256]{3,2,1,0:T(2,128)} custom-call(bf16[2,256,512]{2,1,0:T(8,128)(2,1)} %bitcast.1.stem_ref, bf16[2,512,512]{2,1,0:T(8,128)(2,1)} %reshape.175.weight_ref, bf16[2,2048,256]{2,1,0:T(8,128)(2,1)} %bitcast.53), custom_call_target="tpu_custom_call" | custom-call | flops 536870912 | bytes 3932160 | tf_op jit(solution)/shard_map/pallas_call | solution.py:91
  (26 shorter events, 0.7 us)
Async XLA Ops:
  0.0 10.4 %copy-start = (bf16[8,2,256,256]{3,2,1,0:T(8,128)(2,1)S(1)}, bf16[8,2,256,256]{3,2,1,0:T(8,128)(2,1)}, u32[]{:S(2)}) copy-start(bf16[8,2,256,256]{3,2,1,0:T(8,128)(2,1)} %param.6) | copy-start | bytes 6291460
  0.0 10.0 %copy-start.1 = (s32[256]{0:T(256)S(1)}, s32[256]{0:T(256)}, u32[]{:S(2)}) copy-start(s32[256]{0:T(256)} %param.9) | copy-start | bytes 3076
  0.0 11.2 %collective-permute-start = (s32[2,2]{1,0:T(2,128)}, s32[2,2]{1,0:T(2,128)S(1)}, u32[]{:S(2)}, u32[]{:S(2)}) collective-permute-start(s32[2,2]{1,0:T(2,128)} %bitcast.58), channel_id=1, source_target_pairs={{0,16},{16,0},{1,17},{17,1},{2,18},{18,2},{3,19},{19,3},{4,20},{20... | collective-permute-start | bytes 56 | tf_op jit(solution)/shard_map/ppermute | solution.py:14
  4.9 6.3 %copy-start.2 = (s32[1,2,2]{2,1,0:T(2,128)S(1)}, s32[1,2,2]{2,1,0:T(2,128)}, u32[]{:S(2)}) copy-start(s32[1,2,2]{2,1,0:T(2,128)} %param.8) | copy-start | bytes 52
  4.9 20.9 %all-to-all-start = ((bf16[32,16,512]{2,1,0:T(8,128)(2,1)}), bf16[32,16,512]{2,1,0:T(8,128)(2,1)}, u32[]{:S(2)}, u32[]{:S(2)}) async-start(bf16[32,16,512]{2,1,0:T(8,128)(2,1)} %bitcast), calls=%async_computation | async-start | bytes 1048576 | tf_op jit(solution)/shard_map/all_to_all | solution.py:175

commit v9 on v8

--- a/solution.py
+++ b/solution.py
@@ -175,7 +175,8 @@
     stem_rows = lax.all_to_all(payload, ("cuts", "mode"), 0, 0, tiled=True)
     stem_rows = stem_rows.reshape(block_count, n_mode * t_local, 2 * width)
 
-    all_ids = gather_over_cuts(slice_ids[0], n_cuts)
+    tie = (payload[0, 0, 0] * 0).astype(slice_ids.dtype)
+    all_ids = gather_over_cuts(slice_ids[0] + tie, n_cuts)
     first_ids = all_ids[:, :, 0].T
     second_ids = all_ids[:, :, 1].T
 

time: 29.8 us -> 30.2 us (1.013)
  waiting for transfers between devices: 3.5 us -> 0.69 us
  local copies, waits for them, and re-layouts: 9.94 us -> 11.3 us
  starting transfers between devices: 8 us -> 9.21 us
  between operations: 0.17 us -> 0.82 us
    all_to_all x1, waiting for transfers between devices: 3.5 us -> 0.01 us  [on_device(): stem_rows = lax.all_to_all(payload, ('cuts', 'mode'), 0, 0, tiled=True)]
    all_to_all x1, starting transfers between devices: 5.06 us -> 7.43 us  [on_device(): stem_rows = lax.all_to_all(payload, ('cuts', 'mode'), 0, 0, tiled=True)]
    slice x0 -> x1, local copies, waits for them, and re-layouts: none -> 1.19 us  [on_device(): tie = (payload[0, 0, 0] * 0).astype(slice_ids.dtype)]
    ppermute x1, starting transfers between devices: 2.94 us -> 1.78 us  [gather_over_cuts(): current = lax.ppermute(current, 'cuts', ring)]
    ppermute x1, waiting for transfers between devices: 0.01 us -> 0.69 us  [gather_over_cuts(): current = lax.ppermute(current, 'cuts', ring)]
  transfers between devices with their start and end apart: 2 -> 2, of which waited for: 1 -> 1; matrix products, arithmetic and copies ran while one was open for 48% -> 45% of each run, Pallas kernels for 0% -> 0%
where the time goes in v9:
time: 30.2 us; the launch traced here: 29.9 us
  local copies, waits for them, and re-layouts  11.3 us (37%)
  starting transfers between devices  9.21 us (30%)
  Pallas kernels  3.59 us (12%)
  other arithmetic  3.45 us (11%)
  matrix products  0.83 us (3%)
  between operations  0.82 us (3%)
  waiting for transfers between devices  0.69 us (2%)
    all_to_all x1, starting transfers between devices, on_device(): stem_rows = lax.all_to_all(payload, ('cuts', 'mode'), 0, 0, tiled=True)  7.43 us
    pallas_call x1, Pallas kernels, regroup(): pl.pallas_call(regroup_kernel, out_shape=out_shape, in_specs=[pl.BlockSpe...  3.59 us
    gather x1, local copies, waits for them, and re-layouts, stacked_part(): second = jnp.take(w2_table, second_ids.reshape(-1), axis=0)  2.2 us
    broadcast_in_dim x2, local copies, waits for them, and re-layouts, on_device(): payload = jnp.broadcast_to(pieces, (n_cuts, n_mode, t_local, 2 * width))  2.12 us
    ppermute x1, starting transfers between devices, gather_over_cuts(): current = lax.ppermute(current, 'cuts', ring)  1.78 us
    another operation x2, other arithmetic, stacked_part(): jnp.stack([jnp.stack([real_two, imag_two]), jnp.stack([-imag_two, real_tw...  1.72 us
    reshape x1, local copies, waits for them, and re-layouts, stacked_part(): jnp.transpose(first_w, (2, 4, 3, 1, 5, 0, 6))  1.51 us
    gather x1, local copies, waits for them, and re-layouts, stacked_part(): picked = jnp.take(first_t, first_ids.reshape(-1), axis=0)  1.37 us
  transfers between devices with their start and end apart: 2, of which 1 were waited for; matrix products, arithmetic and copies ran while one was open for 45% of the time, Pallas kernels for 0%

profile of v9, /device:TPU:0, one launch (start us, length us, event | category | flops | bytes accessed | tf_op | source)
XLA Modules:
  0.0 29.9 jit_solution(1090638590877785295)
XLA Ops:
  0.0 1.3 %broadcast_in_dim.34 = bf16[16,16,512]{2,1,0:T(8,128)(2,1)S(1)} reshape(bf16[1,256,2,256]{3,2,1,0:T(2,128)(2,1)} %param.5) | data formatting | bytes 524288 | tf_op jit(solution)/shard_map/broadcast_in_dim | solution.py:173
  1.3 0.9 %broadcast_in_dim.35 = bf16[2,16,16,512]{3,2,1,0:T(8,128)(2,1)} broadcast(bf16[16,16,512]{2,1,0:T(8,128)(2,1)S(1)} %broadcast_in_dim.34), dimensions={1,2,3} | broadcast | bytes 786432 | tf_op jit(solution)/shard_map/broadcast_in_dim | solution.py:173
  2.1 7.4 %all-to-all-start = ((bf16[32,16,512]{2,1,0:T(8,128)(2,1)}), bf16[32,16,512]{2,1,0:T(8,128)(2,1)}, u32[]{:S(2)}, u32[]{:S(2)}) async-start(bf16[32,16,512]{2,1,0:T(8,128)(2,1)} %bitcast), calls=%async_computation | async-start | bytes 1048576 | tf_op jit(solution)/shard_map/all_to_all | solution.py:175
  9.6 1.2 %slice.34 = bf16[1,1,1]{2,1,0:T(2,128)(2,1)} slice(bf16[32,16,512]{2,1,0:T(8,128)(2,1)} %bitcast), slice={[0:1], [0:1], [0:1]} | slice | bytes 4 | tf_op jit(solution)/shard_map/slice | solution.py:178
  11.4 1.8 %collective-permute-start = (s32[2,2]{1,0:T(2,128)S(1)}, s32[2,2]{1,0:T(2,128)S(1)}, u32[]{:S(2)}, u32[]{:S(2)}) collective-permute-start(s32[2,2]{1,0:T(2,128)S(1)} %fusion.12), channel_id=1, source_target_pairs={{0,16},{16,0},{1,17},{17,1},{2,18},{18,2},{3,19},{19,3},{4,20},{20... | collective-permute-start | bytes 56 | tf_op jit(solution)/shard_map/ppermute | solution.py:14
  13.6 0.8 %fusion = bf16[8,2,128,256]{3,2,1,0:T(8,128)(2,1)S(1)} fusion(bf16[8,2,256,256]{3,2,1,0:T(8,128)(2,1)S(1)} %copy-done, s32[128]{0:T(128)S(1)} %eq.17), kind=kOutput, calls=%fused_computation.5 | convolution fusion | flops 268992512 | bytes 3146240 | tf_op jit(solution)/shard_map/nj,spkj->spnk/dot_general | solution.py:197
  14.4 0.7 %collective-permute-done = s32[2,2]{1,0:T(2,128)S(1)} collective-permute-done((s32[2,2]{1,0:T(2,128)S(1)}, s32[2,2]{1,0:T(2,128)S(1)}, u32[]{:S(2)}, u32[]{:S(2)}) %collective-permute-start) | collective-permute-done | bytes 48 | tf_op jit(solution)/shard_map/ppermute | solution.py:14
  15.1 0.6 %gather_fusion = s32[2,2,2]{2,1,0:T(2,128)S(1)} fusion(s32[2,2,2]{2,1,0:T(2,128)S(1)} %pad_add_fusion, s32[1024]{0:T(1024)S(1)} %pad_clamp_fusion.2), kind=kCustom, calls=%fused_computation | custom fusion | bytes 72 | tf_op jit(solution)/shard_map/jit(_take)/gather | solution.py:19
  15.8 0.2 slice_reduce_fusion
  16.0 0.1 copy.16
  16.2 0.1 copy.14
  16.3 1.4 %gather_fusion.1 = bf16[4,2,128,256]{3,2,1,0:T(8,128)(2,1)} fusion(bf16[8,2,128,256]{3,2,1,0:T(8,128)(2,1)S(1)} %fusion, s32[1024]{0:T(1024)S(1)} %pad_clamp_fusion.1), kind=kCustom, calls=%fused_computation.1 | custom fusion | bytes 1048592 | tf_op jit(solution)/shard_map/jit(_take)/gather | solution.py:111
  17.7 1.2 %copy_select_fusion.1 = bf16[2,2,2,8,16,256]{5,4,3,1,0,2:T(8,128)(2,1)S(1)} fusion(bf16[2,2,2,8,16,256]{5,4,3,2,1,0:T(8,128)(2,1)} %bitcast.58, pred[2,2]{1,0:T(4,128)(4,1)S(1)} %copy.14), kind=kLoop, calls=%fused_computation.14 | loop fusion | flops 262144 | bytes 1048580 | tf_op jit(solution)/shard_map/jit(_take)/select_n | solution.py:111
  18.9 0.1 copy.19
  19.0 0.1 copy.20
  19.3 0.1 maximum_bitcast_fusion
  19.4 1.1 %copy.18 = bf16[2,8,2,2,16,2,256]{6,5,4,3,2,1,0:T(2,128)(2,1)S(1)} copy(bf16[2,8,2,2,16,2,256]{6,4,1,2,0,3,5:T(8,128)(2,1)S(1)} %maximum_bitcast_fusion) | data formatting | bytes 2097152 | tf_op jit(solution)/shard_map/transpose | solution.py:117
  20.5 1.5 %reshape.181.weight_ref = bf16[2,512,512]{2,1,0:T(8,128)(2,1)} reshape(bf16[2,8,2,2,16,2,256]{6,5,4,3,2,1,0:T(2,128)(2,1)S(1)} %copy.18) | data formatting | bytes 2097152 | tf_op jit(solution)/shard_map/reshape | solution.py:117
  22.0 2.2 %gather_fusion.2 = bf16[4,2,256,256]{3,2,1,0:T(8,128)(2,1)S(1)} fusion(bf16[8,2,256,256]{3,2,1,0:T(8,128)(2,1)} %param.7, s32[1024]{0:T(1024)S(1)} %pad_clamp_fusion), kind=kCustom, calls=%fused_computation.2 | custom fusion | bytes 2097168 | tf_op jit(solution)/shard_map/jit(_take)/gather | solution.py:121
  24.2 0.2 copy_select_fusion
  24.4 0.1 slice_bitcast_fusion
  24.5 0.2 maximum_bitcast_fusion.1
  24.7 1.5 %pad_maximum_fusion = bf16[2,2,2,2,16,16,256]{6,5,0,3,4,2,1:T(8,128)(2,1)} fusion(bf16[1,2,2,2,16,16,256]{6,5,0,3,4,2,1:T(8,128)(2,1)S(1)} %get-tuple-element.10, bf16[1,2,2,2,16,16,256]{6,5,0,3,4,2,1:T(8,128)(2,1)S(1)} %get-tuple-element.9), kind=kLoop, calls=%fused_computation.3 | loop fusion | flops 1048576 | bytes 4194304 | tf_op jit(solution)/shard_map/stack | solution.py:124
  26.3 3.6 %shard_map.55 = f32[16,8,2,256]{3,2,1,0:T(2,128)} custom-call(bf16[2,256,512]{2,1,0:T(8,128)(2,1)} %bitcast.1.stem_ref, bf16[2,512,512]{2,1,0:T(8,128)(2,1)} %reshape.181.weight_ref, bf16[2,2048,256]{2,1,0:T(8,128)(2,1)} %bitcast.56), custom_call_target="tpu_custom_call" | custom-call | flops 536870912 | bytes 3932160 | tf_op jit(solution)/shard_map/pallas_call | solution.py:91
  (29 shorter events, 0.8 us)
Async XLA Ops:
  0.0 13.6 %copy-start = (bf16[8,2,256,256]{3,2,1,0:T(8,128)(2,1)S(1)}, bf16[8,2,256,256]{3,2,1,0:T(8,128)(2,1)}, u32[]{:S(2)}) copy-start(bf16[8,2,256,256]{3,2,1,0:T(8,128)(2,1)} %param.6) | copy-start | bytes 6291460
  0.0 11.4 %copy-start.1 = (s32[1,2,2]{2,1,0:T(2,128)S(1)}, s32[1,2,2]{2,1,0:T(2,128)}, u32[]{:S(2)}) copy-start(s32[1,2,2]{2,1,0:T(2,128)} %param.8) | copy-start | bytes 52
  0.0 13.3 %copy-start.2 = (s32[256]{0:T(256)S(1)}, s32[256]{0:T(256)}, u32[]{:S(2)}) copy-start(s32[256]{0:T(256)} %param.9) | copy-start | bytes 3076
  2.1 24.1 %all-to-all-start = ((bf16[32,16,512]{2,1,0:T(8,128)(2,1)}), bf16[32,16,512]{2,1,0:T(8,128)(2,1)}, u32[]{:S(2)}, u32[]{:S(2)}) async-start(bf16[32,16,512]{2,1,0:T(8,128)(2,1)} %bitcast), calls=%async_computation | async-start | bytes 1048576 | tf_op jit(solution)/shard_map/all_to_all | solution.py:175
  11.4 3.7 %collective-permute-start = (s32[2,2]{1,0:T(2,128)S(1)}, s32[2,2]{1,0:T(2,128)S(1)}, u32[]{:S(2)}, u32[]{:S(2)}) collective-permute-start(s32[2,2]{1,0:T(2,128)S(1)} %fusion.12), channel_id=1, source_target_pairs={{0,16},{16,0},{1,17},{17,1},{2,18},{18,2},{3,19},{19,3},{4,20},{20... | collective-permute-start | bytes 56 | tf_op jit(solution)/shard_map/ppermute | solution.py:14

commit v10 on v8

--- a/solution.py
+++ b/solution.py
@@ -49,11 +49,13 @@
     return jnp.dot(lhs, second_w, preferred_element_type=jnp.float32)
 
 
-def regroup_kernel(stem_ref, weight_ref, second_ref, out_ref, lhs_ref):
+def regroup_kernel(stem_ref, weight_ref, second_hbm, out_ref, lhs_ref, second_ref, second_sem):
     block_count, rows, _ = stem_ref.shape
     q_local = weight_ref.shape[1] // 64
     t_local = 16
     n_mode = rows // t_local
+    second_copy = pltpu.make_async_copy(second_hbm, second_ref, second_sem)
+    second_copy.start()
     lane = lax.broadcasted_iota(jnp.int32, (t_local, 128), 1)
     low = lane < 64
     for b in range(block_count):
@@ -72,6 +74,7 @@
                 odd = jnp.where(low, pltpu.roll(first, 64, 1), second)
                 lhs_ref[(2 * qp) * t_local:(2 * qp + 1) * t_local, col:col + 128] = even
                 lhs_ref[(2 * qp + 1) * t_local:(2 * qp + 2) * t_local, col:col + 128] = odd
+    second_copy.wait()
     lhs = lhs_ref[...]
     for part in range(second_ref.shape[0]):
         result = jnp.dot(lhs, second_ref[part], preferred_element_type=jnp.float32)
@@ -91,9 +94,13 @@
     return pl.pallas_call(
         regroup_kernel,
         out_shape=out_shape,
-        in_specs=[pl.BlockSpec(memory_space=pltpu.VMEM)] * 3,
+        in_specs=[pl.BlockSpec(memory_space=pltpu.VMEM)] * 2 + [pl.BlockSpec(memory_space=pl.ANY)],
         out_specs=pl.BlockSpec(memory_space=pltpu.VMEM),
-        scratch_shapes=[pltpu.VMEM(lhs_shape, jnp.bfloat16)],
+        scratch_shapes=[
+            pltpu.VMEM(lhs_shape, jnp.bfloat16),
+            pltpu.VMEM(second_w.shape, second_w.dtype),
+            pltpu.SemaphoreType.DMA(()),
+        ],
         cost_estimate=pl.CostEstimate(
             flops=flops,
             transcendentals=0,

time: 29.8 us -> 30.4 us (1.020)
  Pallas kernels: 3.59 us -> 4.19 us
    pallas_call x1, Pallas kernels: 3.59 us -> 4.19 us  [regroup(): pl.pallas_call(regroup_kernel, out_shape=out_shape, in_specs=[pl.BlockSpe...]
  transfers between devices with their start and end apart: 2 -> 2, of which waited for: 1 -> 1; matrix products, arithmetic and copies ran while one was open for 48% -> 47% of each run, Pallas kernels for 0% -> 0%
where the time goes in v10:
time: 30.4 us; the launch traced here: 30.1 us
  local copies, waits for them, and re-layouts  9.94 us (33%)
  starting transfers between devices  8 us (26%)
  Pallas kernels  4.19 us (14%)
  waiting for transfers between devices  3.5 us (12%)
  other arithmetic  3.44 us (11%)
  matrix products  0.83 us (3%)
    all_to_all x1, starting transfers between devices, on_device(): stem_rows = lax.all_to_all(payload, ('cuts', 'mode'), 0, 0, tiled=True)  5.06 us
    pallas_call x1, Pallas kernels, regroup(): pl.pallas_call(regroup_kernel, out_shape=out_shape, in_specs=[pl.BlockSpe...  4.19 us
    all_to_all x1, waiting for transfers between devices, on_device(): stem_rows = lax.all_to_all(payload, ('cuts', 'mode'), 0, 0, tiled=True)  3.5 us
    ppermute x1, starting transfers between devices, gather_over_cuts(): current = lax.ppermute(current, 'cuts', ring)  2.94 us
    gather x1, local copies, waits for them, and re-layouts, stacked_part(): second = jnp.take(w2_table, second_ids.reshape(-1), axis=0)  2.2 us
    broadcast_in_dim x2, local copies, waits for them, and re-layouts, on_device(): payload = jnp.broadcast_to(pieces, (n_cuts, n_mode, t_local, 2 * width))  1.97 us
    another operation x2, other arithmetic, stacked_part(): jnp.stack([jnp.stack([real_two, imag_two]), jnp.stack([-imag_two, real_tw...  1.72 us
    reshape x1, local copies, waits for them, and re-layouts, stacked_part(): jnp.transpose(first_w, (2, 4, 3, 1, 5, 0, 6))  1.51 us
  transfers between devices with their start and end apart: 2, of which 1 were waited for; matrix products, arithmetic and copies ran while one was open for 47% of the time, Pallas kernels for 0%

profile of v10, /device:TPU:0, one launch (start us, length us, event | category | flops | bytes accessed | tf_op | source)
XLA Modules:
  0.0 30.1 jit_solution(8356501217450794095)
XLA Ops:
  0.0 2.9 %collective-permute-start = (s32[2,2]{1,0:T(2,128)}, s32[2,2]{1,0:T(2,128)S(1)}, u32[]{:S(2)}, u32[]{:S(2)}) collective-permute-start(s32[2,2]{1,0:T(2,128)} %bitcast.58), channel_id=1, source_target_pairs={{0,16},{16,0},{1,17},{17,1},{2,18},{18,2},{3,19},{19,3},{4,20},{20... | collective-permute-start | bytes 56 | tf_op jit(solution)/shard_map/ppermute | solution.py:14
  2.9 1.1 %broadcast_in_dim.34 = bf16[16,16,512]{2,1,0:T(8,128)(2,1)S(1)} reshape(bf16[1,256,2,256]{3,2,1,0:T(2,128)(2,1)} %param.5) | data formatting | bytes 524288 | tf_op jit(solution)/shard_map/broadcast_in_dim | solution.py:180
  4.1 0.9 %broadcast_in_dim.35 = bf16[2,16,16,512]{3,2,1,0:T(8,128)(2,1)} broadcast(bf16[16,16,512]{2,1,0:T(8,128)(2,1)S(1)} %broadcast_in_dim.34), dimensions={1,2,3} | broadcast | bytes 786432 | tf_op jit(solution)/shard_map/broadcast_in_dim | solution.py:180
  4.9 5.1 %all-to-all-start = ((bf16[32,16,512]{2,1,0:T(8,128)(2,1)}), bf16[32,16,512]{2,1,0:T(8,128)(2,1)}, u32[]{:S(2)}, u32[]{:S(2)}) async-start(bf16[32,16,512]{2,1,0:T(8,128)(2,1)} %bitcast), calls=%async_computation | async-start | bytes 1048576 | tf_op jit(solution)/shard_map/all_to_all | solution.py:182
  10.4 0.8 %fusion = bf16[8,2,128,256]{3,2,1,0:T(8,128)(2,1)S(1)} fusion(bf16[8,2,256,256]{3,2,1,0:T(8,128)(2,1)S(1)} %copy-done, s32[128]{0:T(128)S(1)} %eq.17), kind=kOutput, calls=%fused_computation.5 | convolution fusion | flops 268992512 | bytes 3146240 | tf_op jit(solution)/shard_map/nj,spkj->spnk/dot_general | solution.py:203
  11.2 0.6 %gather_fusion = s32[2,2,2]{2,1,0:T(2,128)S(1)} fusion(s32[2,2,2]{2,1,0:T(2,128)S(1)} %pad_add_fusion, s32[1024]{0:T(1024)S(1)} %pad_clamp_fusion.2), kind=kCustom, calls=%fused_computation | custom fusion | bytes 72 | tf_op jit(solution)/shard_map/jit(_take)/gather | solution.py:19
  11.9 0.2 slice_reduce_fusion
  12.1 0.1 copy.16
  12.3 0.1 copy.14
  12.4 1.4 %gather_fusion.1 = bf16[4,2,128,256]{3,2,1,0:T(8,128)(2,1)} fusion(bf16[8,2,128,256]{3,2,1,0:T(8,128)(2,1)S(1)} %fusion, s32[1024]{0:T(1024)S(1)} %pad_clamp_fusion.1), kind=kCustom, calls=%fused_computation.1 | custom fusion | bytes 1048592 | tf_op jit(solution)/shard_map/jit(_take)/gather | solution.py:118
  13.8 1.2 %copy_select_fusion.1 = bf16[2,2,2,8,16,256]{5,4,3,1,0,2:T(8,128)(2,1)S(1)} fusion(bf16[2,2,2,8,16,256]{5,4,3,2,1,0:T(8,128)(2,1)} %bitcast.55, pred[2,2]{1,0:T(4,128)(4,1)S(1)} %copy.14), kind=kLoop, calls=%fused_computation.14 | loop fusion | flops 262144 | bytes 1048580 | tf_op jit(solution)/shard_map/jit(_take)/select_n | solution.py:118
  15.0 0.1 copy.19
  15.1 0.1 copy.20
  15.3 0.1 maximum_bitcast_fusion.3
  15.4 0.1 maximum_bitcast_fusion
  15.5 1.1 %copy.18 = bf16[2,8,2,2,16,2,256]{6,5,4,3,2,1,0:T(2,128)(2,1)S(1)} copy(bf16[2,8,2,2,16,2,256]{6,4,1,2,0,3,5:T(8,128)(2,1)S(1)} %maximum_bitcast_fusion) | data formatting | bytes 2097152 | tf_op jit(solution)/shard_map/transpose | solution.py:124
  16.6 1.5 %reshape.175.weight_ref = bf16[2,512,512]{2,1,0:T(8,128)(2,1)} reshape(bf16[2,8,2,2,16,2,256]{6,5,4,3,2,1,0:T(2,128)(2,1)S(1)} %copy.18) | data formatting | bytes 2097152 | tf_op jit(solution)/shard_map/reshape | solution.py:124
  18.1 2.2 %gather_fusion.2 = bf16[4,2,256,256]{3,2,1,0:T(8,128)(2,1)S(1)} fusion(bf16[8,2,256,256]{3,2,1,0:T(8,128)(2,1)} %param.7, s32[1024]{0:T(1024)S(1)} %pad_clamp_fusion), kind=kCustom, calls=%fused_computation.2 | custom fusion | bytes 2097168 | tf_op jit(solution)/shard_map/jit(_take)/gather | solution.py:128
  20.3 0.2 copy_select_fusion
  20.5 0.1 slice_bitcast_fusion
  20.6 0.2 maximum_bitcast_fusion.1
  20.8 1.5 %pad_maximum_fusion = bf16[2,2,2,2,16,16,256]{6,5,0,3,4,2,1:T(8,128)(2,1)} fusion(bf16[1,2,2,2,16,16,256]{6,5,0,3,4,2,1:T(8,128)(2,1)S(1)} %get-tuple-element.10, bf16[1,2,2,2,16,16,256]{6,5,0,3,4,2,1:T(8,128)(2,1)S(1)} %get-tuple-element.9), kind=kLoop, calls=%fused_computation.3 | loop fusion | flops 1048576 | bytes 4194304 | tf_op jit(solution)/shard_map/stack | solution.py:131
  22.4 3.5 %all-to-all-done = bf16[32,16,512]{2,1,0:T(8,128)(2,1)} async-done(((bf16[32,16,512]{2,1,0:T(8,128)(2,1)}), bf16[32,16,512]{2,1,0:T(8,128)(2,1)}, u32[]{:S(2)}, u32[]{:S(2)}) %all-to-all-start) | async-done | bytes 524320 | tf_op jit(solution)/shard_map/all_to_all | solution.py:182
  25.9 4.2 %shard_map.55 = f32[16,8,2,256]{3,2,1,0:T(2,128)} custom-call(bf16[2,256,512]{2,1,0:T(8,128)(2,1)} %bitcast.1.stem_ref, bf16[2,512,512]{2,1,0:T(8,128)(2,1)} %reshape.175.weight_ref, bf16[2,2048,256]{2,1,0:T(8,128)(2,1)} %bitcast.53), custom_call_target="tpu_custom_call" | custom-call | flops 536870912 | bytes 3932160 | tf_op jit(solution)/shard_map/pallas_call | solution.py:94
  (26 shorter events, 0.7 us)
Async XLA Ops:
  0.0 10.4 %copy-start = (bf16[8,2,256,256]{3,2,1,0:T(8,128)(2,1)S(1)}, bf16[8,2,256,256]{3,2,1,0:T(8,128)(2,1)}, u32[]{:S(2)}) copy-start(bf16[8,2,256,256]{3,2,1,0:T(8,128)(2,1)} %param.6) | copy-start | bytes 6291460
  0.0 10.0 %copy-start.1 = (s32[256]{0:T(256)S(1)}, s32[256]{0:T(256)}, u32[]{:S(2)}) copy-start(s32[256]{0:T(256)} %param.9) | copy-start | bytes 3076
  0.0 11.2 %collective-permute-start = (s32[2,2]{1,0:T(2,128)}, s32[2,2]{1,0:T(2,128)S(1)}, u32[]{:S(2)}, u32[]{:S(2)}) collective-permute-start(s32[2,2]{1,0:T(2,128)} %bitcast.58), channel_id=1, source_target_pairs={{0,16},{16,0},{1,17},{17,1},{2,18},{18,2},{3,19},{19,3},{4,20},{20... | collective-permute-start | bytes 56 | tf_op jit(solution)/shard_map/ppermute | solution.py:14
  4.9 6.3 %copy-start.2 = (s32[1,2,2]{2,1,0:T(2,128)S(1)}, s32[1,2,2]{2,1,0:T(2,128)}, u32[]{:S(2)}) copy-start(s32[1,2,2]{2,1,0:T(2,128)} %param.8) | copy-start | bytes 52
  4.9 20.9 %all-to-all-start = ((bf16[32,16,512]{2,1,0:T(8,128)(2,1)}), bf16[32,16,512]{2,1,0:T(8,128)(2,1)}, u32[]{:S(2)}, u32[]{:S(2)}) async-start(bf16[32,16,512]{2,1,0:T(8,128)(2,1)} %bitcast), calls=%async_computation | async-start | bytes 1048576 | tf_op jit(solution)/shard_map/all_to_all | solution.py:182

commit v11 on v8

--- a/solution.py
+++ b/solution.py
@@ -51,15 +51,14 @@
 
 def regroup_kernel(stem_ref, weight_ref, second_ref, out_ref, lhs_ref):
     block_count, rows, _ = stem_ref.shape
-    q_local = weight_ref.shape[1] // 64
+    q_local = weight_ref.shape[2] // 64
     t_local = 16
     n_mode = rows // t_local
     lane = lax.broadcasted_iota(jnp.int32, (t_local, 128), 1)
     low = lane < 64
     for b in range(block_count):
-        product = lax.dot_general(
-            stem_ref[b], weight_ref[b], (((1,), (1,)), ((), ())),
-            preferred_element_type=jnp.float32,
+        product = jnp.dot(
+            stem_ref[b], weight_ref[b], preferred_element_type=jnp.float32
         ).astype(jnp.bfloat16)
         for pair in range(n_mode // 2):
             upper = product[(2 * pair) * t_local:(2 * pair + 1) * t_local]
@@ -127,7 +126,7 @@
         second_w = jnp.transpose(second_w, (1, 2, 4, 3, 0, 5, 6)).reshape(
             2, block_count * n_mode * group, out_width
         )
-        return regroup(stem_rows, first_w, second_w, q_local, t_local)
+        return regroup(stem_rows, jnp.swapaxes(first_w, 1, 2), second_w, q_local, t_local)
     else:
         second = jnp.take(w2_table, second_ids.reshape(-1), axis=0)
         second = jnp.swapaxes(second, 2, 3)

time: 29.8 us -> 29.8 us (level)
  waiting for transfers between devices: 3.5 us -> 1.22 us
  local copies, waits for them, and re-layouts: 9.94 us -> 12.2 us
    all_to_all x1, waiting for transfers between devices: 3.5 us -> 1.22 us  [on_device(): stem_rows = lax.all_to_all(payload, ('cuts', 'mode'), 0, 0, tiled=True)]
    reshape x1 -> x2, local copies, waits for them, and re-layouts: 1.51 us -> 3.78 us  [stacked_part(): jnp.transpose(first_w, (2, 4, 3, 1, 5, 0, 6))]
  transfers between devices with their start and end apart: 2 -> 2, of which waited for: 1 -> 1; matrix products, arithmetic and copies ran while one was open for 48% -> 56% of each run, Pallas kernels for 0% -> 0%
where the time goes in v11:
time: 29.8 us; the launch traced here: 29.4 us
  local copies, waits for them, and re-layouts  12.2 us (41%)
  starting transfers between devices  8 us (27%)
  Pallas kernels  3.56 us (12%)
  other arithmetic  3.44 us (12%)
  waiting for transfers between devices  1.22 us (4%)
  matrix products  0.83 us (3%)
    all_to_all x1, starting transfers between devices, on_device(): stem_rows = lax.all_to_all(payload, ('cuts', 'mode'), 0, 0, tiled=True)  5.06 us
    reshape x2, local copies, waits for them, and re-layouts, stacked_part(): jnp.transpose(first_w, (2, 4, 3, 1, 5, 0, 6))  3.78 us
    pallas_call x1, Pallas kernels, regroup(): pl.pallas_call(regroup_kernel, out_shape=out_shape, in_specs=[pl.BlockSpe...  3.56 us
    ppermute x1, starting transfers between devices, gather_over_cuts(): current = lax.ppermute(current, 'cuts', ring)  2.94 us
    gather x1, local copies, waits for them, and re-layouts, stacked_part(): second = jnp.take(w2_table, second_ids.reshape(-1), axis=0)  2.2 us
    broadcast_in_dim x2, local copies, waits for them, and re-layouts, on_device(): payload = jnp.broadcast_to(pieces, (n_cuts, n_mode, t_local, 2 * width))  1.97 us
    another operation x2, other arithmetic, stacked_part(): jnp.stack([jnp.stack([real_two, imag_two]), jnp.stack([-imag_two, real_tw...  1.72 us
    gather x1, local copies, waits for them, and re-layouts, stacked_part(): picked = jnp.take(first_t, first_ids.reshape(-1), axis=0)  1.37 us
  transfers between devices with their start and end apart: 2, of which 1 were waited for; matrix products, arithmetic and copies ran while one was open for 56% of the time, Pallas kernels for 0%

profile of v11, /device:TPU:0, one launch (start us, length us, event | category | flops | bytes accessed | tf_op | source)
XLA Modules:
  0.0 29.4 jit_solution(14143901368628534863)
XLA Ops:
  0.0 2.9 %collective-permute-start = (s32[2,2]{1,0:T(2,128)}, s32[2,2]{1,0:T(2,128)S(1)}, u32[]{:S(2)}, u32[]{:S(2)}) collective-permute-start(s32[2,2]{1,0:T(2,128)} %bitcast.60), channel_id=1, source_target_pairs={{0,16},{16,0},{1,17},{17,1},{2,18},{18,2},{3,19},{19,3},{4,20},{20... | collective-permute-start | bytes 56 | tf_op jit(solution)/shard_map/ppermute | solution.py:14
  2.9 1.1 %broadcast_in_dim.34 = bf16[16,16,512]{2,1,0:T(8,128)(2,1)S(1)} reshape(bf16[1,256,2,256]{3,2,1,0:T(2,128)(2,1)} %param.5) | data formatting | bytes 524288 | tf_op jit(solution)/shard_map/broadcast_in_dim | solution.py:172
  4.1 0.9 %broadcast_in_dim.35 = bf16[2,16,16,512]{3,2,1,0:T(8,128)(2,1)} broadcast(bf16[16,16,512]{2,1,0:T(8,128)(2,1)S(1)} %broadcast_in_dim.34), dimensions={1,2,3} | broadcast | bytes 786432 | tf_op jit(solution)/shard_map/broadcast_in_dim | solution.py:172
  4.9 5.1 %all-to-all-start = ((bf16[32,16,512]{2,1,0:T(8,128)(2,1)}), bf16[32,16,512]{2,1,0:T(8,128)(2,1)}, u32[]{:S(2)}, u32[]{:S(2)}) async-start(bf16[32,16,512]{2,1,0:T(8,128)(2,1)} %bitcast), calls=%async_computation | async-start | bytes 1048576 | tf_op jit(solution)/shard_map/all_to_all | solution.py:174
  10.4 0.8 %fusion = bf16[8,2,128,256]{3,2,1,0:T(8,128)(2,1)S(1)} fusion(bf16[8,2,256,256]{3,2,1,0:T(8,128)(2,1)S(1)} %copy-done, s32[128]{0:T(128)S(1)} %eq.17), kind=kOutput, calls=%fused_computation.5 | convolution fusion | flops 268992512 | bytes 3146240 | tf_op jit(solution)/shard_map/nj,spkj->spnk/dot_general | solution.py:195
  11.2 0.6 %gather_fusion = s32[2,2,2]{2,1,0:T(2,128)S(1)} fusion(s32[2,2,2]{2,1,0:T(2,128)S(1)} %pad_add_fusion, s32[1024]{0:T(1024)S(1)} %pad_clamp_fusion.2), kind=kCustom, calls=%fused_computation | custom fusion | bytes 72 | tf_op jit(solution)/shard_map/jit(_take)/gather | solution.py:19
  11.9 0.2 slice_reduce_fusion
  12.1 0.1 copy.16
  12.3 0.1 copy.14
  12.4 1.4 %gather_fusion.1 = bf16[4,2,128,256]{3,2,1,0:T(8,128)(2,1)} fusion(bf16[8,2,128,256]{3,2,1,0:T(8,128)(2,1)S(1)} %fusion, s32[1024]{0:T(1024)S(1)} %pad_clamp_fusion.1), kind=kCustom, calls=%fused_computation.1 | custom fusion | bytes 1048592 | tf_op jit(solution)/shard_map/jit(_take)/gather | solution.py:110
  13.8 1.2 %copy_select_fusion.1 = bf16[2,2,2,8,16,256]{5,4,3,1,0,2:T(8,128)(2,1)S(1)} fusion(bf16[2,2,2,8,16,256]{5,4,3,2,1,0:T(8,128)(2,1)} %bitcast.57, pred[2,2]{1,0:T(4,128)(4,1)S(1)} %copy.14), kind=kLoop, calls=%fused_computation.14 | loop fusion | flops 262144 | bytes 1048580 | tf_op jit(solution)/shard_map/jit(_take)/select_n | solution.py:110
  15.0 0.1 copy.20
  15.1 0.1 copy.21
  15.4 0.1 maximum_bitcast_fusion
  15.5 1.1 %copy.18 = bf16[2,8,2,2,16,2,256]{6,5,4,3,2,1,0:T(2,128)(2,1)S(1)} copy(bf16[2,8,2,2,16,2,256]{6,4,1,2,0,3,5:T(8,128)(2,1)S(1)} %maximum_bitcast_fusion) | data formatting | bytes 2097152 | tf_op jit(solution)/shard_map/transpose | solution.py:116
  16.6 1.5 %reshape.175 = bf16[2,512,512]{2,1,0:T(8,128)(2,1)} reshape(bf16[2,8,2,2,16,2,256]{6,5,4,3,2,1,0:T(2,128)(2,1)S(1)} %copy.18) | data formatting | bytes 2097152 | tf_op jit(solution)/shard_map/reshape | solution.py:116
  18.1 2.3 %copy.19 = bf16[2,512,512]{1,2,0:T(8,128)(2,1)} copy(bf16[2,512,512]{2,1,0:T(8,128)(2,1)} %reshape.175) | data formatting | bytes 2097152 | tf_op jit(solution)/shard_map/reshape | solution.py:116
  20.4 2.2 %gather_fusion.2 = bf16[4,2,256,256]{3,2,1,0:T(8,128)(2,1)S(1)} fusion(bf16[8,2,256,256]{3,2,1,0:T(8,128)(2,1)} %param.7, s32[1024]{0:T(1024)S(1)} %pad_clamp_fusion), kind=kCustom, calls=%fused_computation.2 | custom fusion | bytes 2097168 | tf_op jit(solution)/shard_map/jit(_take)/gather | solution.py:120
  22.6 0.2 copy_select_fusion
  22.8 0.1 slice_bitcast_fusion
  22.9 0.2 maximum_bitcast_fusion.1
  23.1 1.5 %pad_maximum_fusion = bf16[2,2,2,2,16,16,256]{6,5,0,3,4,2,1:T(8,128)(2,1)} fusion(bf16[1,2,2,2,16,16,256]{6,5,0,3,4,2,1:T(8,128)(2,1)S(1)} %get-tuple-element.10, bf16[1,2,2,2,16,16,256]{6,5,0,3,4,2,1:T(8,128)(2,1)S(1)} %get-tuple-element.9), kind=kLoop, calls=%fused_computation.3 | loop fusion | flops 1048576 | bytes 4194304 | tf_op jit(solution)/shard_map/stack | solution.py:123
  24.6 1.2 %all-to-all-done = bf16[32,16,512]{2,1,0:T(8,128)(2,1)} async-done(((bf16[32,16,512]{2,1,0:T(8,128)(2,1)}), bf16[32,16,512]{2,1,0:T(8,128)(2,1)}, u32[]{:S(2)}, u32[]{:S(2)}) %all-to-all-start) | async-done | bytes 524320 | tf_op jit(solution)/shard_map/all_to_all | solution.py:174
  25.9 3.6 %shard_map.55 = f32[16,8,2,256]{3,2,1,0:T(2,128)} custom-call(bf16[2,256,512]{2,1,0:T(8,128)(2,1)} %bitcast.1.stem_ref, bf16[2,512,512]{2,1,0:T(8,128)(2,1)} %bitcast.56, bf16[2,2048,256]{2,1,0:T(8,128)(2,1)} %bitcast.54), custom_call_target="tpu_custom_call" | custom-call | flops 536870912 | bytes 3932160 | tf_op jit(solution)/shard_map/pallas_call | solution.py:90
  (27 shorter events, 0.8 us)
Async XLA Ops:
  0.0 10.4 %copy-start = (bf16[8,2,256,256]{3,2,1,0:T(8,128)(2,1)S(1)}, bf16[8,2,256,256]{3,2,1,0:T(8,128)(2,1)}, u32[]{:S(2)}) copy-start(bf16[8,2,256,256]{3,2,1,0:T(8,128)(2,1)} %param.6) | copy-start | bytes 6291460
  0.0 10.0 %copy-start.1 = (s32[256]{0:T(256)S(1)}, s32[256]{0:T(256)}, u32[]{:S(2)}) copy-start(s32[256]{0:T(256)} %param.9) | copy-start | bytes 3076
  0.0 11.2 %collective-permute-start = (s32[2,2]{1,0:T(2,128)}, s32[2,2]{1,0:T(2,128)S(1)}, u32[]{:S(2)}, u32[]{:S(2)}) collective-permute-start(s32[2,2]{1,0:T(2,128)} %bitcast.60), channel_id=1, source_target_pairs={{0,16},{16,0},{1,17},{17,1},{2,18},{18,2},{3,19},{19,3},{4,20},{20... | collective-permute-start | bytes 56 | tf_op jit(solution)/shard_map/ppermute | solution.py:14
  4.9 6.3 %copy-start.2 = (s32[1,2,2]{2,1,0:T(2,128)S(1)}, s32[1,2,2]{2,1,0:T(2,128)}, u32[]{:S(2)}) copy-start(s32[1,2,2]{2,1,0:T(2,128)} %param.8) | copy-start | bytes 52
  4.9 20.9 %all-to-all-start = ((bf16[32,16,512]{2,1,0:T(8,128)(2,1)}), bf16[32,16,512]{2,1,0:T(8,128)(2,1)}, u32[]{:S(2)}, u32[]{:S(2)}) async-start(bf16[32,16,512]{2,1,0:T(8,128)(2,1)} %bitcast), calls=%async_computation | async-start | bytes 1048576 | tf_op jit(solution)/shard_map/all_to_all | solution.py:174

commit v12 on v11

--- a/solution.py
+++ b/solution.py
@@ -93,6 +93,7 @@
         in_specs=[pl.BlockSpec(memory_space=pltpu.VMEM)] * 3,
         out_specs=pl.BlockSpec(memory_space=pltpu.VMEM),
         scratch_shapes=[pltpu.VMEM(lhs_shape, jnp.bfloat16)],
+        compiler_params=pltpu.CompilerParams(vmem_limit_bytes=16 * 1024 * 1024),
         cost_estimate=pl.CostEstimate(
             flops=flops,
             transcendentals=0,

time: 29.8 us -> 30.6 us (1.027)
  local copies, waits for them, and re-layouts: 12.2 us -> 14 us
  other arithmetic: 3.44 us -> 4.66 us
  waiting for transfers between devices: 1.22 us -> 0.01 us
  Pallas kernels: 3.56 us -> 2.52 us
    unnamed x6 -> x8, local copies, waits for them, and re-layouts: 0.01 us -> 1.6 us
    select_n x2, other arithmetic: 0.17 us -> 1.39 us  [stacked_part(): second = jnp.take(w2_table, second_ids.reshape(-1), axis=0)]
    all_to_all x1, waiting for transfers between devices: 1.22 us -> 0.01 us  [on_device(): stem_rows = lax.all_to_all(payload, ('cuts', 'mode'), 0, 0, tiled=True)]
    pallas_call x1, Pallas kernels: 3.56 us -> 2.52 us  [regroup(): pl.pallas_call(regroup_kernel, out_shape=out_shape, in_specs=[pl.BlockSpe...]
    gather x1, local copies, waits for them, and re-layouts: 2.2 us -> 3.17 us  [stacked_part(): second = jnp.take(w2_table, second_ids.reshape(-1), axis=0)]
    reshape x2, local copies, waits for them, and re-layouts: 3.78 us -> 2.98 us  [stacked_part(): jnp.transpose(first_w, (2, 4, 3, 1, 5, 0, 6))]
  transfers between devices with their start and end apart: 2 -> 2, of which waited for: 1 -> 0; matrix products, arithmetic and copies ran while one was open for 56% -> 59% of each run, Pallas kernels for 0% -> 0%
where the time goes in v12:
time: 30.6 us; the launch traced here: 30.1 us
  local copies, waits for them, and re-layouts  14 us (46%)
  starting transfers between devices  8 us (26%)
  other arithmetic  4.66 us (15%)
  Pallas kernels  2.52 us (8%)
  matrix products  0.82 us (3%)
    all_to_all x1, starting transfers between devices, on_device(): stem_rows = lax.all_to_all(payload, ('cuts', 'mode'), 0, 0, tiled=True)  5.06 us
    gather x1, local copies, waits for them, and re-layouts, stacked_part(): second = jnp.take(w2_table, second_ids.reshape(-1), axis=0)  3.17 us
    reshape x2, local copies, waits for them, and re-layouts, stacked_part(): jnp.transpose(first_w, (2, 4, 3, 1, 5, 0, 6))  2.98 us
    ppermute x1, starting transfers between devices, gather_over_cuts(): current = lax.ppermute(current, 'cuts', ring)  2.94 us
    pallas_call x1, Pallas kernels, regroup(): pl.pallas_call(regroup_kernel, out_shape=out_shape, in_specs=[pl.BlockSpe...  2.52 us
    broadcast_in_dim x2, local copies, waits for them, and re-layouts, on_device(): payload = jnp.broadcast_to(pieces, (n_cuts, n_mode, t_local, 2 * width))  1.98 us
    another operation x2, other arithmetic, stacked_part(): jnp.stack([jnp.stack([real_two, imag_two]), jnp.stack([-imag_two, real_tw...  1.72 us
    unnamed x8, local copies, waits for them, and re-layouts  1.6 us
  transfers between devices with their start and end apart: 2, of which 0 were waited for; matrix products, arithmetic and copies ran while one was open for 59% of the time, Pallas kernels for 0%

profile of v12, /device:TPU:0, one launch (start us, length us, event | category | flops | bytes accessed | tf_op | source)
XLA Modules:
  0.0 30.1 jit_solution(13875833793446068173)
XLA Ops:
  0.0 2.9 %collective-permute-start = (s32[2,2]{1,0:T(2,128)}, s32[2,2]{1,0:T(2,128)S(1)}, u32[]{:S(2)}, u32[]{:S(2)}) collective-permute-start(s32[2,2]{1,0:T(2,128)} %bitcast.60), channel_id=1, source_target_pairs={{0,16},{16,0},{1,17},{17,1},{2,18},{18,2},{3,19},{19,3},{4,20},{20... | collective-permute-start | bytes 56 | tf_op jit(solution)/shard_map/ppermute | solution.py:14
  2.9 1.1 %broadcast_in_dim.34 = bf16[16,16,512]{2,1,0:T(8,128)(2,1)S(1)} reshape(bf16[1,256,2,256]{3,2,1,0:T(2,128)(2,1)} %param.5) | data formatting | bytes 524288 | tf_op jit(solution)/shard_map/broadcast_in_dim | solution.py:173
  4.1 0.9 %broadcast_in_dim.35 = bf16[2,16,16,512]{3,2,1,0:T(8,128)(2,1)} broadcast(bf16[16,16,512]{2,1,0:T(8,128)(2,1)S(1)} %broadcast_in_dim.34), dimensions={1,2,3} | broadcast | bytes 786432 | tf_op jit(solution)/shard_map/broadcast_in_dim | solution.py:173
  4.9 5.1 %all-to-all-start = ((bf16[32,16,512]{2,1,0:T(8,128)(2,1)}), bf16[32,16,512]{2,1,0:T(8,128)(2,1)}, u32[]{:S(2)}, u32[]{:S(2)}) async-start(bf16[32,16,512]{2,1,0:T(8,128)(2,1)} %bitcast), calls=%async_computation | async-start | bytes 1048576 | tf_op jit(solution)/shard_map/all_to_all | solution.py:175
  10.4 0.8 %fusion = bf16[8,2,128,256]{3,2,1,0:T(8,128)(2,1)S(1)} fusion(bf16[8,2,256,256]{3,2,1,0:T(8,128)(2,1)S(1)} %copy-done, s32[128]{0:T(128)S(1)} %eq.17), kind=kOutput, calls=%fused_computation.5 | convolution fusion | flops 268992512 | bytes 3146240 | tf_op jit(solution)/shard_map/nj,spkj->spnk/dot_general | solution.py:196
  11.2 0.6 %gather_fusion = s32[2,2,2]{2,1,0:T(2,128)S(1)} fusion(s32[2,2,2]{2,1,0:T(2,128)S(1)} %pad_add_fusion, s32[1024]{0:T(1024)S(1)} %pad_clamp_fusion.2), kind=kCustom, calls=%fused_computation | custom fusion | bytes 72 | tf_op jit(solution)/shard_map/jit(_take)/gather | solution.py:19
  11.9 0.2 slice_reduce_fusion
  12.1 0.1 copy.16
  12.3 0.1 copy.14
  12.4 1.4 %gather_fusion.1 = bf16[4,2,128,256]{3,2,1,0:T(8,128)(2,1)} fusion(bf16[8,2,128,256]{3,2,1,0:T(8,128)(2,1)S(1)} %fusion, s32[1024]{0:T(1024)S(1)} %pad_clamp_fusion.1), kind=kCustom, calls=%fused_computation.1 | custom fusion | bytes 1048592 | tf_op jit(solution)/shard_map/jit(_take)/gather | solution.py:111
  13.8 1.2 %copy_select_fusion.1 = bf16[2,2,2,8,16,256]{5,4,3,1,0,2:T(8,128)(2,1)S(1)} fusion(bf16[2,2,2,8,16,256]{5,4,3,2,1,0:T(8,128)(2,1)} %bitcast.57, pred[2,2]{1,0:T(4,128)(4,1)S(1)} %copy.14), kind=kLoop, calls=%fused_computation.14 | loop fusion | flops 262144 | bytes 1048580 | tf_op jit(solution)/shard_map/jit(_take)/select_n | solution.py:111
  15.0 0.1 copy.20
  15.1 0.1 copy.21
  15.4 0.1 maximum_bitcast_fusion
  15.5 1.1 %copy.18 = bf16[2,8,2,2,16,2,256]{6,5,4,3,2,1,0:T(2,128)(2,1)S(1)} copy(bf16[2,8,2,2,16,2,256]{6,4,1,2,0,3,5:T(8,128)(2,1)S(1)} %maximum_bitcast_fusion) | data formatting | bytes 2097152 | tf_op jit(solution)/shard_map/transpose | solution.py:117
  16.6 1.5 %reshape.175 = bf16[2,512,512]{2,1,0:T(8,128)(2,1)} reshape(bf16[2,8,2,2,16,2,256]{6,5,4,3,2,1,0:T(2,128)(2,1)S(1)} %copy.18) | data formatting | bytes 2097152 | tf_op jit(solution)/shard_map/reshape | solution.py:117
  18.1 1.5 %copy.19 = bf16[2,512,512]{1,2,0:T(8,128)(2,1)S(1)} copy(bf16[2,512,512]{2,1,0:T(8,128)(2,1)} %reshape.175) | data formatting | bytes 2097152 | tf_op jit(solution)/shard_map/reshape | solution.py:117
  19.6 3.2 %gather_fusion.2 = bf16[4,2,256,256]{3,2,1,0:T(8,128)(2,1)} fusion(bf16[8,2,256,256]{3,2,1,0:T(8,128)(2,1)} %param.7, s32[1024]{0:T(1024)S(1)} %pad_clamp_fusion), kind=kCustom, calls=%fused_computation.2 | custom fusion | bytes 2097168 | tf_op jit(solution)/shard_map/jit(_take)/gather | solution.py:121
  22.8 1.4 %copy_select_fusion = bf16[2,2,2,16,16,256]{5,4,1,3,0,2:T(8,128)(2,1)S(1)} fusion(bf16[2,2,2,16,16,256]{5,4,3,2,1,0:T(8,128)(2,1)} %bitcast.56, pred[2,2]{1,0:T(4,128)(4,1)S(1)} %copy.20), kind=kLoop, calls=%fused_computation.9 | loop fusion | flops 524288 | bytes 2097156 | tf_op jit(solution)/shard_map/jit(_take)/select_n | solution.py:121
  24.2 0.1 slice_bitcast_fusion
  24.3 0.2 maximum_bitcast_fusion.1
  24.5 1.5 %pad_maximum_fusion = bf16[2,2,2,2,16,16,256]{6,5,0,3,4,2,1:T(8,128)(2,1)} fusion(bf16[1,2,2,2,16,16,256]{6,5,0,3,4,2,1:T(8,128)(2,1)S(1)} %get-tuple-element.10, bf16[1,2,2,2,16,16,256]{6,5,0,3,4,2,1:T(8,128)(2,1)S(1)} %get-tuple-element.9), kind=kLoop, calls=%fused_computation.3 | loop fusion | flops 1048576 | bytes 4194304 | tf_op jit(solution)/shard_map/stack | solution.py:124
  26.0 1.6 %copy-done.1 = bf16[2,2,2,2,16,16,256]{6,5,0,3,4,2,1:T(8,128)(2,1)S(1)} copy-done((bf16[2,2,2,2,16,16,256]{6,5,0,3,4,2,1:T(8,128)(2,1)S(1)}, bf16[2,2,2,2,16,16,256]{6,5,0,3,4,2,1:T(8,128)(2,1)}, u32[]{:S(2)}) %copy-start.1) | copy-done | bytes 2097176
  27.6 2.5 %shard_map.55 = f32[16,8,2,256]{3,2,1,0:T(2,128)} custom-call(bf16[2,256,512]{2,1,0:T(8,128)(2,1)} %bitcast.1.stem_ref, bf16[2,512,512]{2,1,0:T(8,128)(2,1)S(1)} %bitcast.55, bf16[2,2048,256]{2,1,0:T(8,128)(2,1)S(1)} %bitcast.54), custom_call_target="tpu_custom_call" | custom-call | flops 536870912 | bytes 3932160 | tf_op jit(solution)/shard_map/pallas_call | solution.py:90
  (29 shorter events, 0.8 us)
Async XLA Ops:
  0.0 10.4 %copy-start = (bf16[8,2,256,256]{3,2,1,0:T(8,128)(2,1)S(1)}, bf16[8,2,256,256]{3,2,1,0:T(8,128)(2,1)}, u32[]{:S(2)}) copy-start(bf16[8,2,256,256]{3,2,1,0:T(8,128)(2,1)} %param.6) | copy-start | bytes 6291460
  0.0 10.1 %copy-start.2 = (s32[256]{0:T(256)S(1)}, s32[256]{0:T(256)}, u32[]{:S(2)}) copy-start(s32[256]{0:T(256)} %param.9) | copy-start | bytes 3076
  0.0 11.2 %collective-permute-start = (s32[2,2]{1,0:T(2,128)}, s32[2,2]{1,0:T(2,128)S(1)}, u32[]{:S(2)}, u32[]{:S(2)}) collective-permute-start(s32[2,2]{1,0:T(2,128)} %bitcast.60), channel_id=1, source_target_pairs={{0,16},{16,0},{1,17},{17,1},{2,18},{18,2},{3,19},{19,3},{4,20},{20... | collective-permute-start | bytes 56 | tf_op jit(solution)/shard_map/ppermute | solution.py:14
  4.9 6.3 %copy-start.3 = (s32[1,2,2]{2,1,0:T(2,128)S(1)}, s32[1,2,2]{2,1,0:T(2,128)}, u32[]{:S(2)}) copy-start(s32[1,2,2]{2,1,0:T(2,128)} %param.8) | copy-start | bytes 52
  4.9 21.1 %all-to-all-start = ((bf16[32,16,512]{2,1,0:T(8,128)(2,1)}), bf16[32,16,512]{2,1,0:T(8,128)(2,1)}, u32[]{:S(2)}, u32[]{:S(2)}) async-start(bf16[32,16,512]{2,1,0:T(8,128)(2,1)} %bitcast), calls=%async_computation | async-start | bytes 1048576 | tf_op jit(solution)/shard_map/all_to_all | solution.py:175
  26.0 1.6 %copy-start.1 = (bf16[2,2,2,2,16,16,256]{6,5,0,3,4,2,1:T(8,128)(2,1)S(1)}, bf16[2,2,2,2,16,16,256]{6,5,0,3,4,2,1:T(8,128)(2,1)}, u32[]{:S(2)}) copy-start(bf16[2,2,2,2,16,16,256]{6,5,0,3,4,2,1:T(8,128)(2,1)} %pad_maximum_fusion) | copy-start | bytes 6291460

commit v13 on v11

--- a/solution.py
+++ b/solution.py
@@ -50,16 +50,24 @@
 
 
 def regroup_kernel(stem_ref, weight_ref, second_ref, out_ref, lhs_ref):
-    block_count, rows, _ = stem_ref.shape
+    pieces, t_local, _, width = stem_ref.shape
+    block_count = weight_ref.shape[0]
     q_local = weight_ref.shape[2] // 64
-    t_local = 16
-    n_mode = rows // t_local
+    n_mode = pieces // block_count
+    rows = n_mode * t_local
     lane = lax.broadcasted_iota(jnp.int32, (t_local, 128), 1)
     low = lane < 64
     for b in range(block_count):
+        own = stem_ref[b * n_mode:(b + 1) * n_mode]
         product = jnp.dot(
-            stem_ref[b], weight_ref[b], preferred_element_type=jnp.float32
-        ).astype(jnp.bfloat16)
+            own[:, :, 0, :].reshape(rows, width), weight_ref[b, :width],
+            preferred_element_type=jnp.float32,
+        )
+        product = product + jnp.dot(
+            own[:, :, 1, :].reshape(rows, width), weight_ref[b, width:],
+            preferred_element_type=jnp.float32,
+        )
+        product = product.astype(jnp.bfloat16)
         for pair in range(n_mode // 2):
             upper = product[(2 * pair) * t_local:(2 * pair + 1) * t_local]
             lower = product[(2 * pair + 1) * t_local:(2 * pair + 2) * t_local]
@@ -79,8 +87,9 @@
 
 
 def regroup(stem_rows, first_w, second_w, q_local, t_local):
-    block_count, rows, _ = stem_rows.shape
-    n_mode = rows // t_local
+    block_count = first_w.shape[0]
+    n_mode = stem_rows.shape[0] // block_count
+    rows = n_mode * t_local
     lhs_shape = (q_local * t_local, block_count * n_mode * 64)
     out_shape = jax.ShapeDtypeStruct(
         (t_local, q_local, second_w.shape[0], second_w.shape[2]), jnp.float32
@@ -101,7 +110,7 @@
         ),
     )(stem_rows, first_w, second_w)
 
-def stacked_part(stem_rows, first_t, w2_table, first_ids, second_ids, sizes):
+def stacked_part(stem_rows, first_t, w2_table, first_ids, second_ids, sizes, stem_parts):
     n_mode, t_local, n_cuts, a_count, q_local = sizes
     block_count = stem_rows.shape[0]
     width = first_t.shape[3]
@@ -126,7 +135,7 @@
         second_w = jnp.transpose(second_w, (1, 2, 4, 3, 0, 5, 6)).reshape(
             2, block_count * n_mode * group, out_width
         )
-        return regroup(stem_rows, jnp.swapaxes(first_w, 1, 2), second_w, q_local, t_local)
+        return regroup(stem_parts, jnp.swapaxes(first_w, 1, 2), second_w, q_local, t_local)
     else:
         second = jnp.take(w2_table, second_ids.reshape(-1), axis=0)
         second = jnp.swapaxes(second, 2, 3)
@@ -168,11 +177,11 @@
     me = lax.axis_index("cuts")
     sizes = (n_mode, t_local, n_cuts, a_count, q_local)
 
-    pieces = stem_blocks[0].reshape(1, n_mode, t_local, 2 * width)
-    payload = jnp.broadcast_to(pieces, (n_cuts, n_mode, t_local, 2 * width))
-    payload = payload.reshape(n_cuts * n_mode, t_local, 2 * width)
-    stem_rows = lax.all_to_all(payload, ("cuts", "mode"), 0, 0, tiled=True)
-    stem_rows = stem_rows.reshape(block_count, n_mode * t_local, 2 * width)
+    pieces = stem_blocks[0].reshape(1, n_mode, t_local, 2, width)
+    payload = jnp.broadcast_to(pieces, (n_cuts, n_mode, t_local, 2, width))
+    payload = payload.reshape(n_cuts * n_mode, t_local, 2, width)
+    stem_parts = lax.all_to_all(payload, ("cuts", "mode"), 0, 0, tiled=True)
+    stem_rows = stem_parts.reshape(block_count, n_mode * t_local, 2 * width)
 
     all_ids = gather_over_cuts(slice_ids[0], n_cuts)
     first_ids = all_ids[:, :, 0].T
@@ -195,7 +204,7 @@
         first_t = jnp.einsum(
             "nj,spkj->spnk", picker_t, w1_table, preferred_element_type=jnp.float32
         ).astype(w1_table.dtype)
-        return stacked_part(stem_rows, first_t, w2_table, first_ids, second_ids, sizes)
+        return stacked_part(stem_rows, first_t, w2_table, first_ids, second_ids, sizes, stem_parts)
     else:
         def one_block(index, running):
             stem_one = lax.dynamic_slice_in_dim(stem_rows, index, 1, axis=0)

time: 29.8 us -> 30.9 us (1.037)
  local copies, waits for them, and re-layouts: 12.2 us -> 13.1 us
  Pallas kernels: 3.56 us -> 4.4 us
  waiting for transfers between devices: 1.22 us -> 0.59 us
    pallas_call x1, Pallas kernels: 3.56 us -> 4.4 us  [regroup(): pl.pallas_call(regroup_kernel, out_shape=out_shape, in_specs=[pl.BlockSpe...]
    reshape x1, local copies, waits for them, and re-layouts: 0.08 us -> 0.76 us  [on_device(): perm_grid = mode_perm.reshape(a_count, q_count)]
    all_to_all x1, waiting for transfers between devices: 1.22 us -> 0.58 us  [on_device(): stem_parts = lax.all_to_all(payload, ('cuts', 'mode'), 0, 0, tiled=True)]
    broadcast_in_dim x2 -> x1, local copies, waits for them, and re-layouts: 1.97 us -> 2.24 us  [on_device(): payload = jnp.broadcast_to(pieces, (n_cuts, n_mode, t_local, 2, width))]
  transfers between devices with their start and end apart: 2 -> 2, of which waited for: 1 -> 1; matrix products, arithmetic and copies ran while one was open for 56% -> 57% of each run, Pallas kernels for 0% -> 0%
where the time goes in v13:
time: 30.9 us; the launch traced here: 30.6 us
  local copies, waits for them, and re-layouts  13.1 us (42%)
  starting transfers between devices  8.05 us (26%)
  Pallas kernels  4.4 us (14%)
  other arithmetic  3.43 us (11%)
  matrix products  0.82 us (3%)
  waiting for transfers between devices  0.59 us (2%)
    all_to_all x1, starting transfers between devices, on_device(): stem_parts = lax.all_to_all(payload, ('cuts', 'mode'), 0, 0, tiled=True)  5.11 us
    pallas_call x1, Pallas kernels, regroup(): pl.pallas_call(regroup_kernel, out_shape=out_shape, in_specs=[pl.BlockSpe...  4.4 us
    reshape x2, local copies, waits for them, and re-layouts, stacked_part(): jnp.transpose(first_w, (2, 4, 3, 1, 5, 0, 6))  3.77 us
    ppermute x1, starting transfers between devices, gather_over_cuts(): current = lax.ppermute(current, 'cuts', ring)  2.94 us
    broadcast_in_dim x1, local copies, waits for them, and re-layouts, on_device(): payload = jnp.broadcast_to(pieces, (n_cuts, n_mode, t_local, 2, width))  2.24 us
    gather x1, local copies, waits for them, and re-layouts, stacked_part(): second = jnp.take(w2_table, second_ids.reshape(-1), axis=0)  2.2 us
    another operation x2, other arithmetic, stacked_part(): jnp.stack([jnp.stack([real_two, imag_two]), jnp.stack([-imag_two, real_tw...  1.71 us
    gather x1, local copies, waits for them, and re-layouts, stacked_part(): picked = jnp.take(first_t, first_ids.reshape(-1), axis=0)  1.37 us
  transfers between devices with their start and end apart: 2, of which 1 were waited for; matrix products, arithmetic and copies ran while one was open for 57% of the time, Pallas kernels for 0%

profile of v13, /device:TPU:0, one launch (start us, length us, event | category | flops | bytes accessed | tf_op | source)
XLA Modules:
  0.0 30.6 jit_solution(6008990010714760108)
XLA Ops:
  0.0 2.9 %collective-permute-start = (s32[2,2]{1,0:T(2,128)}, s32[2,2]{1,0:T(2,128)S(1)}, u32[]{:S(2)}, u32[]{:S(2)}) collective-permute-start(s32[2,2]{1,0:T(2,128)} %bitcast.61), channel_id=1, source_target_pairs={{0,16},{16,0},{1,17},{17,1},{2,18},{18,2},{3,19},{19,3},{4,20},{20... | collective-permute-start | bytes 56 | tf_op jit(solution)/shard_map/ppermute | solution.py:14
  2.9 2.2 %broadcast_in_dim.35 = bf16[2,16,16,2,256]{4,3,2,1,0:T(2,128)(2,1)} broadcast(bf16[16,16,2,256]{3,2,1,0:T(2,128)(2,1)} %bitcast.58), dimensions={1,2,3,4} | broadcast | bytes 786432 | tf_op jit(solution)/shard_map/broadcast_in_dim | solution.py:181
  5.2 5.1 %all-to-all-start = ((bf16[32,16,2,256]{3,2,1,0:T(2,128)(2,1)}), bf16[32,16,2,256]{3,2,1,0:T(2,128)(2,1)}, u32[]{:S(2)}, u32[]{:S(2)}) async-start(bf16[32,16,2,256]{3,2,1,0:T(2,128)(2,1)} %bitcast.1), calls=%async_computation | async-start | bytes 1048576 | tf_op jit(solution)/shard_map/all_to_all | solution.py:183
  10.4 0.8 %reshape.169 = s32[16,16]{1,0:T(8,128)S(1)} reshape(s32[256]{0:T(256)} %param.9) | data formatting | bytes 2048 | tf_op jit(solution)/shard_map/reshape | solution.py:190
  11.4 0.8 %fusion = bf16[8,2,128,256]{3,2,1,0:T(8,128)(2,1)S(1)} fusion(bf16[8,2,256,256]{3,2,1,0:T(8,128)(2,1)S(1)} %copy-done, s32[128]{0:T(128)S(1)} %eq.17), kind=kOutput, calls=%fused_computation.5 | convolution fusion | flops 268992512 | bytes 3146240 | tf_op jit(solution)/shard_map/nj,spkj->spnk/dot_general | solution.py:204
  12.2 0.6 %gather_fusion = s32[2,2,2]{2,1,0:T(2,128)S(1)} fusion(s32[2,2,2]{2,1,0:T(2,128)S(1)} %pad_add_fusion, s32[1024]{0:T(1024)S(1)} %pad_clamp_fusion.2), kind=kCustom, calls=%fused_computation | custom fusion | bytes 72 | tf_op jit(solution)/shard_map/jit(_take)/gather | solution.py:19
  12.9 0.2 slice_reduce_fusion
  13.1 0.1 copy.16
  13.3 0.1 copy.14
  13.4 1.4 %gather_fusion.1 = bf16[4,2,128,256]{3,2,1,0:T(8,128)(2,1)} fusion(bf16[8,2,128,256]{3,2,1,0:T(8,128)(2,1)S(1)} %fusion, s32[1024]{0:T(1024)S(1)} %pad_clamp_fusion.1), kind=kCustom, calls=%fused_computation.1 | custom fusion | bytes 1048592 | tf_op jit(solution)/shard_map/jit(_take)/gather | solution.py:119
  14.8 1.2 %copy_select_fusion.1 = bf16[2,2,2,8,16,256]{5,4,3,1,0,2:T(8,128)(2,1)S(1)} fusion(bf16[2,2,2,8,16,256]{5,4,3,2,1,0:T(8,128)(2,1)} %bitcast.57, pred[2,2]{1,0:T(4,128)(4,1)S(1)} %copy.14), kind=kLoop, calls=%fused_computation.14 | loop fusion | flops 262144 | bytes 1048580 | tf_op jit(solution)/shard_map/jit(_take)/select_n | solution.py:119
  16.0 0.1 copy.20
  16.1 0.1 copy.21
  16.4 0.1 maximum_bitcast_fusion
  16.5 1.1 %copy.18 = bf16[2,8,2,2,16,2,256]{6,5,4,3,2,1,0:T(2,128)(2,1)S(1)} copy(bf16[2,8,2,2,16,2,256]{6,4,1,2,0,3,5:T(8,128)(2,1)S(1)} %maximum_bitcast_fusion) | data formatting | bytes 2097152 | tf_op jit(solution)/shard_map/transpose | solution.py:125
  17.6 1.5 %reshape.171 = bf16[2,512,512]{2,1,0:T(8,128)(2,1)} reshape(bf16[2,8,2,2,16,2,256]{6,5,4,3,2,1,0:T(2,128)(2,1)S(1)} %copy.18) | data formatting | bytes 2097152 | tf_op jit(solution)/shard_map/reshape | solution.py:125
  19.1 2.3 %copy.19 = bf16[2,512,512]{1,2,0:T(8,128)(2,1)} copy(bf16[2,512,512]{2,1,0:T(8,128)(2,1)} %reshape.171) | data formatting | bytes 2097152 | tf_op jit(solution)/shard_map/reshape | solution.py:125
  21.4 2.2 %gather_fusion.2 = bf16[4,2,256,256]{3,2,1,0:T(8,128)(2,1)S(1)} fusion(bf16[8,2,256,256]{3,2,1,0:T(8,128)(2,1)} %param.7, s32[1024]{0:T(1024)S(1)} %pad_clamp_fusion), kind=kCustom, calls=%fused_computation.2 | custom fusion | bytes 2097168 | tf_op jit(solution)/shard_map/jit(_take)/gather | solution.py:129
  23.6 0.2 copy_select_fusion
  23.8 0.1 slice_bitcast_fusion
  23.9 0.2 maximum_bitcast_fusion.1
  24.1 1.5 %pad_maximum_fusion = bf16[2,2,2,2,16,16,256]{6,5,0,3,4,2,1:T(8,128)(2,1)} fusion(bf16[1,2,2,2,16,16,256]{6,5,0,3,4,2,1:T(8,128)(2,1)S(1)} %get-tuple-element.10, bf16[1,2,2,2,16,16,256]{6,5,0,3,4,2,1:T(8,128)(2,1)S(1)} %get-tuple-element.9), kind=kLoop, calls=%fused_computation.3 | loop fusion | flops 1048576 | bytes 4194304 | tf_op jit(solution)/shard_map/stack | solution.py:132
  25.6 0.6 %all-to-all-done.stem_ref = bf16[32,16,2,256]{3,2,1,0:T(2,128)(2,1)} async-done(((bf16[32,16,2,256]{3,2,1,0:T(2,128)(2,1)}), bf16[32,16,2,256]{3,2,1,0:T(2,128)(2,1)}, u32[]{:S(2)}, u32[]{:S(2)}) %all-to-all-start) | async-done | bytes 524320 | tf_op jit(solution)/shard_map/all_to_all | solution.py:183
  26.2 4.4 %shard_map.55 = f32[16,8,2,256]{3,2,1,0:T(2,128)} custom-call(bf16[32,16,2,256]{3,2,1,0:T(2,128)(2,1)} %all-to-all-done.stem_ref, bf16[2,512,512]{2,1,0:T(8,128)(2,1)} %bitcast.56, bf16[2,2048,256]{2,1,0:T(8,128)(2,1)} %bitcast.54), custom_call_target="tpu_custom_call" | custom-call | flops 536870912 | bytes 3932160 | tf_op jit(solution)/shard_map/pallas_call | solution.py:99
  (24 shorter events, 0.7 us)
Async XLA Ops:
  0.0 11.4 %copy-start = (bf16[8,2,256,256]{3,2,1,0:T(8,128)(2,1)S(1)}, bf16[8,2,256,256]{3,2,1,0:T(8,128)(2,1)}, u32[]{:S(2)}) copy-start(bf16[8,2,256,256]{3,2,1,0:T(8,128)(2,1)} %param.6) | copy-start | bytes 6291460
  0.0 12.2 %collective-permute-start = (s32[2,2]{1,0:T(2,128)}, s32[2,2]{1,0:T(2,128)S(1)}, u32[]{:S(2)}, u32[]{:S(2)}) collective-permute-start(s32[2,2]{1,0:T(2,128)} %bitcast.61), channel_id=1, source_target_pairs={{0,16},{16,0},{1,17},{17,1},{2,18},{18,2},{3,19},{19,3},{4,20},{20... | collective-permute-start | bytes 56 | tf_op jit(solution)/shard_map/ppermute | solution.py:14
  5.2 7.0 %copy-start.1 = (s32[1,2,2]{2,1,0:T(2,128)S(1)}, s32[1,2,2]{2,1,0:T(2,128)}, u32[]{:S(2)}) copy-start(s32[1,2,2]{2,1,0:T(2,128)} %param.8) | copy-start | bytes 52
  5.2 21.0 %all-to-all-start = ((bf16[32,16,2,256]{3,2,1,0:T(2,128)(2,1)}), bf16[32,16,2,256]{3,2,1,0:T(2,128)(2,1)}, u32[]{:S(2)}, u32[]{:S(2)}) async-start(bf16[32,16,2,256]{3,2,1,0:T(2,128)(2,1)} %bitcast.1), calls=%async_computation | async-start | bytes 1048576 | tf_op jit(solution)/shard_map/all_to_all | solution.py:183

commit v14 on v12

--- a/solution.py
+++ b/solution.py
@@ -49,13 +49,21 @@
     return jnp.dot(lhs, second_w, preferred_element_type=jnp.float32)
 
 
-def regroup_kernel(stem_ref, weight_ref, second_ref, out_ref, lhs_ref):
+def regroup_kernel(stem_ref, weight_ref, second_ref, out_ref, real_ref, imag_ref):
     block_count, rows, _ = stem_ref.shape
     q_local = weight_ref.shape[2] // 64
     t_local = 16
     n_mode = rows // t_local
     lane = lax.broadcasted_iota(jnp.int32, (t_local, 128), 1)
     low = lane < 64
+    imag_lane = (lane // 16) % 2 == 1
+
+    def store(row, col, tile):
+        real_ref[row:row + t_local, col:col + 128] = jnp.where(imag_lane, -tile, tile)
+        imag_ref[row:row + t_local, col:col + 128] = jnp.where(
+            imag_lane, pltpu.roll(tile, 16, 1), pltpu.roll(tile, 112, 1)
+        )
+
     for b in range(block_count):
         product = jnp.dot(
             stem_ref[b], weight_ref[b], preferred_element_type=jnp.float32
@@ -67,13 +75,11 @@
             for qp in range(q_local // 2):
                 first = upper[:, qp * 128:(qp + 1) * 128]
                 second = lower[:, qp * 128:(qp + 1) * 128]
-                even = jnp.where(low, first, pltpu.roll(second, 64, 1))
-                odd = jnp.where(low, pltpu.roll(first, 64, 1), second)
-                lhs_ref[(2 * qp) * t_local:(2 * qp + 1) * t_local, col:col + 128] = even
-                lhs_ref[(2 * qp + 1) * t_local:(2 * qp + 2) * t_local, col:col + 128] = odd
-    lhs = lhs_ref[...]
-    for part in range(second_ref.shape[0]):
-        result = jnp.dot(lhs, second_ref[part], preferred_element_type=jnp.float32)
+                store((2 * qp) * t_local, col, jnp.where(low, first, pltpu.roll(second, 64, 1)))
+                store((2 * qp + 1) * t_local, col, jnp.where(low, pltpu.roll(first, 64, 1), second))
+    weights = second_ref[...]
+    for part, lhs_ref in enumerate((real_ref, imag_ref)):
+        result = jnp.dot(lhs_ref[...], weights, preferred_element_type=jnp.float32)
         for q in range(q_local):
             out_ref[:, q, part, :] = result[q * t_local:(q + 1) * t_local]
 
@@ -83,22 +89,22 @@
     n_mode = rows // t_local
     lhs_shape = (q_local * t_local, block_count * n_mode * 64)
     out_shape = jax.ShapeDtypeStruct(
-        (t_local, q_local, second_w.shape[0], second_w.shape[2]), jnp.float32
+        (t_local, q_local, 2, second_w.shape[1]), jnp.float32
     )
     flops = 2 * block_count * rows * first_w.shape[1] * first_w.shape[2]
-    flops += 2 * lhs_shape[0] * lhs_shape[1] * second_w.shape[0] * second_w.shape[2]
+    flops += 2 * 2 * lhs_shape[0] * lhs_shape[1] * second_w.shape[1]
     return pl.pallas_call(
         regroup_kernel,
         out_shape=out_shape,
         in_specs=[pl.BlockSpec(memory_space=pltpu.VMEM)] * 3,
         out_specs=pl.BlockSpec(memory_space=pltpu.VMEM),
-        scratch_shapes=[pltpu.VMEM(lhs_shape, jnp.bfloat16)],
+        scratch_shapes=[pltpu.VMEM(lhs_shape, jnp.bfloat16)] * 2,
         compiler_params=pltpu.CompilerParams(vmem_limit_bytes=16 * 1024 * 1024),
         cost_estimate=pl.CostEstimate(
             flops=flops,
             transcendentals=0,
             bytes_accessed=2 * (stem_rows.size + first_w.size + second_w.size)
-            + 4 * lhs_shape[0] * second_w.shape[0] * second_w.shape[2],
+            + 4 * lhs_shape[0] * 2 * second_w.shape[1],
         ),
     )(stem_rows, first_w, second_w)
 
@@ -120,12 +126,8 @@
     if group == 64 and t_local == 16 and n_mode % 2 == 0 and q_local % 2 == 0:
         second = jnp.take(w2_table, second_ids.reshape(-1), axis=0)
         second = second.reshape(block_count, n_cuts, 2, n_mode, a_count, out_width)
-        real_two, imag_two = second[:, :, 0], second[:, :, 1]
-        second_w = jnp.stack(
-            [jnp.stack([real_two, imag_two]), jnp.stack([-imag_two, real_two])]
-        )
-        second_w = jnp.transpose(second_w, (1, 2, 4, 3, 0, 5, 6)).reshape(
-            2, block_count * n_mode * group, out_width
+        second_w = jnp.transpose(second, (0, 3, 1, 2, 4, 5)).reshape(
+            block_count * n_mode * group, out_width
         )
         return regroup(stem_rows, jnp.swapaxes(first_w, 1, 2), second_w, q_local, t_local)
     else:

time: 30.6 us -> 30.3 us (level)
  other arithmetic: 4.66 us -> 2.91 us
  waiting for transfers between devices: 0.01 us -> 0.89 us
    another operation x2 -> x0, other arithmetic: 1.72 us -> none  [stacked_part(): jnp.stack([jnp.stack([real_two, imag_two]), jnp.stack([-imag_two, real_tw...]
    all_to_all x1, waiting for transfers between devices: 0.01 us -> 0.89 us  [on_device(): stem_rows = lax.all_to_all(payload, ('cuts', 'mode'), 0, 0, tiled=True)]
    reshape x2, local copies, waits for them, and re-layouts: 2.98 us -> 3.76 us  [stacked_part(): jnp.transpose(first_w, (2, 4, 3, 1, 5, 0, 6))]
    unnamed x8, local copies, waits for them, and re-layouts: 1.6 us -> 1.24 us
  transfers between devices with their start and end apart: 2 -> 2, of which waited for: 0 -> 1; matrix products, arithmetic and copies ran while one was open for 59% -> 56% of each run, Pallas kernels for 0% -> 0%
where the time goes in v14:
time: 30.3 us; the launch traced here: 29.8 us
  local copies, waits for them, and re-layouts  14.3 us (47%)
  starting transfers between devices  8 us (26%)
  other arithmetic  2.91 us (10%)
  Pallas kernels  2.73 us (9%)
  waiting for transfers between devices  0.89 us (3%)
  matrix products  0.81 us (3%)
    all_to_all x1, starting transfers between devices, on_device(): stem_rows = lax.all_to_all(payload, ('cuts', 'mode'), 0, 0, tiled=True)  5.06 us
    reshape x2, local copies, waits for them, and re-layouts, stacked_part(): jnp.transpose(first_w, (2, 4, 3, 1, 5, 0, 6))  3.76 us
    gather x1, local copies, waits for them, and re-layouts, stacked_part(): second = jnp.take(w2_table, second_ids.reshape(-1), axis=0)  3.22 us
    ppermute x1, starting transfers between devices, gather_over_cuts(): current = lax.ppermute(current, 'cuts', ring)  2.94 us
    pallas_call x1, Pallas kernels, regroup(): pl.pallas_call(regroup_kernel, out_shape=out_shape, in_specs=[pl.BlockSpe...  2.73 us
    broadcast_in_dim x2, local copies, waits for them, and re-layouts, on_device(): payload = jnp.broadcast_to(pieces, (n_cuts, n_mode, t_local, 2 * width))  1.98 us
    select_n x2, other arithmetic, stacked_part(): second = jnp.take(w2_table, second_ids.reshape(-1), axis=0)  1.4 us
    gather x1, local copies, waits for them, and re-layouts, stacked_part(): picked = jnp.take(first_t, first_ids.reshape(-1), axis=0)  1.36 us
  transfers between devices with their start and end apart: 2, of which 1 were waited for; matrix products, arithmetic and copies ran while one was open for 56% of the time, Pallas kernels for 0%

profile of v14, /device:TPU:0, one launch (start us, length us, event | category | flops | bytes accessed | tf_op | source)
XLA Modules:
  0.0 29.8 jit_solution(556699463764278747)
XLA Ops:
  0.0 2.9 %collective-permute-start = (s32[2,2]{1,0:T(2,128)}, s32[2,2]{1,0:T(2,128)S(1)}, u32[]{:S(2)}, u32[]{:S(2)}) collective-permute-start(s32[2,2]{1,0:T(2,128)} %bitcast.48), channel_id=1, source_target_pairs={{0,16},{16,0},{1,17},{17,1},{2,18},{18,2},{3,19},{19,3},{4,20},{20... | collective-permute-start | bytes 56 | tf_op jit(solution)/shard_map/ppermute | solution.py:14
  2.9 1.1 %broadcast_in_dim.34 = bf16[16,16,512]{2,1,0:T(8,128)(2,1)S(1)} reshape(bf16[1,256,2,256]{3,2,1,0:T(2,128)(2,1)} %param.5) | data formatting | bytes 524288 | tf_op jit(solution)/shard_map/broadcast_in_dim | solution.py:175
  4.1 0.9 %broadcast_in_dim.35 = bf16[2,16,16,512]{3,2,1,0:T(8,128)(2,1)} broadcast(bf16[16,16,512]{2,1,0:T(8,128)(2,1)S(1)} %broadcast_in_dim.34), dimensions={1,2,3} | broadcast | bytes 786432 | tf_op jit(solution)/shard_map/broadcast_in_dim | solution.py:175
  4.9 5.1 %all-to-all-start = ((bf16[32,16,512]{2,1,0:T(8,128)(2,1)}), bf16[32,16,512]{2,1,0:T(8,128)(2,1)}, u32[]{:S(2)}, u32[]{:S(2)}) async-start(bf16[32,16,512]{2,1,0:T(8,128)(2,1)} %bitcast), calls=%async_computation | async-start | bytes 1048576 | tf_op jit(solution)/shard_map/all_to_all | solution.py:177
  10.4 0.8 %fusion = bf16[8,2,128,256]{3,2,1,0:T(8,128)(2,1)S(1)} fusion(bf16[8,2,256,256]{3,2,1,0:T(8,128)(2,1)S(1)} %copy-done, s32[128]{0:T(128)S(1)} %eq.17), kind=kOutput, calls=%fused_computation.4 | convolution fusion | flops 268992512 | bytes 3146240 | tf_op jit(solution)/shard_map/nj,spkj->spnk/dot_general | solution.py:198
  11.2 0.6 %gather_fusion = s32[2,2,2]{2,1,0:T(2,128)S(1)} fusion(s32[2,2,2]{2,1,0:T(2,128)S(1)} %pad_add_fusion, s32[1024]{0:T(1024)S(1)} %pad_clamp_fusion.2), kind=kCustom, calls=%fused_computation | custom fusion | bytes 72 | tf_op jit(solution)/shard_map/jit(_take)/gather | solution.py:19
  11.9 0.2 slice_reduce_fusion
  12.1 0.1 copy.15
  12.3 0.1 copy.13
  12.4 1.4 %gather_fusion.1 = bf16[4,2,128,256]{3,2,1,0:T(8,128)(2,1)} fusion(bf16[8,2,128,256]{3,2,1,0:T(8,128)(2,1)S(1)} %fusion, s32[1024]{0:T(1024)S(1)} %pad_clamp_fusion.1), kind=kCustom, calls=%fused_computation.1 | custom fusion | bytes 1048592 | tf_op jit(solution)/shard_map/jit(_take)/gather | solution.py:117
  13.8 1.2 %copy_select_fusion.1 = bf16[2,2,2,8,16,256]{5,4,3,1,0,2:T(8,128)(2,1)S(1)} fusion(bf16[2,2,2,8,16,256]{5,4,3,2,1,0:T(8,128)(2,1)} %bitcast.45, pred[2,2]{1,0:T(4,128)(4,1)S(1)} %copy.13), kind=kLoop, calls=%fused_computation.9 | loop fusion | flops 262144 | bytes 1048580 | tf_op jit(solution)/shard_map/jit(_take)/select_n | solution.py:117
  15.0 0.1 maximum_bitcast_fusion.1
  15.1 0.1 maximum_bitcast_fusion
  15.2 1.1 %copy.17 = bf16[2,8,2,2,16,2,256]{6,5,4,3,2,1,0:T(2,128)(2,1)S(1)} copy(bf16[2,8,2,2,16,2,256]{6,4,1,2,0,3,5:T(8,128)(2,1)S(1)} %maximum_bitcast_fusion) | data formatting | bytes 2097152 | tf_op jit(solution)/shard_map/transpose | solution.py:123
  16.3 1.5 %reshape.165 = bf16[2,512,512]{2,1,0:T(8,128)(2,1)} reshape(bf16[2,8,2,2,16,2,256]{6,5,4,3,2,1,0:T(2,128)(2,1)S(1)} %copy.17) | data formatting | bytes 2097152 | tf_op jit(solution)/shard_map/reshape | solution.py:123
  17.8 2.3 %copy.18 = bf16[2,512,512]{1,2,0:T(8,128)(2,1)} copy(bf16[2,512,512]{2,1,0:T(8,128)(2,1)} %reshape.165) | data formatting | bytes 2097152 | tf_op jit(solution)/shard_map/reshape | solution.py:123
  20.1 0.1 copy.19
  20.2 0.1 copy.20
  20.3 0.1 reshape.166
  20.4 3.2 %gather_fusion.2 = bf16[4,2,256,256]{3,2,1,0:T(8,128)(2,1)} fusion(bf16[8,2,256,256]{3,2,1,0:T(8,128)(2,1)} %param.7, s32[1024]{0:T(1024)S(1)} %pad_clamp_fusion), kind=kCustom, calls=%fused_computation.2 | custom fusion | bytes 2097168 | tf_op jit(solution)/shard_map/jit(_take)/gather | solution.py:127
  23.6 1.4 %copy_select_fusion = bf16[2,2,2,16,16,256]{5,4,2,1,3,0:T(8,128)(2,1)S(1)} fusion(bf16[2,2,2,16,16,256]{5,4,3,2,1,0:T(8,128)(2,1)} %bitcast.44, pred[2,2]{1,0:T(4,128)(4,1)S(1)} %copy.19), kind=kLoop, calls=%fused_computation.6 | loop fusion | flops 524288 | bytes 2097156 | tf_op jit(solution)/shard_map/jit(_take)/select_n | solution.py:127
  25.0 0.9 %all-to-all-done = bf16[32,16,512]{2,1,0:T(8,128)(2,1)} async-done(((bf16[32,16,512]{2,1,0:T(8,128)(2,1)}), bf16[32,16,512]{2,1,0:T(8,128)(2,1)}, u32[]{:S(2)}, u32[]{:S(2)}) %all-to-all-start) | async-done | bytes 524320 | tf_op jit(solution)/shard_map/all_to_all | solution.py:177
  25.9 1.2 %copy-done.1 = bf16[2,512,512]{1,2,0:T(8,128)(2,1)S(1)} copy-done((bf16[2,512,512]{1,2,0:T(8,128)(2,1)S(1)}, bf16[2,512,512]{1,2,0:T(8,128)(2,1)}, u32[]{:S(2)}) %copy-start.1) | copy-done | bytes 1048600
  27.1 2.7 %shard_map.55 = f32[16,8,2,256]{3,2,1,0:T(2,128)} custom-call(bf16[2,256,512]{2,1,0:T(8,128)(2,1)} %bitcast.1.stem_ref, bf16[2,512,512]{2,1,0:T(8,128)(2,1)S(1)} %bitcast.43, bf16[2048,256]{1,0:T(8,128)(2,1)S(1)} %bitcast.42), custom_call_target="tpu_custom_call" | custom-call | flops 536870912 | bytes 2883584 | tf_op jit(solution)/shard_map/pallas_call | solution.py:96
  (25 shorter events, 0.6 us)
Async XLA Ops:
  0.0 10.4 %copy-start = (bf16[8,2,256,256]{3,2,1,0:T(8,128)(2,1)S(1)}, bf16[8,2,256,256]{3,2,1,0:T(8,128)(2,1)}, u32[]{:S(2)}) copy-start(bf16[8,2,256,256]{3,2,1,0:T(8,128)(2,1)} %param.6) | copy-start | bytes 6291460
  0.0 10.0 %copy-start.2 = (s32[256]{0:T(256)S(1)}, s32[256]{0:T(256)}, u32[]{:S(2)}) copy-start(s32[256]{0:T(256)} %param.9) | copy-start | bytes 3076
  0.0 11.2 %collective-permute-start = (s32[2,2]{1,0:T(2,128)}, s32[2,2]{1,0:T(2,128)S(1)}, u32[]{:S(2)}, u32[]{:S(2)}) collective-permute-start(s32[2,2]{1,0:T(2,128)} %bitcast.48), channel_id=1, source_target_pairs={{0,16},{16,0},{1,17},{17,1},{2,18},{18,2},{3,19},{19,3},{4,20},{20... | collective-permute-start | bytes 56 | tf_op jit(solution)/shard_map/ppermute | solution.py:14
  4.9 6.3 %copy-start.3 = (s32[1,2,2]{2,1,0:T(2,128)S(1)}, s32[1,2,2]{2,1,0:T(2,128)}, u32[]{:S(2)}) copy-start(s32[1,2,2]{2,1,0:T(2,128)} %param.8) | copy-start | bytes 52
  4.9 20.9 %all-to-all-start = ((bf16[32,16,512]{2,1,0:T(8,128)(2,1)}), bf16[32,16,512]{2,1,0:T(8,128)(2,1)}, u32[]{:S(2)}, u32[]{:S(2)}) async-start(bf16[32,16,512]{2,1,0:T(8,128)(2,1)} %bitcast), calls=%async_computation | async-start | bytes 1048576 | tf_op jit(solution)/shard_map/all_to_all | solution.py:177
  25.9 1.2 %copy-start.1 = (bf16[2,512,512]{1,2,0:T(8,128)(2,1)S(1)}, bf16[2,512,512]{1,2,0:T(8,128)(2,1)}, u32[]{:S(2)}) copy-start(bf16[2,512,512]{1,2,0:T(8,128)(2,1)} %copy.18) | copy-start | bytes 3145732

commit v15 on v14

--- a/solution.py
+++ b/solution.py
@@ -99,7 +99,6 @@
         in_specs=[pl.BlockSpec(memory_space=pltpu.VMEM)] * 3,
         out_specs=pl.BlockSpec(memory_space=pltpu.VMEM),
         scratch_shapes=[pltpu.VMEM(lhs_shape, jnp.bfloat16)] * 2,
-        compiler_params=pltpu.CompilerParams(vmem_limit_bytes=16 * 1024 * 1024),
         cost_estimate=pl.CostEstimate(
             flops=flops,
             transcendentals=0,

time: 30.3 us -> 29.6 us (0.977)
  local copies, waits for them, and re-layouts: 14.3 us -> 12.1 us
  waiting for transfers between devices: 0.89 us -> 2.11 us
  Pallas kernels: 2.73 us -> 3.39 us
    unnamed x8 -> x6, local copies, waits for them, and re-layouts: 1.24 us -> 0.01 us
    all_to_all x1, waiting for transfers between devices: 0.89 us -> 2.11 us  [on_device(): stem_rows = lax.all_to_all(payload, ('cuts', 'mode'), 0, 0, tiled=True)]
    gather x1, local copies, waits for them, and re-layouts: 3.22 us -> 2.2 us  [stacked_part(): second = jnp.take(w2_table, second_ids.reshape(-1), axis=0)]
    pallas_call x1, Pallas kernels: 2.73 us -> 3.39 us  [regroup(): pl.pallas_call(regroup_kernel, out_shape=out_shape, in_specs=[pl.BlockSpe...]
  transfers between devices with their start and end apart: 2 -> 2, of which waited for: 1 -> 1; matrix products, arithmetic and copies ran while one was open for 56% -> 53% of each run, Pallas kernels for 0% -> 0%
where the time goes in v15:
time: 29.6 us; the launch traced here: 29.3 us
  local copies, waits for them, and re-layouts  12.1 us (41%)
  starting transfers between devices  8 us (27%)
  Pallas kernels  3.39 us (11%)
  other arithmetic  2.69 us (9%)
  waiting for transfers between devices  2.11 us (7%)
  matrix products  0.81 us (3%)
    all_to_all x1, starting transfers between devices, on_device(): stem_rows = lax.all_to_all(payload, ('cuts', 'mode'), 0, 0, tiled=True)  5.06 us
    reshape x2, local copies, waits for them, and re-layouts, stacked_part(): jnp.transpose(first_w, (2, 4, 3, 1, 5, 0, 6))  3.76 us
    pallas_call x1, Pallas kernels, regroup(): pl.pallas_call(regroup_kernel, out_shape=out_shape, in_specs=[pl.BlockSpe...  3.39 us
    ppermute x1, starting transfers between devices, gather_over_cuts(): current = lax.ppermute(current, 'cuts', ring)  2.94 us
    gather x1, local copies, waits for them, and re-layouts, stacked_part(): second = jnp.take(w2_table, second_ids.reshape(-1), axis=0)  2.2 us
    all_to_all x1, waiting for transfers between devices, on_device(): stem_rows = lax.all_to_all(payload, ('cuts', 'mode'), 0, 0, tiled=True)  2.11 us
    broadcast_in_dim x2, local copies, waits for them, and re-layouts, on_device(): payload = jnp.broadcast_to(pieces, (n_cuts, n_mode, t_local, 2 * width))  1.98 us
    gather x1, local copies, waits for them, and re-layouts, stacked_part(): picked = jnp.take(first_t, first_ids.reshape(-1), axis=0)  1.38 us
  transfers between devices with their start and end apart: 2, of which 1 were waited for; matrix products, arithmetic and copies ran while one was open for 53% of the time, Pallas kernels for 0%

profile of v15, /device:TPU:0, one launch (start us, length us, event | category | flops | bytes accessed | tf_op | source)
XLA Modules:
  0.0 29.3 jit_solution(3218679721859232181)
XLA Ops:
  0.0 2.9 %collective-permute-start = (s32[2,2]{1,0:T(2,128)}, s32[2,2]{1,0:T(2,128)S(1)}, u32[]{:S(2)}, u32[]{:S(2)}) collective-permute-start(s32[2,2]{1,0:T(2,128)} %bitcast.48), channel_id=1, source_target_pairs={{0,16},{16,0},{1,17},{17,1},{2,18},{18,2},{3,19},{19,3},{4,20},{20... | collective-permute-start | bytes 56 | tf_op jit(solution)/shard_map/ppermute | solution.py:14
  2.9 1.1 %broadcast_in_dim.34 = bf16[16,16,512]{2,1,0:T(8,128)(2,1)S(1)} reshape(bf16[1,256,2,256]{3,2,1,0:T(2,128)(2,1)} %param.5) | data formatting | bytes 524288 | tf_op jit(solution)/shard_map/broadcast_in_dim | solution.py:174
  4.1 0.9 %broadcast_in_dim.35 = bf16[2,16,16,512]{3,2,1,0:T(8,128)(2,1)} broadcast(bf16[16,16,512]{2,1,0:T(8,128)(2,1)S(1)} %broadcast_in_dim.34), dimensions={1,2,3} | broadcast | bytes 786432 | tf_op jit(solution)/shard_map/broadcast_in_dim | solution.py:174
  4.9 5.1 %all-to-all-start = ((bf16[32,16,512]{2,1,0:T(8,128)(2,1)}), bf16[32,16,512]{2,1,0:T(8,128)(2,1)}, u32[]{:S(2)}, u32[]{:S(2)}) async-start(bf16[32,16,512]{2,1,0:T(8,128)(2,1)} %bitcast), calls=%async_computation | async-start | bytes 1048576 | tf_op jit(solution)/shard_map/all_to_all | solution.py:176
  10.4 0.8 %fusion = bf16[8,2,128,256]{3,2,1,0:T(8,128)(2,1)S(1)} fusion(bf16[8,2,256,256]{3,2,1,0:T(8,128)(2,1)S(1)} %copy-done, s32[128]{0:T(128)S(1)} %eq.17), kind=kOutput, calls=%fused_computation.4 | convolution fusion | flops 268992512 | bytes 3146240 | tf_op jit(solution)/shard_map/nj,spkj->spnk/dot_general | solution.py:197
  11.2 0.6 %gather_fusion = s32[2,2,2]{2,1,0:T(2,128)S(1)} fusion(s32[2,2,2]{2,1,0:T(2,128)S(1)} %pad_add_fusion, s32[1024]{0:T(1024)S(1)} %pad_clamp_fusion.2), kind=kCustom, calls=%fused_computation | custom fusion | bytes 72 | tf_op jit(solution)/shard_map/jit(_take)/gather | solution.py:19
  11.9 0.2 slice_reduce_fusion
  12.1 0.1 copy.15
  12.2 0.1 reshape.164
  12.3 0.1 copy.13
  12.4 1.4 %gather_fusion.1 = bf16[4,2,128,256]{3,2,1,0:T(8,128)(2,1)} fusion(bf16[8,2,128,256]{3,2,1,0:T(8,128)(2,1)S(1)} %fusion, s32[1024]{0:T(1024)S(1)} %pad_clamp_fusion.1), kind=kCustom, calls=%fused_computation.1 | custom fusion | bytes 1048592 | tf_op jit(solution)/shard_map/jit(_take)/gather | solution.py:116
  13.8 1.2 %copy_select_fusion.1 = bf16[2,2,2,8,16,256]{5,4,3,1,0,2:T(8,128)(2,1)S(1)} fusion(bf16[2,2,2,8,16,256]{5,4,3,2,1,0:T(8,128)(2,1)} %bitcast.45, pred[2,2]{1,0:T(4,128)(4,1)S(1)} %copy.13), kind=kLoop, calls=%fused_computation.9 | loop fusion | flops 262144 | bytes 1048580 | tf_op jit(solution)/shard_map/jit(_take)/select_n | solution.py:116
  15.0 0.1 maximum_bitcast_fusion.1
  15.1 0.1 maximum_bitcast_fusion
  15.2 1.1 %copy.17 = bf16[2,8,2,2,16,2,256]{6,5,4,3,2,1,0:T(2,128)(2,1)S(1)} copy(bf16[2,8,2,2,16,2,256]{6,4,1,2,0,3,5:T(8,128)(2,1)S(1)} %maximum_bitcast_fusion) | data formatting | bytes 2097152 | tf_op jit(solution)/shard_map/transpose | solution.py:122
  16.3 1.5 %reshape.165 = bf16[2,512,512]{2,1,0:T(8,128)(2,1)} reshape(bf16[2,8,2,2,16,2,256]{6,5,4,3,2,1,0:T(2,128)(2,1)S(1)} %copy.17) | data formatting | bytes 2097152 | tf_op jit(solution)/shard_map/reshape | solution.py:122
  17.8 2.3 %copy.18 = bf16[2,512,512]{1,2,0:T(8,128)(2,1)} copy(bf16[2,512,512]{2,1,0:T(8,128)(2,1)} %reshape.165) | data formatting | bytes 2097152 | tf_op jit(solution)/shard_map/reshape | solution.py:122
  20.1 0.1 copy.19
  20.2 0.1 copy.20
  20.3 0.1 reshape.166
  20.4 2.2 %gather_fusion.2 = bf16[4,2,256,256]{3,2,1,0:T(8,128)(2,1)S(1)} fusion(bf16[8,2,256,256]{3,2,1,0:T(8,128)(2,1)} %param.7, s32[1024]{0:T(1024)S(1)} %pad_clamp_fusion), kind=kCustom, calls=%fused_computation.2 | custom fusion | bytes 2097168 | tf_op jit(solution)/shard_map/jit(_take)/gather | solution.py:126
  22.6 1.2 %copy_select_fusion = bf16[2,2,2,16,16,256]{5,4,2,1,3,0:T(8,128)(2,1)} fusion(bf16[2,2,2,16,16,256]{5,4,3,2,1,0:T(8,128)(2,1)S(1)} %bitcast.42, pred[2,2]{1,0:T(4,128)(4,1)S(1)} %copy.19), kind=kLoop, calls=%fused_computation.6 | loop fusion | flops 524288 | bytes 2097156 | tf_op jit(solution)/shard_map/jit(_take)/select_n | solution.py:126
  23.8 2.1 %all-to-all-done = bf16[32,16,512]{2,1,0:T(8,128)(2,1)} async-done(((bf16[32,16,512]{2,1,0:T(8,128)(2,1)}), bf16[32,16,512]{2,1,0:T(8,128)(2,1)}, u32[]{:S(2)}, u32[]{:S(2)}) %all-to-all-start) | async-done | bytes 524320 | tf_op jit(solution)/shard_map/all_to_all | solution.py:176
  25.9 3.4 %shard_map.55 = f32[16,8,2,256]{3,2,1,0:T(2,128)} custom-call(bf16[2,256,512]{2,1,0:T(8,128)(2,1)} %bitcast.1.stem_ref, bf16[2,512,512]{2,1,0:T(8,128)(2,1)} %bitcast.44, bf16[2048,256]{1,0:T(8,128)(2,1)} %bitcast.43), custom_call_target="tpu_custom_call" | custom-call | flops 536870912 | bytes 2883584 | tf_op jit(solution)/shard_map/pallas_call | solution.py:96
  (23 shorter events, 0.5 us)
Async XLA Ops:
  0.0 10.4 %copy-start = (bf16[8,2,256,256]{3,2,1,0:T(8,128)(2,1)S(1)}, bf16[8,2,256,256]{3,2,1,0:T(8,128)(2,1)}, u32[]{:S(2)}) copy-start(bf16[8,2,256,256]{3,2,1,0:T(8,128)(2,1)} %param.6) | copy-start | bytes 6291460
  0.0 10.0 %copy-start.1 = (s32[256]{0:T(256)S(1)}, s32[256]{0:T(256)}, u32[]{:S(2)}) copy-start(s32[256]{0:T(256)} %param.9) | copy-start | bytes 3076
  0.0 11.2 %collective-permute-start = (s32[2,2]{1,0:T(2,128)}, s32[2,2]{1,0:T(2,128)S(1)}, u32[]{:S(2)}, u32[]{:S(2)}) collective-permute-start(s32[2,2]{1,0:T(2,128)} %bitcast.48), channel_id=1, source_target_pairs={{0,16},{16,0},{1,17},{17,1},{2,18},{18,2},{3,19},{19,3},{4,20},{20... | collective-permute-start | bytes 56 | tf_op jit(solution)/shard_map/ppermute | solution.py:14
  4.9 6.3 %copy-start.2 = (s32[1,2,2]{2,1,0:T(2,128)S(1)}, s32[1,2,2]{2,1,0:T(2,128)}, u32[]{:S(2)}) copy-start(s32[1,2,2]{2,1,0:T(2,128)} %param.8) | copy-start | bytes 52
  4.9 20.9 %all-to-all-start = ((bf16[32,16,512]{2,1,0:T(8,128)(2,1)}), bf16[32,16,512]{2,1,0:T(8,128)(2,1)}, u32[]{:S(2)}, u32[]{:S(2)}) async-start(bf16[32,16,512]{2,1,0:T(8,128)(2,1)} %bitcast), calls=%async_computation | async-start | bytes 1048576 | tf_op jit(solution)/shard_map/all_to_all | solution.py:176

commit v16 on v15

--- a/solution.py
+++ b/solution.py
@@ -49,7 +49,7 @@
     return jnp.dot(lhs, second_w, preferred_element_type=jnp.float32)
 
 
-def regroup_kernel(stem_ref, weight_ref, second_ref, out_ref, real_ref, imag_ref):
+def regroup_kernel(stem_ref, weight_ref, second_ref, out_ref, lhs_ref):
     block_count, rows, _ = stem_ref.shape
     q_local = weight_ref.shape[2] // 64
     t_local = 16
@@ -58,9 +58,11 @@
     low = lane < 64
     imag_lane = (lane // 16) % 2 == 1
 
+    half = q_local * t_local
+
     def store(row, col, tile):
-        real_ref[row:row + t_local, col:col + 128] = jnp.where(imag_lane, -tile, tile)
-        imag_ref[row:row + t_local, col:col + 128] = jnp.where(
+        lhs_ref[row:row + t_local, col:col + 128] = jnp.where(imag_lane, -tile, tile)
+        lhs_ref[half + row:half + row + t_local, col:col + 128] = jnp.where(
             imag_lane, pltpu.roll(tile, 16, 1), pltpu.roll(tile, 112, 1)
         )
 
@@ -77,11 +79,11 @@
                 second = lower[:, qp * 128:(qp + 1) * 128]
                 store((2 * qp) * t_local, col, jnp.where(low, first, pltpu.roll(second, 64, 1)))
                 store((2 * qp + 1) * t_local, col, jnp.where(low, pltpu.roll(first, 64, 1), second))
-    weights = second_ref[...]
-    for part, lhs_ref in enumerate((real_ref, imag_ref)):
-        result = jnp.dot(lhs_ref[...], weights, preferred_element_type=jnp.float32)
+    result = jnp.dot(lhs_ref[...], second_ref[...], preferred_element_type=jnp.float32)
+    for part in range(2):
         for q in range(q_local):
-            out_ref[:, q, part, :] = result[q * t_local:(q + 1) * t_local]
+            row = part * half + q * t_local
+            out_ref[:, q, part, :] = result[row:row + t_local]
 
 
 def regroup(stem_rows, first_w, second_w, q_local, t_local):
@@ -98,7 +100,7 @@
         out_shape=out_shape,
         in_specs=[pl.BlockSpec(memory_space=pltpu.VMEM)] * 3,
         out_specs=pl.BlockSpec(memory_space=pltpu.VMEM),
-        scratch_shapes=[pltpu.VMEM(lhs_shape, jnp.bfloat16)] * 2,
+        scratch_shapes=[pltpu.VMEM((2 * lhs_shape[0], lhs_shape[1]), jnp.bfloat16)],
         cost_estimate=pl.CostEstimate(
             flops=flops,
             transcendentals=0,

time: 29.6 us -> 30.1 us (1.017)
  Pallas kernels: 3.39 us -> 3.9 us
    pallas_call x1, Pallas kernels: 3.39 us -> 3.9 us  [regroup(): pl.pallas_call(regroup_kernel, out_shape=out_shape, in_specs=[pl.BlockSpe...]
  transfers between devices with their start and end apart: 2 -> 2, of which waited for: 1 -> 1; matrix products, arithmetic and copies ran while one was open for 53% -> 52% of each run, Pallas kernels for 0% -> 0%
where the time goes in v16:
time: 30.1 us; the launch traced here: 29.8 us
  local copies, waits for them, and re-layouts  12.1 us (40%)
  starting transfers between devices  8 us (27%)
  Pallas kernels  3.9 us (13%)
  other arithmetic  2.69 us (9%)
  waiting for transfers between devices  2.11 us (7%)
  matrix products  0.81 us (3%)
    all_to_all x1, starting transfers between devices, on_device(): stem_rows = lax.all_to_all(payload, ('cuts', 'mode'), 0, 0, tiled=True)  5.06 us
    pallas_call x1, Pallas kernels, regroup(): pl.pallas_call(regroup_kernel, out_shape=out_shape, in_specs=[pl.BlockSpe...  3.9 us
    reshape x2, local copies, waits for them, and re-layouts, stacked_part(): jnp.transpose(first_w, (2, 4, 3, 1, 5, 0, 6))  3.76 us
    ppermute x1, starting transfers between devices, gather_over_cuts(): current = lax.ppermute(current, 'cuts', ring)  2.94 us
    gather x1, local copies, waits for them, and re-layouts, stacked_part(): second = jnp.take(w2_table, second_ids.reshape(-1), axis=0)  2.2 us
    all_to_all x1, waiting for transfers between devices, on_device(): stem_rows = lax.all_to_all(payload, ('cuts', 'mode'), 0, 0, tiled=True)  2.11 us
    broadcast_in_dim x2, local copies, waits for them, and re-layouts, on_device(): payload = jnp.broadcast_to(pieces, (n_cuts, n_mode, t_local, 2 * width))  1.98 us
    gather x1, local copies, waits for them, and re-layouts, stacked_part(): picked = jnp.take(first_t, first_ids.reshape(-1), axis=0)  1.38 us
  transfers between devices with their start and end apart: 2, of which 1 were waited for; matrix products, arithmetic and copies ran while one was open for 52% of the time, Pallas kernels for 0%

profile of v16, /device:TPU:0, one launch (start us, length us, event | category | flops | bytes accessed | tf_op | source)
XLA Modules:
  0.0 29.8 jit_solution(9676237478079613678)
XLA Ops:
  0.0 2.9 %collective-permute-start = (s32[2,2]{1,0:T(2,128)}, s32[2,2]{1,0:T(2,128)S(1)}, u32[]{:S(2)}, u32[]{:S(2)}) collective-permute-start(s32[2,2]{1,0:T(2,128)} %bitcast.48), channel_id=1, source_target_pairs={{0,16},{16,0},{1,17},{17,1},{2,18},{18,2},{3,19},{19,3},{4,20},{20... | collective-permute-start | bytes 56 | tf_op jit(solution)/shard_map/ppermute | solution.py:14
  2.9 1.1 %broadcast_in_dim.34 = bf16[16,16,512]{2,1,0:T(8,128)(2,1)S(1)} reshape(bf16[1,256,2,256]{3,2,1,0:T(2,128)(2,1)} %param.5) | data formatting | bytes 524288 | tf_op jit(solution)/shard_map/broadcast_in_dim | solution.py:176
  4.1 0.9 %broadcast_in_dim.35 = bf16[2,16,16,512]{3,2,1,0:T(8,128)(2,1)} broadcast(bf16[16,16,512]{2,1,0:T(8,128)(2,1)S(1)} %broadcast_in_dim.34), dimensions={1,2,3} | broadcast | bytes 786432 | tf_op jit(solution)/shard_map/broadcast_in_dim | solution.py:176
  4.9 5.1 %all-to-all-start = ((bf16[32,16,512]{2,1,0:T(8,128)(2,1)}), bf16[32,16,512]{2,1,0:T(8,128)(2,1)}, u32[]{:S(2)}, u32[]{:S(2)}) async-start(bf16[32,16,512]{2,1,0:T(8,128)(2,1)} %bitcast), calls=%async_computation | async-start | bytes 1048576 | tf_op jit(solution)/shard_map/all_to_all | solution.py:178
  10.4 0.8 %fusion = bf16[8,2,128,256]{3,2,1,0:T(8,128)(2,1)S(1)} fusion(bf16[8,2,256,256]{3,2,1,0:T(8,128)(2,1)S(1)} %copy-done, s32[128]{0:T(128)S(1)} %eq.17), kind=kOutput, calls=%fused_computation.4 | convolution fusion | flops 268992512 | bytes 3146240 | tf_op jit(solution)/shard_map/nj,spkj->spnk/dot_general | solution.py:199
  11.2 0.6 %gather_fusion = s32[2,2,2]{2,1,0:T(2,128)S(1)} fusion(s32[2,2,2]{2,1,0:T(2,128)S(1)} %pad_add_fusion, s32[1024]{0:T(1024)S(1)} %pad_clamp_fusion.2), kind=kCustom, calls=%fused_computation | custom fusion | bytes 72 | tf_op jit(solution)/shard_map/jit(_take)/gather | solution.py:19
  11.9 0.2 slice_reduce_fusion
  12.1 0.1 copy.15
  12.2 0.1 reshape.164
  12.3 0.1 copy.13
  12.4 1.4 %gather_fusion.1 = bf16[4,2,128,256]{3,2,1,0:T(8,128)(2,1)} fusion(bf16[8,2,128,256]{3,2,1,0:T(8,128)(2,1)S(1)} %fusion, s32[1024]{0:T(1024)S(1)} %pad_clamp_fusion.1), kind=kCustom, calls=%fused_computation.1 | custom fusion | bytes 1048592 | tf_op jit(solution)/shard_map/jit(_take)/gather | solution.py:118
  13.8 1.2 %copy_select_fusion.1 = bf16[2,2,2,8,16,256]{5,4,3,1,0,2:T(8,128)(2,1)S(1)} fusion(bf16[2,2,2,8,16,256]{5,4,3,2,1,0:T(8,128)(2,1)} %bitcast.45, pred[2,2]{1,0:T(4,128)(4,1)S(1)} %copy.13), kind=kLoop, calls=%fused_computation.9 | loop fusion | flops 262144 | bytes 1048580 | tf_op jit(solution)/shard_map/jit(_take)/select_n | solution.py:118
  15.0 0.1 maximum_bitcast_fusion.1
  15.1 0.1 maximum_bitcast_fusion
  15.2 1.1 %copy.17 = bf16[2,8,2,2,16,2,256]{6,5,4,3,2,1,0:T(2,128)(2,1)S(1)} copy(bf16[2,8,2,2,16,2,256]{6,4,1,2,0,3,5:T(8,128)(2,1)S(1)} %maximum_bitcast_fusion) | data formatting | bytes 2097152 | tf_op jit(solution)/shard_map/transpose | solution.py:124
  16.3 1.5 %reshape.165 = bf16[2,512,512]{2,1,0:T(8,128)(2,1)} reshape(bf16[2,8,2,2,16,2,256]{6,5,4,3,2,1,0:T(2,128)(2,1)S(1)} %copy.17) | data formatting | bytes 2097152 | tf_op jit(solution)/shard_map/reshape | solution.py:124
  17.8 2.3 %copy.18 = bf16[2,512,512]{1,2,0:T(8,128)(2,1)} copy(bf16[2,512,512]{2,1,0:T(8,128)(2,1)} %reshape.165) | data formatting | bytes 2097152 | tf_op jit(solution)/shard_map/reshape | solution.py:124
  20.1 0.1 copy.19
  20.2 0.1 copy.20
  20.3 0.1 reshape.166
  20.4 2.2 %gather_fusion.2 = bf16[4,2,256,256]{3,2,1,0:T(8,128)(2,1)S(1)} fusion(bf16[8,2,256,256]{3,2,1,0:T(8,128)(2,1)} %param.7, s32[1024]{0:T(1024)S(1)} %pad_clamp_fusion), kind=kCustom, calls=%fused_computation.2 | custom fusion | bytes 2097168 | tf_op jit(solution)/shard_map/jit(_take)/gather | solution.py:128
  22.6 1.2 %copy_select_fusion = bf16[2,2,2,16,16,256]{5,4,2,1,3,0:T(8,128)(2,1)} fusion(bf16[2,2,2,16,16,256]{5,4,3,2,1,0:T(8,128)(2,1)S(1)} %bitcast.42, pred[2,2]{1,0:T(4,128)(4,1)S(1)} %copy.19), kind=kLoop, calls=%fused_computation.6 | loop fusion | flops 524288 | bytes 2097156 | tf_op jit(solution)/shard_map/jit(_take)/select_n | solution.py:128
  23.8 2.1 %all-to-all-done = bf16[32,16,512]{2,1,0:T(8,128)(2,1)} async-done(((bf16[32,16,512]{2,1,0:T(8,128)(2,1)}), bf16[32,16,512]{2,1,0:T(8,128)(2,1)}, u32[]{:S(2)}, u32[]{:S(2)}) %all-to-all-start) | async-done | bytes 524320 | tf_op jit(solution)/shard_map/all_to_all | solution.py:178
  25.9 3.9 %shard_map.55 = f32[16,8,2,256]{3,2,1,0:T(2,128)} custom-call(bf16[2,256,512]{2,1,0:T(8,128)(2,1)} %bitcast.1.stem_ref, bf16[2,512,512]{2,1,0:T(8,128)(2,1)} %bitcast.44, bf16[2048,256]{1,0:T(8,128)(2,1)} %bitcast.43), custom_call_target="tpu_custom_call" | custom-call | flops 536870912 | bytes 2883584 | tf_op jit(solution)/shard_map/pallas_call | solution.py:98
  (23 shorter events, 0.5 us)
Async XLA Ops:
  0.0 10.4 %copy-start = (bf16[8,2,256,256]{3,2,1,0:T(8,128)(2,1)S(1)}, bf16[8,2,256,256]{3,2,1,0:T(8,128)(2,1)}, u32[]{:S(2)}) copy-start(bf16[8,2,256,256]{3,2,1,0:T(8,128)(2,1)} %param.6) | copy-start | bytes 6291460
  0.0 10.0 %copy-start.1 = (s32[256]{0:T(256)S(1)}, s32[256]{0:T(256)}, u32[]{:S(2)}) copy-start(s32[256]{0:T(256)} %param.9) | copy-start | bytes 3076
  0.0 11.2 %collective-permute-start = (s32[2,2]{1,0:T(2,128)}, s32[2,2]{1,0:T(2,128)S(1)}, u32[]{:S(2)}, u32[]{:S(2)}) collective-permute-start(s32[2,2]{1,0:T(2,128)} %bitcast.48), channel_id=1, source_target_pairs={{0,16},{16,0},{1,17},{17,1},{2,18},{18,2},{3,19},{19,3},{4,20},{20... | collective-permute-start | bytes 56 | tf_op jit(solution)/shard_map/ppermute | solution.py:14
  4.9 6.3 %copy-start.2 = (s32[1,2,2]{2,1,0:T(2,128)S(1)}, s32[1,2,2]{2,1,0:T(2,128)}, u32[]{:S(2)}) copy-start(s32[1,2,2]{2,1,0:T(2,128)} %param.8) | copy-start | bytes 52
  4.9 20.9 %all-to-all-start = ((bf16[32,16,512]{2,1,0:T(8,128)(2,1)}), bf16[32,16,512]{2,1,0:T(8,128)(2,1)}, u32[]{:S(2)}, u32[]{:S(2)}) async-start(bf16[32,16,512]{2,1,0:T(8,128)(2,1)} %bitcast), calls=%async_computation | async-start | bytes 1048576 | tf_op jit(solution)/shard_map/all_to_all | solution.py:178

commit v17 on v15

--- a/solution.py
+++ b/solution.py
@@ -47,6 +47,24 @@
         w2_table.reshape(slice_count, 2 * inner, out_width), second_ids, axis=0
     ).reshape(chunk * n_cuts * 2 * inner, out_width)
     return jnp.dot(lhs, second_w, preferred_element_type=jnp.float32)
+
+
+def payload_kernel(stem_ref, out_ref):
+    width = stem_ref.shape[3]
+    for part in range(2):
+        plane = stem_ref[0, :, part, :]
+        for cut in range(out_ref.shape[0]):
+            out_ref[cut, :, part * width:(part + 1) * width] = plane
+
+
+def build_payload(stem_blocks, n_cuts):
+    rows, width = stem_blocks.shape[1], stem_blocks.shape[3]
+    return pl.pallas_call(
+        payload_kernel,
+        out_shape=jax.ShapeDtypeStruct((n_cuts, rows, 2 * width), stem_blocks.dtype),
+        in_specs=[pl.BlockSpec(memory_space=pltpu.VMEM)],
+        out_specs=pl.BlockSpec(memory_space=pltpu.VMEM),
+    )(stem_blocks)
 
 
 def regroup_kernel(stem_ref, weight_ref, second_ref, out_ref, real_ref, imag_ref):
@@ -170,9 +188,7 @@
     me = lax.axis_index("cuts")
     sizes = (n_mode, t_local, n_cuts, a_count, q_local)
 
-    pieces = stem_blocks[0].reshape(1, n_mode, t_local, 2 * width)
-    payload = jnp.broadcast_to(pieces, (n_cuts, n_mode, t_local, 2 * width))
-    payload = payload.reshape(n_cuts * n_mode, t_local, 2 * width)
+    payload = build_payload(stem_blocks, n_cuts).reshape(n_cuts * n_mode, t_local, 2 * width)
     stem_rows = lax.all_to_all(payload, ("cuts", "mode"), 0, 0, tiled=True)
     stem_rows = stem_rows.reshape(block_count, n_mode * t_local, 2 * width)
 

time: 29.6 us -> 30 us (1.014)
  Pallas kernels: 3.39 us -> 5.7 us
  local copies, waits for them, and re-layouts: 12.1 us -> 10.8 us
  waiting for transfers between devices: 2.11 us -> 1.46 us
    pallas_call x0 -> x1, Pallas kernels: none -> 2.31 us  [build_payload(): pl.pallas_call(payload_kernel, out_shape=jax.ShapeDtypeStruct((n_cuts, ro...]
    broadcast_in_dim x2 -> x0, local copies, waits for them, and re-layouts: 1.98 us -> none  [on_device(): payload = jnp.broadcast_to(pieces, (n_cuts, n_mode, t_local, 2 * width))]
    reshape x1, local copies, waits for them, and re-layouts: 0.08 us -> 0.76 us  [on_device(): perm_grid = mode_perm.reshape(a_count, q_count)]
    all_to_all x1, waiting for transfers between devices: 2.11 us -> 1.46 us  [on_device(): stem_rows = lax.all_to_all(payload, ('cuts', 'mode'), 0, 0, tiled=True)]
  transfers between devices with their start and end apart: 2 -> 2, of which waited for: 1 -> 1; matrix products, arithmetic and copies ran while one was open for 53% -> 48% of each run, Pallas kernels for 0% -> 8%
where the time goes in v17:
time: 30 us; the launch traced here: 29.6 us
  local copies, waits for them, and re-layouts  10.8 us (36%)
  starting transfers between devices  8.05 us (27%)
  Pallas kernels  5.7 us (19%)
  other arithmetic  2.69 us (9%)
  waiting for transfers between devices  1.46 us (5%)
  matrix products  0.81 us (3%)
    all_to_all x1, starting transfers between devices, on_device(): stem_rows = lax.all_to_all(payload, ('cuts', 'mode'), 0, 0, tiled=True)  5.11 us
    reshape x2, local copies, waits for them, and re-layouts, stacked_part(): jnp.transpose(first_w, (2, 4, 3, 1, 5, 0, 6))  3.75 us
    pallas_call x1, Pallas kernels, regroup(): pl.pallas_call(regroup_kernel, out_shape=out_shape, in_specs=[pl.BlockSpe...  3.39 us
    ppermute x1, starting transfers between devices, gather_over_cuts(): current = lax.ppermute(current, 'cuts', ring)  2.94 us
    pallas_call x1, Pallas kernels, build_payload(): pl.pallas_call(payload_kernel, out_shape=jax.ShapeDtypeStruct((n_cuts, ro...  2.31 us
    gather x1, local copies, waits for them, and re-layouts, stacked_part(): second = jnp.take(w2_table, second_ids.reshape(-1), axis=0)  2.2 us
    all_to_all x1, waiting for transfers between devices, on_device(): stem_rows = lax.all_to_all(payload, ('cuts', 'mode'), 0, 0, tiled=True)  1.46 us
    gather x1, local copies, waits for them, and re-layouts, stacked_part(): picked = jnp.take(first_t, first_ids.reshape(-1), axis=0)  1.37 us
  transfers between devices with their start and end apart: 2, of which 1 were waited for; matrix products, arithmetic and copies ran while one was open for 48% of the time, Pallas kernels for 8%

profile of v17, /device:TPU:0, one launch (start us, length us, event | category | flops | bytes accessed | tf_op | source)
XLA Modules:
  0.0 29.6 jit_solution(5105925673751991137)
XLA Ops:
  0.0 2.9 %collective-permute-start = (s32[2,2]{1,0:T(2,128)}, s32[2,2]{1,0:T(2,128)S(1)}, u32[]{:S(2)}, u32[]{:S(2)}) collective-permute-start(s32[2,2]{1,0:T(2,128)} %bitcast.49), channel_id=1, source_target_pairs={{0,16},{16,0},{1,17},{17,1},{2,18},{18,2},{3,19},{19,3},{4,20},{20... | collective-permute-start | bytes 56 | tf_op jit(solution)/shard_map/ppermute | solution.py:14
  2.9 2.3 %shard_map.55 = bf16[2,256,512]{2,1,0:T(8,128)(2,1)} custom-call(bf16[1,256,2,256]{3,2,1,0:T(2,128)(2,1)} %stem_ref.1), custom_call_target="tpu_custom_call" | custom-call | tf_op jit(solution)/shard_map/pallas_call | solution.py:62
  5.3 5.1 %all-to-all-start = ((bf16[32,16,512]{2,1,0:T(8,128)(2,1)}), bf16[32,16,512]{2,1,0:T(8,128)(2,1)}, u32[]{:S(2)}, u32[]{:S(2)}) async-start(bf16[32,16,512]{2,1,0:T(8,128)(2,1)} %bitcast.45), calls=%async_computation | async-start | bytes 1048576 | tf_op jit(solution)/shard_map/all_to_all | solution.py:192
  10.4 0.8 %reshape.162 = s32[16,16]{1,0:T(8,128)S(1)} reshape(s32[256]{0:T(256)} %param.9) | data formatting | bytes 2048 | tf_op jit(solution)/shard_map/reshape | solution.py:199
  11.4 0.8 %fusion = bf16[8,2,128,256]{3,2,1,0:T(8,128)(2,1)S(1)} fusion(bf16[8,2,256,256]{3,2,1,0:T(8,128)(2,1)S(1)} %copy-done, s32[128]{0:T(128)S(1)} %eq.17), kind=kOutput, calls=%fused_computation.4 | convolution fusion | flops 268992512 | bytes 3146240 | tf_op jit(solution)/shard_map/nj,spkj->spnk/dot_general | solution.py:213
  12.3 0.6 %gather_fusion = s32[2,2,2]{2,1,0:T(2,128)S(1)} fusion(s32[2,2,2]{2,1,0:T(2,128)S(1)} %pad_add_fusion, s32[1024]{0:T(1024)S(1)} %pad_clamp_fusion.2), kind=kCustom, calls=%fused_computation | custom fusion | bytes 72 | tf_op jit(solution)/shard_map/jit(_take)/gather | solution.py:19
  12.9 0.2 slice_reduce_fusion
  13.1 0.1 copy.15
  13.2 0.1 reshape.163
  13.4 0.1 copy.13
  13.5 1.4 %gather_fusion.1 = bf16[4,2,128,256]{3,2,1,0:T(8,128)(2,1)} fusion(bf16[8,2,128,256]{3,2,1,0:T(8,128)(2,1)S(1)} %fusion, s32[1024]{0:T(1024)S(1)} %pad_clamp_fusion.1), kind=kCustom, calls=%fused_computation.1 | custom fusion | bytes 1048592 | tf_op jit(solution)/shard_map/jit(_take)/gather | solution.py:134
  14.8 1.2 %copy_select_fusion.1 = bf16[2,2,2,8,16,256]{5,4,3,1,0,2:T(8,128)(2,1)S(1)} fusion(bf16[2,2,2,8,16,256]{5,4,3,2,1,0:T(8,128)(2,1)} %bitcast.46, pred[2,2]{1,0:T(4,128)(4,1)S(1)} %copy.13), kind=kLoop, calls=%fused_computation.9 | loop fusion | flops 262144 | bytes 1048580 | tf_op jit(solution)/shard_map/jit(_take)/select_n | solution.py:134
  16.1 0.1 maximum_bitcast_fusion.1
  16.2 0.1 maximum_bitcast_fusion
  16.3 1.1 %copy.17 = bf16[2,8,2,2,16,2,256]{6,5,4,3,2,1,0:T(2,128)(2,1)S(1)} copy(bf16[2,8,2,2,16,2,256]{6,4,1,2,0,3,5:T(8,128)(2,1)S(1)} %maximum_bitcast_fusion) | data formatting | bytes 2097152 | tf_op jit(solution)/shard_map/transpose | solution.py:140
  17.4 1.5 %reshape.164 = bf16[2,512,512]{2,1,0:T(8,128)(2,1)} reshape(bf16[2,8,2,2,16,2,256]{6,5,4,3,2,1,0:T(2,128)(2,1)S(1)} %copy.17) | data formatting | bytes 2097152 | tf_op jit(solution)/shard_map/reshape | solution.py:140
  18.8 2.3 %copy.18 = bf16[2,512,512]{1,2,0:T(8,128)(2,1)} copy(bf16[2,512,512]{2,1,0:T(8,128)(2,1)} %reshape.164) | data formatting | bytes 2097152 | tf_op jit(solution)/shard_map/reshape | solution.py:140
  21.1 0.1 copy.19
  21.2 0.1 copy.20
  21.3 0.1 reshape.165
  21.4 2.2 %gather_fusion.2 = bf16[4,2,256,256]{3,2,1,0:T(8,128)(2,1)S(1)} fusion(bf16[8,2,256,256]{3,2,1,0:T(8,128)(2,1)} %param.7, s32[1024]{0:T(1024)S(1)} %pad_clamp_fusion), kind=kCustom, calls=%fused_computation.2 | custom fusion | bytes 2097168 | tf_op jit(solution)/shard_map/jit(_take)/gather | solution.py:144
  23.6 1.2 %copy_select_fusion = bf16[2,2,2,16,16,256]{5,4,2,1,3,0:T(8,128)(2,1)} fusion(bf16[2,2,2,16,16,256]{5,4,3,2,1,0:T(8,128)(2,1)S(1)} %bitcast.42, pred[2,2]{1,0:T(4,128)(4,1)S(1)} %copy.19), kind=kLoop, calls=%fused_computation.6 | loop fusion | flops 524288 | bytes 2097156 | tf_op jit(solution)/shard_map/jit(_take)/select_n | solution.py:144
  24.8 1.5 %all-to-all-done = bf16[32,16,512]{2,1,0:T(8,128)(2,1)} async-done(((bf16[32,16,512]{2,1,0:T(8,128)(2,1)}), bf16[32,16,512]{2,1,0:T(8,128)(2,1)}, u32[]{:S(2)}, u32[]{:S(2)}) %all-to-all-start) | async-done | bytes 524320 | tf_op jit(solution)/shard_map/all_to_all | solution.py:192
  26.3 3.4 %shard_map.56 = f32[16,8,2,256]{3,2,1,0:T(2,128)} custom-call(bf16[2,256,512]{2,1,0:T(8,128)(2,1)} %bitcast.1.stem_ref, bf16[2,512,512]{2,1,0:T(8,128)(2,1)} %bitcast.44, bf16[2048,256]{1,0:T(8,128)(2,1)} %bitcast.43), custom_call_target="tpu_custom_call" | custom-call | flops 536870912 | bytes 2883584 | tf_op jit(solution)/shard_map/pallas_call | solution.py:114
  (20 shorter events, 0.4 us)
Async XLA Ops:
  0.0 11.4 %copy-start = (bf16[8,2,256,256]{3,2,1,0:T(8,128)(2,1)S(1)}, bf16[8,2,256,256]{3,2,1,0:T(8,128)(2,1)}, u32[]{:S(2)}) copy-start(bf16[8,2,256,256]{3,2,1,0:T(8,128)(2,1)} %param.6) | copy-start | bytes 6291460
  0.0 12.3 %collective-permute-start = (s32[2,2]{1,0:T(2,128)}, s32[2,2]{1,0:T(2,128)S(1)}, u32[]{:S(2)}, u32[]{:S(2)}) collective-permute-start(s32[2,2]{1,0:T(2,128)} %bitcast.49), channel_id=1, source_target_pairs={{0,16},{16,0},{1,17},{17,1},{2,18},{18,2},{3,19},{19,3},{4,20},{20... | collective-permute-start | bytes 56 | tf_op jit(solution)/shard_map/ppermute | solution.py:14
  5.3 7.0 %copy-start.1 = (s32[1,2,2]{2,1,0:T(2,128)S(1)}, s32[1,2,2]{2,1,0:T(2,128)}, u32[]{:S(2)}) copy-start(s32[1,2,2]{2,1,0:T(2,128)} %param.8) | copy-start | bytes 52
  5.3 21.0 %all-to-all-start = ((bf16[32,16,512]{2,1,0:T(8,128)(2,1)}), bf16[32,16,512]{2,1,0:T(8,128)(2,1)}, u32[]{:S(2)}, u32[]{:S(2)}) async-start(bf16[32,16,512]{2,1,0:T(8,128)(2,1)} %bitcast.45), calls=%async_computation | async-start | bytes 1048576 | tf_op jit(solution)/shard_map/all_to_all | solution.py:192

commit v18 on v15

--- a/solution.py
+++ b/solution.py
@@ -50,38 +50,42 @@
 
 
 def regroup_kernel(stem_ref, weight_ref, second_ref, out_ref, real_ref, imag_ref):
-    block_count, rows, _ = stem_ref.shape
+    _, rows, _ = stem_ref.shape
     q_local = weight_ref.shape[2] // 64
     t_local = 16
     n_mode = rows // t_local
+    b = pl.program_id(0)
     lane = lax.broadcasted_iota(jnp.int32, (t_local, 128), 1)
     low = lane < 64
     imag_lane = (lane // 16) % 2 == 1
 
     def store(row, col, tile):
-        real_ref[row:row + t_local, col:col + 128] = jnp.where(imag_lane, -tile, tile)
-        imag_ref[row:row + t_local, col:col + 128] = jnp.where(
+        col = pl.ds(pl.multiple_of(col, 128), 128)
+        real_ref[row:row + t_local, col] = jnp.where(imag_lane, -tile, tile)
+        imag_ref[row:row + t_local, col] = jnp.where(
             imag_lane, pltpu.roll(tile, 16, 1), pltpu.roll(tile, 112, 1)
         )
 
-    for b in range(block_count):
-        product = jnp.dot(
-            stem_ref[b], weight_ref[b], preferred_element_type=jnp.float32
-        ).astype(jnp.bfloat16)
-        for pair in range(n_mode // 2):
-            upper = product[(2 * pair) * t_local:(2 * pair + 1) * t_local]
-            lower = product[(2 * pair + 1) * t_local:(2 * pair + 2) * t_local]
-            col = (b * n_mode // 2 + pair) * 128
-            for qp in range(q_local // 2):
-                first = upper[:, qp * 128:(qp + 1) * 128]
-                second = lower[:, qp * 128:(qp + 1) * 128]
-                store((2 * qp) * t_local, col, jnp.where(low, first, pltpu.roll(second, 64, 1)))
-                store((2 * qp + 1) * t_local, col, jnp.where(low, pltpu.roll(first, 64, 1), second))
-    weights = second_ref[...]
-    for part, lhs_ref in enumerate((real_ref, imag_ref)):
-        result = jnp.dot(lhs_ref[...], weights, preferred_element_type=jnp.float32)
-        for q in range(q_local):
-            out_ref[:, q, part, :] = result[q * t_local:(q + 1) * t_local]
+    product = jnp.dot(
+        stem_ref[0], weight_ref[0], preferred_element_type=jnp.float32
+    ).astype(jnp.bfloat16)
+    for pair in range(n_mode // 2):
+        upper = product[(2 * pair) * t_local:(2 * pair + 1) * t_local]
+        lower = product[(2 * pair + 1) * t_local:(2 * pair + 2) * t_local]
+        col = (b * (n_mode // 2) + pair) * 128
+        for qp in range(q_local // 2):
+            first = upper[:, qp * 128:(qp + 1) * 128]
+            second = lower[:, qp * 128:(qp + 1) * 128]
+            store((2 * qp) * t_local, col, jnp.where(low, first, pltpu.roll(second, 64, 1)))
+            store((2 * qp + 1) * t_local, col, jnp.where(low, pltpu.roll(first, 64, 1), second))
+
+    @pl.when(b == pl.num_programs(0) - 1)
+    def _():
+        weights = second_ref[...]
+        for part, lhs_ref in enumerate((real_ref, imag_ref)):
+            result = jnp.dot(lhs_ref[...], weights, preferred_element_type=jnp.float32)
+            for q in range(q_local):
+                out_ref[:, q, part, :] = result[q * t_local:(q + 1) * t_local]
 
 
 def regroup(stem_rows, first_w, second_w, q_local, t_local):
@@ -96,8 +100,13 @@
     return pl.pallas_call(
         regroup_kernel,
         out_shape=out_shape,
-        in_specs=[pl.BlockSpec(memory_space=pltpu.VMEM)] * 3,
-        out_specs=pl.BlockSpec(memory_space=pltpu.VMEM),
+        grid=(block_count,),
+        in_specs=[
+            pl.BlockSpec((1,) + stem_rows.shape[1:], lambda b: (b, 0, 0)),
+            pl.BlockSpec((1,) + first_w.shape[1:], lambda b: (b, 0, 0)),
+            pl.BlockSpec(second_w.shape, lambda b: (0, 0)),
+        ],
+        out_specs=pl.BlockSpec(out_shape.shape, lambda b: (0, 0, 0, 0)),
         scratch_shapes=[pltpu.VMEM(lhs_shape, jnp.bfloat16)] * 2,
         cost_estimate=pl.CostEstimate(
             flops=flops,

time: 29.6 us -> 29.9 us (1.010)
  Pallas kernels: 3.39 us -> 3.7 us
    pallas_call x1, Pallas kernels: 3.39 us -> 3.7 us  [regroup(): pl.pallas_call(regroup_kernel, out_shape=out_shape, grid=(block_count,),...]
where the time goes in v18:
time: 29.9 us; the launch traced here: 29.6 us
  local copies, waits for them, and re-layouts  12.1 us (40%)
  starting transfers between devices  8 us (27%)
  Pallas kernels  3.7 us (12%)
  other arithmetic  2.69 us (9%)
  waiting for transfers between devices  2.11 us (7%)
  matrix products  0.81 us (3%)
    all_to_all x1, starting transfers between devices, on_device(): stem_rows = lax.all_to_all(payload, ('cuts', 'mode'), 0, 0, tiled=True)  5.06 us
    reshape x2, local copies, waits for them, and re-layouts, stacked_part(): jnp.transpose(first_w, (2, 4, 3, 1, 5, 0, 6))  3.76 us
    pallas_call x1, Pallas kernels, regroup(): pl.pallas_call(regroup_kernel, out_shape=out_shape, grid=(block_count,),...  3.7 us
    ppermute x1, starting transfers between devices, gather_over_cuts(): current = lax.ppermute(current, 'cuts', ring)  2.94 us
    gather x1, local copies, waits for them, and re-layouts, stacked_part(): second = jnp.take(w2_table, second_ids.reshape(-1), axis=0)  2.2 us
    all_to_all x1, waiting for transfers between devices, on_device(): stem_rows = lax.all_to_all(payload, ('cuts', 'mode'), 0, 0, tiled=True)  2.11 us
    broadcast_in_dim x2, local copies, waits for them, and re-layouts, on_device(): payload = jnp.broadcast_to(pieces, (n_cuts, n_mode, t_local, 2 * width))  1.98 us
    gather x1, local copies, waits for them, and re-layouts, stacked_part(): picked = jnp.take(first_t, first_ids.reshape(-1), axis=0)  1.38 us
  transfers between devices with their start and end apart: 2, of which 1 were waited for; matrix products, arithmetic and copies ran while one was open for 53% of the time, Pallas kernels for 0%

profile of v18, /device:TPU:0, one launch (start us, length us, event | category | flops | bytes accessed | tf_op | source)
XLA Modules:
  0.0 29.6 jit_solution(14924648613118124759)
XLA Ops:
  0.0 2.9 %collective-permute-start = (s32[2,2]{1,0:T(2,128)}, s32[2,2]{1,0:T(2,128)S(1)}, u32[]{:S(2)}, u32[]{:S(2)}) collective-permute-start(s32[2,2]{1,0:T(2,128)} %bitcast.48), channel_id=1, source_target_pairs={{0,16},{16,0},{1,17},{17,1},{2,18},{18,2},{3,19},{19,3},{4,20},{20... | collective-permute-start | bytes 56 | tf_op jit(solution)/shard_map/ppermute | solution.py:14
  2.9 1.1 %broadcast_in_dim.34 = bf16[16,16,512]{2,1,0:T(8,128)(2,1)S(1)} reshape(bf16[1,256,2,256]{3,2,1,0:T(2,128)(2,1)} %param.5) | data formatting | bytes 524288 | tf_op jit(solution)/shard_map/broadcast_in_dim | solution.py:183
  4.1 0.9 %broadcast_in_dim.35 = bf16[2,16,16,512]{3,2,1,0:T(8,128)(2,1)} broadcast(bf16[16,16,512]{2,1,0:T(8,128)(2,1)S(1)} %broadcast_in_dim.34), dimensions={1,2,3} | broadcast | bytes 786432 | tf_op jit(solution)/shard_map/broadcast_in_dim | solution.py:183
  4.9 5.1 %all-to-all-start = ((bf16[32,16,512]{2,1,0:T(8,128)(2,1)}), bf16[32,16,512]{2,1,0:T(8,128)(2,1)}, u32[]{:S(2)}, u32[]{:S(2)}) async-start(bf16[32,16,512]{2,1,0:T(8,128)(2,1)} %bitcast), calls=%async_computation | async-start | bytes 1048576 | tf_op jit(solution)/shard_map/all_to_all | solution.py:185
  10.4 0.8 %fusion = bf16[8,2,128,256]{3,2,1,0:T(8,128)(2,1)S(1)} fusion(bf16[8,2,256,256]{3,2,1,0:T(8,128)(2,1)S(1)} %copy-done, s32[128]{0:T(128)S(1)} %eq.17), kind=kOutput, calls=%fused_computation.4 | convolution fusion | flops 268992512 | bytes 3146240 | tf_op jit(solution)/shard_map/nj,spkj->spnk/dot_general | solution.py:206
  11.2 0.6 %gather_fusion = s32[2,2,2]{2,1,0:T(2,128)S(1)} fusion(s32[2,2,2]{2,1,0:T(2,128)S(1)} %pad_add_fusion, s32[1024]{0:T(1024)S(1)} %pad_clamp_fusion.2), kind=kCustom, calls=%fused_computation | custom fusion | bytes 72 | tf_op jit(solution)/shard_map/jit(_take)/gather | solution.py:19
  11.9 0.2 slice_reduce_fusion
  12.1 0.1 copy.15
  12.2 0.1 reshape.164
  12.3 0.1 copy.13
  12.4 1.4 %gather_fusion.1 = bf16[4,2,128,256]{3,2,1,0:T(8,128)(2,1)} fusion(bf16[8,2,128,256]{3,2,1,0:T(8,128)(2,1)S(1)} %fusion, s32[1024]{0:T(1024)S(1)} %pad_clamp_fusion.1), kind=kCustom, calls=%fused_computation.1 | custom fusion | bytes 1048592 | tf_op jit(solution)/shard_map/jit(_take)/gather | solution.py:125
  13.8 1.2 %copy_select_fusion.1 = bf16[2,2,2,8,16,256]{5,4,3,1,0,2:T(8,128)(2,1)S(1)} fusion(bf16[2,2,2,8,16,256]{5,4,3,2,1,0:T(8,128)(2,1)} %bitcast.45, pred[2,2]{1,0:T(4,128)(4,1)S(1)} %copy.13), kind=kLoop, calls=%fused_computation.9 | loop fusion | flops 262144 | bytes 1048580 | tf_op jit(solution)/shard_map/jit(_take)/select_n | solution.py:125
  15.0 0.1 maximum_bitcast_fusion.1
  15.1 0.1 maximum_bitcast_fusion
  15.2 1.1 %copy.17 = bf16[2,8,2,2,16,2,256]{6,5,4,3,2,1,0:T(2,128)(2,1)S(1)} copy(bf16[2,8,2,2,16,2,256]{6,4,1,2,0,3,5:T(8,128)(2,1)S(1)} %maximum_bitcast_fusion) | data formatting | bytes 2097152 | tf_op jit(solution)/shard_map/transpose | solution.py:131
  16.3 1.5 %reshape.165 = bf16[2,512,512]{2,1,0:T(8,128)(2,1)} reshape(bf16[2,8,2,2,16,2,256]{6,5,4,3,2,1,0:T(2,128)(2,1)S(1)} %copy.17) | data formatting | bytes 2097152 | tf_op jit(solution)/shard_map/reshape | solution.py:131
  17.8 2.3 %copy.18 = bf16[2,512,512]{1,2,0:T(8,128)(2,1)} copy(bf16[2,512,512]{2,1,0:T(8,128)(2,1)} %reshape.165) | data formatting | bytes 2097152 | tf_op jit(solution)/shard_map/reshape | solution.py:131
  20.1 0.1 copy.19
  20.2 0.1 copy.20
  20.3 0.1 reshape.166
  20.4 2.2 %gather_fusion.2 = bf16[4,2,256,256]{3,2,1,0:T(8,128)(2,1)S(1)} fusion(bf16[8,2,256,256]{3,2,1,0:T(8,128)(2,1)} %param.7, s32[1024]{0:T(1024)S(1)} %pad_clamp_fusion), kind=kCustom, calls=%fused_computation.2 | custom fusion | bytes 2097168 | tf_op jit(solution)/shard_map/jit(_take)/gather | solution.py:135
  22.6 1.2 %copy_select_fusion = bf16[2,2,2,16,16,256]{5,4,2,1,3,0:T(8,128)(2,1)} fusion(bf16[2,2,2,16,16,256]{5,4,3,2,1,0:T(8,128)(2,1)S(1)} %bitcast.42, pred[2,2]{1,0:T(4,128)(4,1)S(1)} %copy.19), kind=kLoop, calls=%fused_computation.6 | loop fusion | flops 524288 | bytes 2097156 | tf_op jit(solution)/shard_map/jit(_take)/select_n | solution.py:135
  23.8 2.1 %all-to-all-done = bf16[32,16,512]{2,1,0:T(8,128)(2,1)} async-done(((bf16[32,16,512]{2,1,0:T(8,128)(2,1)}), bf16[32,16,512]{2,1,0:T(8,128)(2,1)}, u32[]{:S(2)}, u32[]{:S(2)}) %all-to-all-start) | async-done | bytes 524320 | tf_op jit(solution)/shard_map/all_to_all | solution.py:185
  25.9 3.7 %shard_map.55 = f32[16,8,2,256]{3,2,1,0:T(2,128)} custom-call(bf16[2,256,512]{2,1,0:T(8,128)(2,1)} %bitcast.1.stem_ref, bf16[2,512,512]{2,1,0:T(8,128)(2,1)} %bitcast.44, bf16[2048,256]{1,0:T(8,128)(2,1)} %bitcast.43), custom_call_target="tpu_custom_call" | custom-call | flops 536870912 | bytes 2883584 | tf_op jit(solution)/shard_map/pallas_call | solution.py:100
  (23 shorter events, 0.5 us)
Async XLA Ops:
  0.0 10.4 %copy-start = (bf16[8,2,256,256]{3,2,1,0:T(8,128)(2,1)S(1)}, bf16[8,2,256,256]{3,2,1,0:T(8,128)(2,1)}, u32[]{:S(2)}) copy-start(bf16[8,2,256,256]{3,2,1,0:T(8,128)(2,1)} %param.6) | copy-start | bytes 6291460
  0.0 10.0 %copy-start.1 = (s32[256]{0:T(256)S(1)}, s32[256]{0:T(256)}, u32[]{:S(2)}) copy-start(s32[256]{0:T(256)} %param.9) | copy-start | bytes 3076
  0.0 11.2 %collective-permute-start = (s32[2,2]{1,0:T(2,128)}, s32[2,2]{1,0:T(2,128)S(1)}, u32[]{:S(2)}, u32[]{:S(2)}) collective-permute-start(s32[2,2]{1,0:T(2,128)} %bitcast.48), channel_id=1, source_target_pairs={{0,16},{16,0},{1,17},{17,1},{2,18},{18,2},{3,19},{19,3},{4,20},{20... | collective-permute-start | bytes 56 | tf_op jit(solution)/shard_map/ppermute | solution.py:14
  4.9 6.3 %copy-start.2 = (s32[1,2,2]{2,1,0:T(2,128)S(1)}, s32[1,2,2]{2,1,0:T(2,128)}, u32[]{:S(2)}) copy-start(s32[1,2,2]{2,1,0:T(2,128)} %param.8) | copy-start | bytes 52
  4.9 20.9 %all-to-all-start = ((bf16[32,16,512]{2,1,0:T(8,128)(2,1)}), bf16[32,16,512]{2,1,0:T(8,128)(2,1)}, u32[]{:S(2)}, u32[]{:S(2)}) async-start(bf16[32,16,512]{2,1,0:T(8,128)(2,1)} %bitcast), calls=%async_computation | async-start | bytes 1048576 | tf_op jit(solution)/shard_map/all_to_all | solution.py:185

commit v19 on v15

--- a/solution.py
+++ b/solution.py
@@ -78,10 +78,11 @@
                 store((2 * qp) * t_local, col, jnp.where(low, first, pltpu.roll(second, 64, 1)))
                 store((2 * qp + 1) * t_local, col, jnp.where(low, pltpu.roll(first, 64, 1), second))
     weights = second_ref[...]
-    for part, lhs_ref in enumerate((real_ref, imag_ref)):
-        result = jnp.dot(lhs_ref[...], weights, preferred_element_type=jnp.float32)
-        for q in range(q_local):
-            out_ref[:, q, part, :] = result[q * t_local:(q + 1) * t_local]
+    real_out = jnp.dot(real_ref[...], weights, preferred_element_type=jnp.float32)
+    imag_out = jnp.dot(imag_ref[...], weights, preferred_element_type=jnp.float32)
+    for q in range(q_local):
+        rows = slice(q * t_local, (q + 1) * t_local)
+        out_ref[:, q] = jnp.stack([real_out[rows], imag_out[rows]], axis=1)
 
 
 def regroup(stem_rows, first_w, second_w, q_local, t_local):

time: 29.6 us -> 29.7 us (level)
  no operation moved by 1% of the time
where the time goes in v19:
time: 29.7 us; the launch traced here: 29.4 us
  local copies, waits for them, and re-layouts  12.1 us (41%)
  starting transfers between devices  8 us (27%)
  Pallas kernels  3.48 us (12%)
  other arithmetic  2.69 us (9%)
  waiting for transfers between devices  2.11 us (7%)
  matrix products  0.81 us (3%)
    all_to_all x1, starting transfers between devices, on_device(): stem_rows = lax.all_to_all(payload, ('cuts', 'mode'), 0, 0, tiled=True)  5.06 us
    reshape x2, local copies, waits for them, and re-layouts, stacked_part(): jnp.transpose(first_w, (2, 4, 3, 1, 5, 0, 6))  3.76 us
    pallas_call x1, Pallas kernels, regroup(): pl.pallas_call(regroup_kernel, out_shape=out_shape, in_specs=[pl.BlockSpe...  3.48 us
    ppermute x1, starting transfers between devices, gather_over_cuts(): current = lax.ppermute(current, 'cuts', ring)  2.94 us
    gather x1, local copies, waits for them, and re-layouts, stacked_part(): second = jnp.take(w2_table, second_ids.reshape(-1), axis=0)  2.2 us
    all_to_all x1, waiting for transfers between devices, on_device(): stem_rows = lax.all_to_all(payload, ('cuts', 'mode'), 0, 0, tiled=True)  2.11 us
    broadcast_in_dim x2, local copies, waits for them, and re-layouts, on_device(): payload = jnp.broadcast_to(pieces, (n_cuts, n_mode, t_local, 2 * width))  1.98 us
    gather x1, local copies, waits for them, and re-layouts, stacked_part(): picked = jnp.take(first_t, first_ids.reshape(-1), axis=0)  1.38 us
  transfers between devices with their start and end apart: 2, of which 1 were waited for; matrix products, arithmetic and copies ran while one was open for 53% of the time, Pallas kernels for 0%

profile of v19, /device:TPU:0, one launch (start us, length us, event | category | flops | bytes accessed | tf_op | source)
XLA Modules:
  0.0 29.4 jit_solution(1670473708985531049)
XLA Ops:
  0.0 2.9 %collective-permute-start = (s32[2,2]{1,0:T(2,128)}, s32[2,2]{1,0:T(2,128)S(1)}, u32[]{:S(2)}, u32[]{:S(2)}) collective-permute-start(s32[2,2]{1,0:T(2,128)} %bitcast.48), channel_id=1, source_target_pairs={{0,16},{16,0},{1,17},{17,1},{2,18},{18,2},{3,19},{19,3},{4,20},{20... | collective-permute-start | bytes 56 | tf_op jit(solution)/shard_map/ppermute | solution.py:14
  2.9 1.1 %broadcast_in_dim.34 = bf16[16,16,512]{2,1,0:T(8,128)(2,1)S(1)} reshape(bf16[1,256,2,256]{3,2,1,0:T(2,128)(2,1)} %param.5) | data formatting | bytes 524288 | tf_op jit(solution)/shard_map/broadcast_in_dim | solution.py:175
  4.1 0.9 %broadcast_in_dim.35 = bf16[2,16,16,512]{3,2,1,0:T(8,128)(2,1)} broadcast(bf16[16,16,512]{2,1,0:T(8,128)(2,1)S(1)} %broadcast_in_dim.34), dimensions={1,2,3} | broadcast | bytes 786432 | tf_op jit(solution)/shard_map/broadcast_in_dim | solution.py:175
  4.9 5.1 %all-to-all-start = ((bf16[32,16,512]{2,1,0:T(8,128)(2,1)}), bf16[32,16,512]{2,1,0:T(8,128)(2,1)}, u32[]{:S(2)}, u32[]{:S(2)}) async-start(bf16[32,16,512]{2,1,0:T(8,128)(2,1)} %bitcast), calls=%async_computation | async-start | bytes 1048576 | tf_op jit(solution)/shard_map/all_to_all | solution.py:177
  10.4 0.8 %fusion = bf16[8,2,128,256]{3,2,1,0:T(8,128)(2,1)S(1)} fusion(bf16[8,2,256,256]{3,2,1,0:T(8,128)(2,1)S(1)} %copy-done, s32[128]{0:T(128)S(1)} %eq.17), kind=kOutput, calls=%fused_computation.4 | convolution fusion | flops 268992512 | bytes 3146240 | tf_op jit(solution)/shard_map/nj,spkj->spnk/dot_general | solution.py:198
  11.2 0.6 %gather_fusion = s32[2,2,2]{2,1,0:T(2,128)S(1)} fusion(s32[2,2,2]{2,1,0:T(2,128)S(1)} %pad_add_fusion, s32[1024]{0:T(1024)S(1)} %pad_clamp_fusion.2), kind=kCustom, calls=%fused_computation | custom fusion | bytes 72 | tf_op jit(solution)/shard_map/jit(_take)/gather | solution.py:19
  11.9 0.2 slice_reduce_fusion
  12.1 0.1 copy.15
  12.2 0.1 reshape.164
  12.3 0.1 copy.13
  12.4 1.4 %gather_fusion.1 = bf16[4,2,128,256]{3,2,1,0:T(8,128)(2,1)} fusion(bf16[8,2,128,256]{3,2,1,0:T(8,128)(2,1)S(1)} %fusion, s32[1024]{0:T(1024)S(1)} %pad_clamp_fusion.1), kind=kCustom, calls=%fused_computation.1 | custom fusion | bytes 1048592 | tf_op jit(solution)/shard_map/jit(_take)/gather | solution.py:117
  13.8 1.2 %copy_select_fusion.1 = bf16[2,2,2,8,16,256]{5,4,3,1,0,2:T(8,128)(2,1)S(1)} fusion(bf16[2,2,2,8,16,256]{5,4,3,2,1,0:T(8,128)(2,1)} %bitcast.45, pred[2,2]{1,0:T(4,128)(4,1)S(1)} %copy.13), kind=kLoop, calls=%fused_computation.9 | loop fusion | flops 262144 | bytes 1048580 | tf_op jit(solution)/shard_map/jit(_take)/select_n | solution.py:117
  15.0 0.1 maximum_bitcast_fusion.1
  15.1 0.1 maximum_bitcast_fusion
  15.2 1.1 %copy.17 = bf16[2,8,2,2,16,2,256]{6,5,4,3,2,1,0:T(2,128)(2,1)S(1)} copy(bf16[2,8,2,2,16,2,256]{6,4,1,2,0,3,5:T(8,128)(2,1)S(1)} %maximum_bitcast_fusion) | data formatting | bytes 2097152 | tf_op jit(solution)/shard_map/transpose | solution.py:123
  16.3 1.5 %reshape.165 = bf16[2,512,512]{2,1,0:T(8,128)(2,1)} reshape(bf16[2,8,2,2,16,2,256]{6,5,4,3,2,1,0:T(2,128)(2,1)S(1)} %copy.17) | data formatting | bytes 2097152 | tf_op jit(solution)/shard_map/reshape | solution.py:123
  17.8 2.3 %copy.18 = bf16[2,512,512]{1,2,0:T(8,128)(2,1)} copy(bf16[2,512,512]{2,1,0:T(8,128)(2,1)} %reshape.165) | data formatting | bytes 2097152 | tf_op jit(solution)/shard_map/reshape | solution.py:123
  20.1 0.1 copy.19
  20.2 0.1 copy.20
  20.3 0.1 reshape.166
  20.4 2.2 %gather_fusion.2 = bf16[4,2,256,256]{3,2,1,0:T(8,128)(2,1)S(1)} fusion(bf16[8,2,256,256]{3,2,1,0:T(8,128)(2,1)} %param.7, s32[1024]{0:T(1024)S(1)} %pad_clamp_fusion), kind=kCustom, calls=%fused_computation.2 | custom fusion | bytes 2097168 | tf_op jit(solution)/shard_map/jit(_take)/gather | solution.py:127
  22.6 1.2 %copy_select_fusion = bf16[2,2,2,16,16,256]{5,4,2,1,3,0:T(8,128)(2,1)} fusion(bf16[2,2,2,16,16,256]{5,4,3,2,1,0:T(8,128)(2,1)S(1)} %bitcast.42, pred[2,2]{1,0:T(4,128)(4,1)S(1)} %copy.19), kind=kLoop, calls=%fused_computation.6 | loop fusion | flops 524288 | bytes 2097156 | tf_op jit(solution)/shard_map/jit(_take)/select_n | solution.py:127
  23.8 2.1 %all-to-all-done = bf16[32,16,512]{2,1,0:T(8,128)(2,1)} async-done(((bf16[32,16,512]{2,1,0:T(8,128)(2,1)}), bf16[32,16,512]{2,1,0:T(8,128)(2,1)}, u32[]{:S(2)}, u32[]{:S(2)}) %all-to-all-start) | async-done | bytes 524320 | tf_op jit(solution)/shard_map/all_to_all | solution.py:177
  25.9 3.5 %shard_map.55 = f32[16,8,2,256]{3,2,1,0:T(2,128)} custom-call(bf16[2,256,512]{2,1,0:T(8,128)(2,1)} %bitcast.1.stem_ref, bf16[2,512,512]{2,1,0:T(8,128)(2,1)} %bitcast.44, bf16[2048,256]{1,0:T(8,128)(2,1)} %bitcast.43), custom_call_target="tpu_custom_call" | custom-call | flops 536870912 | bytes 2883584 | tf_op jit(solution)/shard_map/pallas_call | solution.py:97
  (23 shorter events, 0.5 us)
Async XLA Ops:
  0.0 10.4 %copy-start = (bf16[8,2,256,256]{3,2,1,0:T(8,128)(2,1)S(1)}, bf16[8,2,256,256]{3,2,1,0:T(8,128)(2,1)}, u32[]{:S(2)}) copy-start(bf16[8,2,256,256]{3,2,1,0:T(8,128)(2,1)} %param.6) | copy-start | bytes 6291460
  0.0 10.0 %copy-start.1 = (s32[256]{0:T(256)S(1)}, s32[256]{0:T(256)}, u32[]{:S(2)}) copy-start(s32[256]{0:T(256)} %param.9) | copy-start | bytes 3076
  0.0 11.2 %collective-permute-start = (s32[2,2]{1,0:T(2,128)}, s32[2,2]{1,0:T(2,128)S(1)}, u32[]{:S(2)}, u32[]{:S(2)}) collective-permute-start(s32[2,2]{1,0:T(2,128)} %bitcast.48), channel_id=1, source_target_pairs={{0,16},{16,0},{1,17},{17,1},{2,18},{18,2},{3,19},{19,3},{4,20},{20... | collective-permute-start | bytes 56 | tf_op jit(solution)/shard_map/ppermute | solution.py:14
  4.9 6.3 %copy-start.2 = (s32[1,2,2]{2,1,0:T(2,128)S(1)}, s32[1,2,2]{2,1,0:T(2,128)}, u32[]{:S(2)}) copy-start(s32[1,2,2]{2,1,0:T(2,128)} %param.8) | copy-start | bytes 52
  4.9 20.9 %all-to-all-start = ((bf16[32,16,512]{2,1,0:T(8,128)(2,1)}), bf16[32,16,512]{2,1,0:T(8,128)(2,1)}, u32[]{:S(2)}, u32[]{:S(2)}) async-start(bf16[32,16,512]{2,1,0:T(8,128)(2,1)} %bitcast), calls=%async_computation | async-start | bytes 1048576 | tf_op jit(solution)/shard_map/all_to_all | solution.py:177

commit v20 on v14

--- a/solution.py
+++ b/solution.py
@@ -65,9 +65,19 @@
         )
 
     for b in range(block_count):
-        product = jnp.dot(
-            stem_ref[b], weight_ref[b], preferred_element_type=jnp.float32
-        ).astype(jnp.bfloat16)
+        width = weight_ref.shape[1]
+        from_real = jnp.dot(
+            stem_ref[b, :, :width], weight_ref[b], preferred_element_type=jnp.float32
+        )
+        from_imag = jnp.dot(
+            stem_ref[b, :, width:], weight_ref[b], preferred_element_type=jnp.float32
+        )
+        wide_lane = lax.broadcasted_iota(jnp.int32, from_imag.shape, 1)
+        second_group = (wide_lane // 16) % 2 == 1
+        product = from_real + jnp.where(
+            second_group, pltpu.roll(from_imag, 16, 1), -pltpu.roll(from_imag, 496, 1)
+        )
+        product = product.astype(jnp.bfloat16)
         for pair in range(n_mode // 2):
             upper = product[(2 * pair) * t_local:(2 * pair + 1) * t_local]
             lower = product[(2 * pair + 1) * t_local:(2 * pair + 2) * t_local]
@@ -129,7 +139,10 @@
         second_w = jnp.transpose(second, (0, 3, 1, 2, 4, 5)).reshape(
             block_count * n_mode * group, out_width
         )
-        return regroup(stem_rows, jnp.swapaxes(first_w, 1, 2), second_w, q_local, t_local)
+        first_half = jnp.transpose(picked, (0, 5, 3, 1, 2, 4)).reshape(
+            block_count, width, q_local * group
+        )
+        return regroup(stem_rows, first_half, second_w, q_local, t_local)
     else:
         second = jnp.take(w2_table, second_ids.reshape(-1), axis=0)
         second = jnp.swapaxes(second, 2, 3)

time: 30.3 us -> 34.2 us (1.13)
  waiting for transfers between devices: 0.89 us -> 5.07 us
  Pallas kernels: 2.73 us -> 6.88 us
  local copies, waits for them, and re-layouts: 14.3 us -> 10.2 us
    all_to_all x1, waiting for transfers between devices: 0.89 us -> 5.06 us  [on_device(): stem_rows = lax.all_to_all(payload, ('cuts', 'mode'), 0, 0, tiled=True)]
    pallas_call x1, Pallas kernels: 2.73 us -> 6.88 us  [regroup(): pl.pallas_call(regroup_kernel, out_shape=out_shape, in_specs=[pl.BlockSpe...]
    reshape x2 -> x1, local copies, waits for them, and re-layouts: 3.76 us -> 1.01 us  [stacked_part(): jnp.transpose(picked, (0, 5, 3, 1, 2, 4))]
    transpose x1 -> x0, local copies, waits for them, and re-layouts: 1.08 us -> none  [stacked_part(): jnp.transpose(first_w, (2, 4, 3, 1, 5, 0, 6))]
  transfers between devices with their start and end apart: 2 -> 2, of which waited for: 1 -> 1; matrix products, arithmetic and copies ran while one was open for 56% -> 37% of each run, Pallas kernels for 0% -> 0%
where the time goes in v20:
time: 34.2 us; the launch traced here: 33.8 us
  local copies, waits for them, and re-layouts  10.2 us (30%)
  starting transfers between devices  8 us (23%)
  Pallas kernels  6.88 us (20%)
  waiting for transfers between devices  5.07 us (15%)
  other arithmetic  2.69 us (8%)
  matrix products  0.81 us (2%)
    pallas_call x1, Pallas kernels, regroup(): pl.pallas_call(regroup_kernel, out_shape=out_shape, in_specs=[pl.BlockSpe...  6.88 us
    all_to_all x1, waiting for transfers between devices, on_device(): stem_rows = lax.all_to_all(payload, ('cuts', 'mode'), 0, 0, tiled=True)  5.06 us
    all_to_all x1, starting transfers between devices, on_device(): stem_rows = lax.all_to_all(payload, ('cuts', 'mode'), 0, 0, tiled=True)  5.06 us
    gather x1, local copies, waits for them, and re-layouts, stacked_part(): second = jnp.take(w2_table, second_ids.reshape(-1), axis=0)  3.17 us
    ppermute x1, starting transfers between devices, gather_over_cuts(): current = lax.ppermute(current, 'cuts', ring)  2.94 us
    broadcast_in_dim x2, local copies, waits for them, and re-layouts, on_device(): payload = jnp.broadcast_to(pieces, (n_cuts, n_mode, t_local, 2 * width))  1.96 us
    select_n x2, other arithmetic, stacked_part(): second = jnp.take(w2_table, second_ids.reshape(-1), axis=0)  1.4 us
    gather x1, local copies, waits for them, and re-layouts, stacked_part(): picked = jnp.take(first_t, first_ids.reshape(-1), axis=0)  1.37 us
  transfers between devices with their start and end apart: 2, of which 1 were waited for; matrix products, arithmetic and copies ran while one was open for 37% of the time, Pallas kernels for 0%

profile of v20, /device:TPU:0, one launch (start us, length us, event | category | flops | bytes accessed | tf_op | source)
XLA Modules:
  0.0 33.8 jit_solution(15876556194178289708)
XLA Ops:
  0.0 2.9 %collective-permute-start = (s32[2,2]{1,0:T(2,128)}, s32[2,2]{1,0:T(2,128)S(1)}, u32[]{:S(2)}, u32[]{:S(2)}) collective-permute-start(s32[2,2]{1,0:T(2,128)} %bitcast.38), channel_id=1, source_target_pairs={{0,16},{16,0},{1,17},{17,1},{2,18},{18,2},{3,19},{19,3},{4,20},{20... | collective-permute-start | bytes 56 | tf_op jit(solution)/shard_map/ppermute | solution.py:14
  2.9 1.1 %broadcast_in_dim.34 = bf16[16,16,512]{2,1,0:T(8,128)(2,1)S(1)} reshape(bf16[1,256,2,256]{3,2,1,0:T(2,128)(2,1)} %param.5) | data formatting | bytes 524288 | tf_op jit(solution)/shard_map/broadcast_in_dim | solution.py:188
  4.1 0.8 %broadcast_in_dim.35 = bf16[2,16,16,512]{3,2,1,0:T(8,128)(2,1)} broadcast(bf16[16,16,512]{2,1,0:T(8,128)(2,1)S(1)} %broadcast_in_dim.34), dimensions={1,2,3} | broadcast | bytes 786432 | tf_op jit(solution)/shard_map/broadcast_in_dim | solution.py:188
  4.9 5.1 %all-to-all-start = ((bf16[32,16,512]{2,1,0:T(8,128)(2,1)}), bf16[32,16,512]{2,1,0:T(8,128)(2,1)}, u32[]{:S(2)}, u32[]{:S(2)}) async-start(bf16[32,16,512]{2,1,0:T(8,128)(2,1)} %bitcast), calls=%async_computation | async-start | bytes 1048576 | tf_op jit(solution)/shard_map/all_to_all | solution.py:190
  10.0 0.1 reshape.153
  10.1 0.1 dynamic-slice_bitcast_fusion
  10.3 0.1 eq.17
  10.4 0.8 %fusion = bf16[8,2,128,256]{3,2,1,0:T(8,128)(2,1)S(1)} fusion(bf16[8,2,256,256]{3,2,1,0:T(8,128)(2,1)S(1)} %copy-done, s32[128]{0:T(128)S(1)} %eq.17), kind=kOutput, calls=%fused_computation.4 | convolution fusion | flops 268992512 | bytes 3146240 | tf_op jit(solution)/shard_map/nj,spkj->spnk/dot_general | solution.py:211
  11.2 0.6 %gather_fusion = s32[2,2,2]{2,1,0:T(2,128)S(1)} fusion(s32[2,2,2]{2,1,0:T(2,128)S(1)} %pad_add_fusion, s32[1024]{0:T(1024)S(1)} %pad_clamp_fusion.2), kind=kCustom, calls=%fused_computation | custom fusion | bytes 72 | tf_op jit(solution)/shard_map/jit(_take)/gather | solution.py:19
  11.9 0.2 slice_reduce_fusion
  12.1 0.1 copy.14
  12.2 0.1 reshape.154
  12.3 0.1 copy.12
  12.4 1.4 %gather_fusion.1 = bf16[4,2,128,256]{3,2,1,0:T(8,128)(2,1)} fusion(bf16[8,2,128,256]{3,2,1,0:T(8,128)(2,1)S(1)} %fusion, s32[1024]{0:T(1024)S(1)} %pad_clamp_fusion.1), kind=kCustom, calls=%fused_computation.1 | custom fusion | bytes 1048592 | tf_op jit(solution)/shard_map/jit(_take)/gather | solution.py:127
  13.8 1.2 %copy_select_fusion.1 = bf16[2,2,2,8,16,256]{5,4,2,1,3,0:T(8,128)(2,1)S(1)} fusion(bf16[2,2,2,8,16,256]{5,4,3,2,1,0:T(8,128)(2,1)} %bitcast.35, pred[2,2]{1,0:T(4,128)(4,1)S(1)} %copy.12), kind=kLoop, calls=%fused_computation.6 | loop fusion | flops 262144 | bytes 1048580 | tf_op jit(solution)/shard_map/jit(_take)/select_n | solution.py:127
  14.9 1.0 %copy.19.weight_ref = bf16[2,256,512]{2,1,0:T(8,128)(2,1)} copy(bf16[2,256,512]{1,2,0:T(8,128)(2,1)S(1)} %bitcast.34) | data formatting | bytes 1048576 | tf_op jit(solution)/shard_map/reshape | solution.py:142
  15.9 0.1 copy.16
  16.0 0.1 copy.17
  16.1 0.1 reshape.156
  16.2 3.2 %gather_fusion.2 = bf16[4,2,256,256]{3,2,1,0:T(8,128)(2,1)} fusion(bf16[8,2,256,256]{3,2,1,0:T(8,128)(2,1)} %param.7, s32[1024]{0:T(1024)S(1)} %pad_clamp_fusion), kind=kCustom, calls=%fused_computation.2 | custom fusion | bytes 2097168 | tf_op jit(solution)/shard_map/jit(_take)/gather | solution.py:137
  19.4 1.4 %copy_select_fusion = bf16[2,2,2,16,16,256]{5,4,2,1,3,0:T(8,128)(2,1)S(1)} fusion(bf16[2,2,2,16,16,256]{5,4,3,2,1,0:T(8,128)(2,1)} %bitcast.33, pred[2,2]{1,0:T(4,128)(4,1)S(1)} %copy.16), kind=kLoop, calls=%fused_computation.5 | loop fusion | flops 524288 | bytes 2097156 | tf_op jit(solution)/shard_map/jit(_take)/select_n | solution.py:137
  20.8 5.1 %all-to-all-done = bf16[32,16,512]{2,1,0:T(8,128)(2,1)} async-done(((bf16[32,16,512]{2,1,0:T(8,128)(2,1)}), bf16[32,16,512]{2,1,0:T(8,128)(2,1)}, u32[]{:S(2)}, u32[]{:S(2)}) %all-to-all-start) | async-done | bytes 524320 | tf_op jit(solution)/shard_map/all_to_all | solution.py:190
  25.9 1.0 %copy-done.1 = bf16[2,256,512]{2,1,0:T(8,128)(2,1)S(1)} copy-done((bf16[2,256,512]{2,1,0:T(8,128)(2,1)S(1)}, bf16[2,256,512]{2,1,0:T(8,128)(2,1)}, u32[]{:S(2)}) %copy-start.1) | copy-done | bytes 524312
  26.9 6.9 %shard_map.55 = f32[16,8,2,256]{3,2,1,0:T(2,128)} custom-call(bf16[2,256,512]{2,1,0:T(8,128)(2,1)} %bitcast.1.stem_ref, bf16[2,256,512]{2,1,0:T(8,128)(2,1)S(1)} %copy-done.1, bf16[2048,256]{1,0:T(8,128)(2,1)S(1)} %bitcast.32), custom_call_target="tpu_custom_call" | custom-call | flops 402653184 | bytes 2359296 | tf_op jit(solution)/shard_map/pallas_call | solution.py:106
  (19 shorter events, 0.2 us)
Async XLA Ops:
  0.0 10.4 %copy-start = (bf16[8,2,256,256]{3,2,1,0:T(8,128)(2,1)S(1)}, bf16[8,2,256,256]{3,2,1,0:T(8,128)(2,1)}, u32[]{:S(2)}) copy-start(bf16[8,2,256,256]{3,2,1,0:T(8,128)(2,1)} %param.6) | copy-start | bytes 6291460
  0.0 10.0 %copy-start.2 = (s32[256]{0:T(256)S(1)}, s32[256]{0:T(256)}, u32[]{:S(2)}) copy-start(s32[256]{0:T(256)} %param.9) | copy-start | bytes 3076
  0.0 11.2 %collective-permute-start = (s32[2,2]{1,0:T(2,128)}, s32[2,2]{1,0:T(2,128)S(1)}, u32[]{:S(2)}, u32[]{:S(2)}) collective-permute-start(s32[2,2]{1,0:T(2,128)} %bitcast.38), channel_id=1, source_target_pairs={{0,16},{16,0},{1,17},{17,1},{2,18},{18,2},{3,19},{19,3},{4,20},{20... | collective-permute-start | bytes 56 | tf_op jit(solution)/shard_map/ppermute | solution.py:14
  4.9 6.3 %copy-start.3 = (s32[1,2,2]{2,1,0:T(2,128)S(1)}, s32[1,2,2]{2,1,0:T(2,128)}, u32[]{:S(2)}) copy-start(s32[1,2,2]{2,1,0:T(2,128)} %param.8) | copy-start | bytes 52
  4.9 20.9 %all-to-all-start = ((bf16[32,16,512]{2,1,0:T(8,128)(2,1)}), bf16[32,16,512]{2,1,0:T(8,128)(2,1)}, u32[]{:S(2)}, u32[]{:S(2)}) async-start(bf16[32,16,512]{2,1,0:T(8,128)(2,1)} %bitcast), calls=%async_computation | async-start | bytes 1048576 | tf_op jit(solution)/shard_map/all_to_all | solution.py:190
  25.9 1.0 %copy-start.1 = (bf16[2,256,512]{2,1,0:T(8,128)(2,1)S(1)}, bf16[2,256,512]{2,1,0:T(8,128)(2,1)}, u32[]{:S(2)}) copy-start(bf16[2,256,512]{2,1,0:T(8,128)(2,1)} %copy.19.weight_ref) | copy-start | bytes 1572868

commit v21 on v15

--- a/solution.py
+++ b/solution.py
@@ -176,7 +176,8 @@
     stem_rows = lax.all_to_all(payload, ("cuts", "mode"), 0, 0, tiled=True)
     stem_rows = stem_rows.reshape(block_count, n_mode * t_local, 2 * width)
 
-    all_ids = gather_over_cuts(slice_ids[0], n_cuts)
+    tie = (payload[0, 0, 0] * 0).astype(slice_ids.dtype)
+    all_ids = gather_over_cuts(slice_ids[0] + tie, n_cuts)
     first_ids = all_ids[:, :, 0].T
     second_ids = all_ids[:, :, 1].T
 

time: 29.6 us -> 31.4 us (1.061)
  waiting for transfers between devices: 2.11 us -> 0.68 us
  local copies, waits for them, and re-layouts: 12.1 us -> 13.5 us
  starting transfers between devices: 8 us -> 9.21 us
  between operations: 0.16 us -> 0.8 us
    all_to_all x1, starting transfers between devices: 5.06 us -> 7.43 us  [on_device(): stem_rows = lax.all_to_all(payload, ('cuts', 'mode'), 0, 0, tiled=True)]
    all_to_all x1, waiting for transfers between devices: 2.11 us -> 0.01 us  [on_device(): stem_rows = lax.all_to_all(payload, ('cuts', 'mode'), 0, 0, tiled=True)]
    slice x0 -> x1, local copies, waits for them, and re-layouts: none -> 1.2 us  [on_device(): tie = (payload[0, 0, 0] * 0).astype(slice_ids.dtype)]
    ppermute x1, starting transfers between devices: 2.94 us -> 1.78 us  [gather_over_cuts(): current = lax.ppermute(current, 'cuts', ring)]
    ppermute x1, waiting for transfers between devices: 0.01 us -> 0.67 us  [gather_over_cuts(): current = lax.ppermute(current, 'cuts', ring)]
  transfers between devices with their start and end apart: 2 -> 2, of which waited for: 1 -> 1; matrix products, arithmetic and copies ran while one was open for 53% -> 48% of each run, Pallas kernels for 0% -> 0%
where the time goes in v21:
time: 31.4 us; the launch traced here: 31 us
  local copies, waits for them, and re-layouts  13.5 us (43%)
  starting transfers between devices  9.21 us (29%)
  Pallas kernels  3.39 us (11%)
  other arithmetic  2.69 us (9%)
  matrix products  0.82 us (3%)
  between operations  0.8 us (3%)
  waiting for transfers between devices  0.68 us (2%)
    all_to_all x1, starting transfers between devices, on_device(): stem_rows = lax.all_to_all(payload, ('cuts', 'mode'), 0, 0, tiled=True)  7.43 us
    reshape x2, local copies, waits for them, and re-layouts, stacked_part(): jnp.transpose(first_w, (2, 4, 3, 1, 5, 0, 6))  3.76 us
    pallas_call x1, Pallas kernels, regroup(): pl.pallas_call(regroup_kernel, out_shape=out_shape, in_specs=[pl.BlockSpe...  3.39 us
    gather x1, local copies, waits for them, and re-layouts, stacked_part(): second = jnp.take(w2_table, second_ids.reshape(-1), axis=0)  2.21 us
    broadcast_in_dim x2, local copies, waits for them, and re-layouts, on_device(): payload = jnp.broadcast_to(pieces, (n_cuts, n_mode, t_local, 2 * width))  2.13 us
    ppermute x1, starting transfers between devices, gather_over_cuts(): current = lax.ppermute(current, 'cuts', ring)  1.78 us
    gather x1, local copies, waits for them, and re-layouts, stacked_part(): picked = jnp.take(first_t, first_ids.reshape(-1), axis=0)  1.38 us
    slice x1, local copies, waits for them, and re-layouts, on_device(): tie = (payload[0, 0, 0] * 0).astype(slice_ids.dtype)  1.2 us
  transfers between devices with their start and end apart: 2, of which 1 were waited for; matrix products, arithmetic and copies ran while one was open for 48% of the time, Pallas kernels for 0%

profile of v21, /device:TPU:0, one launch (start us, length us, event | category | flops | bytes accessed | tf_op | source)
XLA Modules:
  0.0 31.0 jit_solution(3500977960543006954)
XLA Ops:
  0.0 1.3 %broadcast_in_dim.34 = bf16[16,16,512]{2,1,0:T(8,128)(2,1)S(1)} reshape(bf16[1,256,2,256]{3,2,1,0:T(2,128)(2,1)} %param.5) | data formatting | bytes 524288 | tf_op jit(solution)/shard_map/broadcast_in_dim | solution.py:174
  1.3 0.9 %broadcast_in_dim.35 = bf16[2,16,16,512]{3,2,1,0:T(8,128)(2,1)} broadcast(bf16[16,16,512]{2,1,0:T(8,128)(2,1)S(1)} %broadcast_in_dim.34), dimensions={1,2,3} | broadcast | bytes 786432 | tf_op jit(solution)/shard_map/broadcast_in_dim | solution.py:174
  2.1 7.4 %all-to-all-start = ((bf16[32,16,512]{2,1,0:T(8,128)(2,1)}), bf16[32,16,512]{2,1,0:T(8,128)(2,1)}, u32[]{:S(2)}, u32[]{:S(2)}) async-start(bf16[32,16,512]{2,1,0:T(8,128)(2,1)} %bitcast), calls=%async_computation | async-start | bytes 1048576 | tf_op jit(solution)/shard_map/all_to_all | solution.py:176
  9.6 1.2 %slice.26 = bf16[1,1,1]{2,1,0:T(2,128)(2,1)} slice(bf16[32,16,512]{2,1,0:T(8,128)(2,1)} %bitcast), slice={[0:1], [0:1], [0:1]} | slice | bytes 4 | tf_op jit(solution)/shard_map/slice | solution.py:179
  11.5 1.8 %collective-permute-start = (s32[2,2]{1,0:T(2,128)S(1)}, s32[2,2]{1,0:T(2,128)S(1)}, u32[]{:S(2)}, u32[]{:S(2)}) collective-permute-start(s32[2,2]{1,0:T(2,128)S(1)} %fusion.11), channel_id=1, source_target_pairs={{0,16},{16,0},{1,17},{17,1},{2,18},{18,2},{3,19},{19,3},{4,20},{20... | collective-permute-start | bytes 56 | tf_op jit(solution)/shard_map/ppermute | solution.py:14
  13.6 0.8 %fusion = bf16[8,2,128,256]{3,2,1,0:T(8,128)(2,1)S(1)} fusion(bf16[8,2,256,256]{3,2,1,0:T(8,128)(2,1)S(1)} %copy-done, s32[128]{0:T(128)S(1)} %eq.17), kind=kOutput, calls=%fused_computation.4 | convolution fusion | flops 268992512 | bytes 3146240 | tf_op jit(solution)/shard_map/nj,spkj->spnk/dot_general | solution.py:198
  14.5 0.7 %collective-permute-done = s32[2,2]{1,0:T(2,128)S(1)} collective-permute-done((s32[2,2]{1,0:T(2,128)S(1)}, s32[2,2]{1,0:T(2,128)S(1)}, u32[]{:S(2)}, u32[]{:S(2)}) %collective-permute-start) | collective-permute-done | bytes 48 | tf_op jit(solution)/shard_map/ppermute | solution.py:14
  15.1 0.6 %gather_fusion = s32[2,2,2]{2,1,0:T(2,128)S(1)} fusion(s32[2,2,2]{2,1,0:T(2,128)S(1)} %pad_add_fusion, s32[1024]{0:T(1024)S(1)} %pad_clamp_fusion.2), kind=kCustom, calls=%fused_computation | custom fusion | bytes 72 | tf_op jit(solution)/shard_map/jit(_take)/gather | solution.py:19
  15.8 0.2 slice_reduce_fusion
  16.0 0.1 copy.15
  16.1 0.1 reshape.170
  16.2 0.1 copy.20
  16.4 0.1 copy.19
  16.5 0.1 copy.13
  16.6 1.4 %gather_fusion.1 = bf16[4,2,128,256]{3,2,1,0:T(8,128)(2,1)} fusion(bf16[8,2,128,256]{3,2,1,0:T(8,128)(2,1)S(1)} %fusion, s32[1024]{0:T(1024)S(1)} %pad_clamp_fusion.1), kind=kCustom, calls=%fused_computation.1 | custom fusion | bytes 1048592 | tf_op jit(solution)/shard_map/jit(_take)/gather | solution.py:116
  18.0 1.2 %copy_select_fusion.1 = bf16[2,2,2,8,16,256]{5,4,3,1,0,2:T(8,128)(2,1)S(1)} fusion(bf16[2,2,2,8,16,256]{5,4,3,2,1,0:T(8,128)(2,1)} %bitcast.48, pred[2,2]{1,0:T(4,128)(4,1)S(1)} %copy.13), kind=kLoop, calls=%fused_computation.9 | loop fusion | flops 262144 | bytes 1048580 | tf_op jit(solution)/shard_map/jit(_take)/select_n | solution.py:116
  19.2 0.1 maximum_bitcast_fusion.1
  19.3 0.1 maximum_bitcast_fusion
  19.4 1.1 %copy.17 = bf16[2,8,2,2,16,2,256]{6,5,4,3,2,1,0:T(2,128)(2,1)S(1)} copy(bf16[2,8,2,2,16,2,256]{6,4,1,2,0,3,5:T(8,128)(2,1)S(1)} %maximum_bitcast_fusion) | data formatting | bytes 2097152 | tf_op jit(solution)/shard_map/transpose | solution.py:122
  20.5 1.5 %reshape.171 = bf16[2,512,512]{2,1,0:T(8,128)(2,1)} reshape(bf16[2,8,2,2,16,2,256]{6,5,4,3,2,1,0:T(2,128)(2,1)S(1)} %copy.17) | data formatting | bytes 2097152 | tf_op jit(solution)/shard_map/reshape | solution.py:122
  22.0 2.3 %copy.18 = bf16[2,512,512]{1,2,0:T(8,128)(2,1)} copy(bf16[2,512,512]{2,1,0:T(8,128)(2,1)} %reshape.171) | data formatting | bytes 2097152 | tf_op jit(solution)/shard_map/reshape | solution.py:122
  24.3 2.2 %gather_fusion.2 = bf16[4,2,256,256]{3,2,1,0:T(8,128)(2,1)S(1)} fusion(bf16[8,2,256,256]{3,2,1,0:T(8,128)(2,1)} %param.7, s32[1024]{0:T(1024)S(1)} %pad_clamp_fusion), kind=kCustom, calls=%fused_computation.2 | custom fusion | bytes 2097168 | tf_op jit(solution)/shard_map/jit(_take)/gather | solution.py:126
  26.5 1.2 %copy_select_fusion = bf16[2,2,2,16,16,256]{5,4,2,1,3,0:T(8,128)(2,1)} fusion(bf16[2,2,2,16,16,256]{5,4,3,2,1,0:T(8,128)(2,1)S(1)} %bitcast.45, pred[2,2]{1,0:T(4,128)(4,1)S(1)} %copy.19), kind=kLoop, calls=%fused_computation.6 | loop fusion | flops 524288 | bytes 2097156 | tf_op jit(solution)/shard_map/jit(_take)/select_n | solution.py:126
  27.7 3.4 %shard_map.55 = f32[16,8,2,256]{3,2,1,0:T(2,128)} custom-call(bf16[2,256,512]{2,1,0:T(8,128)(2,1)} %bitcast.1.stem_ref, bf16[2,512,512]{2,1,0:T(8,128)(2,1)} %bitcast.47, bf16[2048,256]{1,0:T(8,128)(2,1)} %bitcast.46), custom_call_target="tpu_custom_call" | custom-call | flops 536870912 | bytes 2883584 | tf_op jit(solution)/shard_map/pallas_call | solution.py:96
  (26 shorter events, 0.6 us)
Async XLA Ops:
  0.0 13.6 %copy-start = (bf16[8,2,256,256]{3,2,1,0:T(8,128)(2,1)S(1)}, bf16[8,2,256,256]{3,2,1,0:T(8,128)(2,1)}, u32[]{:S(2)}) copy-start(bf16[8,2,256,256]{3,2,1,0:T(8,128)(2,1)} %param.6) | copy-start | bytes 6291460
  0.0 11.4 %copy-start.1 = (s32[1,2,2]{2,1,0:T(2,128)S(1)}, s32[1,2,2]{2,1,0:T(2,128)}, u32[]{:S(2)}) copy-start(s32[1,2,2]{2,1,0:T(2,128)} %param.8) | copy-start | bytes 52
  0.0 13.3 %copy-start.2 = (s32[256]{0:T(256)S(1)}, s32[256]{0:T(256)}, u32[]{:S(2)}) copy-start(s32[256]{0:T(256)} %param.9) | copy-start | bytes 3076
  2.1 25.5 %all-to-all-start = ((bf16[32,16,512]{2,1,0:T(8,128)(2,1)}), bf16[32,16,512]{2,1,0:T(8,128)(2,1)}, u32[]{:S(2)}, u32[]{:S(2)}) async-start(bf16[32,16,512]{2,1,0:T(8,128)(2,1)} %bitcast), calls=%async_computation | async-start | bytes 1048576 | tf_op jit(solution)/shard_map/all_to_all | solution.py:176
  11.5 3.7 %collective-permute-start = (s32[2,2]{1,0:T(2,128)S(1)}, s32[2,2]{1,0:T(2,128)S(1)}, u32[]{:S(2)}, u32[]{:S(2)}) collective-permute-start(s32[2,2]{1,0:T(2,128)S(1)} %fusion.11), channel_id=1, source_target_pairs={{0,16},{16,0},{1,17},{17,1},{2,18},{18,2},{3,19},{19,3},{4,20},{20... | collective-permute-start | bytes 56 | tf_op jit(solution)/shard_map/ppermute | solution.py:14

commit v22 on v15

--- a/solution.py
+++ b/solution.py
@@ -51,7 +51,7 @@
 
 def regroup_kernel(stem_ref, weight_ref, second_ref, out_ref, real_ref, imag_ref):
     block_count, rows, _ = stem_ref.shape
-    q_local = weight_ref.shape[2] // 64
+    q_local = weight_ref.shape[1] // 64
     t_local = 16
     n_mode = rows // t_local
     lane = lax.broadcasted_iota(jnp.int32, (t_local, 128), 1)
@@ -65,8 +65,9 @@
         )
 
     for b in range(block_count):
-        product = jnp.dot(
-            stem_ref[b], weight_ref[b], preferred_element_type=jnp.float32
+        product = lax.dot_general(
+            stem_ref[b], weight_ref[b], (((1,), (1,)), ((), ())),
+            preferred_element_type=jnp.float32,
         ).astype(jnp.bfloat16)
         for pair in range(n_mode // 2):
             upper = product[(2 * pair) * t_local:(2 * pair + 1) * t_local]
@@ -128,7 +129,7 @@
         second_w = jnp.transpose(second, (0, 3, 1, 2, 4, 5)).reshape(
             block_count * n_mode * group, out_width
         )
-        return regroup(stem_rows, jnp.swapaxes(first_w, 1, 2), second_w, q_local, t_local)
+        return regroup(stem_rows, first_w, second_w, q_local, t_local)
     else:
         second = jnp.take(w2_table, second_ids.reshape(-1), axis=0)
         second = jnp.swapaxes(second, 2, 3)

time: 29.6 us -> 29.6 us (level)
  waiting for transfers between devices: 2.11 us -> 4.38 us
  local copies, waits for them, and re-layouts: 12.1 us -> 9.85 us
    all_to_all x1, waiting for transfers between devices: 2.11 us -> 4.38 us  [on_device(): stem_rows = lax.all_to_all(payload, ('cuts', 'mode'), 0, 0, tiled=True)]
    reshape x2 -> x1, local copies, waits for them, and re-layouts: 3.76 us -> 1.49 us  [stacked_part(): jnp.transpose(first_w, (2, 4, 3, 1, 5, 0, 6))]
  transfers between devices with their start and end apart: 2 -> 2, of which waited for: 1 -> 1; matrix products, arithmetic and copies ran while one was open for 53% -> 46% of each run, Pallas kernels for 0% -> 0%
where the time goes in v22:
time: 29.6 us; the launch traced here: 29.3 us
  local copies, waits for them, and re-layouts  9.85 us (33%)
  starting transfers between devices  8 us (27%)
  waiting for transfers between devices  4.38 us (15%)
  Pallas kernels  3.42 us (12%)
  other arithmetic  2.69 us (9%)
  matrix products  0.81 us (3%)
    all_to_all x1, starting transfers between devices, on_device(): stem_rows = lax.all_to_all(payload, ('cuts', 'mode'), 0, 0, tiled=True)  5.06 us
    all_to_all x1, waiting for transfers between devices, on_device(): stem_rows = lax.all_to_all(payload, ('cuts', 'mode'), 0, 0, tiled=True)  4.38 us
    pallas_call x1, Pallas kernels, regroup(): pl.pallas_call(regroup_kernel, out_shape=out_shape, in_specs=[pl.BlockSpe...  3.42 us
    ppermute x1, starting transfers between devices, gather_over_cuts(): current = lax.ppermute(current, 'cuts', ring)  2.94 us
    gather x1, local copies, waits for them, and re-layouts, stacked_part(): second = jnp.take(w2_table, second_ids.reshape(-1), axis=0)  2.2 us
    broadcast_in_dim x2, local copies, waits for them, and re-layouts, on_device(): payload = jnp.broadcast_to(pieces, (n_cuts, n_mode, t_local, 2 * width))  1.98 us
    reshape x1, local copies, waits for them, and re-layouts, stacked_part(): jnp.transpose(first_w, (2, 4, 3, 1, 5, 0, 6))  1.49 us
    gather x1, local copies, waits for them, and re-layouts, stacked_part(): picked = jnp.take(first_t, first_ids.reshape(-1), axis=0)  1.38 us
  transfers between devices with their start and end apart: 2, of which 1 were waited for; matrix products, arithmetic and copies ran while one was open for 46% of the time, Pallas kernels for 0%

profile of v22, /device:TPU:0, one launch (start us, length us, event | category | flops | bytes accessed | tf_op | source)
XLA Modules:
  0.0 29.3 jit_solution(7784209317499933016)
XLA Ops:
  0.0 2.9 %collective-permute-start = (s32[2,2]{1,0:T(2,128)}, s32[2,2]{1,0:T(2,128)S(1)}, u32[]{:S(2)}, u32[]{:S(2)}) collective-permute-start(s32[2,2]{1,0:T(2,128)} %bitcast.46), channel_id=1, source_target_pairs={{0,16},{16,0},{1,17},{17,1},{2,18},{18,2},{3,19},{19,3},{4,20},{20... | collective-permute-start | bytes 56 | tf_op jit(solution)/shard_map/ppermute | solution.py:14
  2.9 1.1 %broadcast_in_dim.34 = bf16[16,16,512]{2,1,0:T(8,128)(2,1)S(1)} reshape(bf16[1,256,2,256]{3,2,1,0:T(2,128)(2,1)} %param.5) | data formatting | bytes 524288 | tf_op jit(solution)/shard_map/broadcast_in_dim | solution.py:175
  4.1 0.9 %broadcast_in_dim.35 = bf16[2,16,16,512]{3,2,1,0:T(8,128)(2,1)} broadcast(bf16[16,16,512]{2,1,0:T(8,128)(2,1)S(1)} %broadcast_in_dim.34), dimensions={1,2,3} | broadcast | bytes 786432 | tf_op jit(solution)/shard_map/broadcast_in_dim | solution.py:175
  4.9 5.1 %all-to-all-start = ((bf16[32,16,512]{2,1,0:T(8,128)(2,1)}), bf16[32,16,512]{2,1,0:T(8,128)(2,1)}, u32[]{:S(2)}, u32[]{:S(2)}) async-start(bf16[32,16,512]{2,1,0:T(8,128)(2,1)} %bitcast), calls=%async_computation | async-start | bytes 1048576 | tf_op jit(solution)/shard_map/all_to_all | solution.py:177
  10.3 0.1 eq.17
  10.4 0.8 %fusion = bf16[8,2,128,256]{3,2,1,0:T(8,128)(2,1)S(1)} fusion(bf16[8,2,256,256]{3,2,1,0:T(8,128)(2,1)S(1)} %copy-done, s32[128]{0:T(128)S(1)} %eq.17), kind=kOutput, calls=%fused_computation.4 | convolution fusion | flops 268992512 | bytes 3146240 | tf_op jit(solution)/shard_map/nj,spkj->spnk/dot_general | solution.py:198
  11.2 0.6 %gather_fusion = s32[2,2,2]{2,1,0:T(2,128)S(1)} fusion(s32[2,2,2]{2,1,0:T(2,128)S(1)} %pad_add_fusion, s32[1024]{0:T(1024)S(1)} %pad_clamp_fusion.2), kind=kCustom, calls=%fused_computation | custom fusion | bytes 72 | tf_op jit(solution)/shard_map/jit(_take)/gather | solution.py:19
  11.9 0.2 slice_reduce_fusion
  12.1 0.1 copy.15
  12.2 0.1 reshape.164
  12.3 0.1 copy.13
  12.4 1.4 %gather_fusion.1 = bf16[4,2,128,256]{3,2,1,0:T(8,128)(2,1)} fusion(bf16[8,2,128,256]{3,2,1,0:T(8,128)(2,1)S(1)} %fusion, s32[1024]{0:T(1024)S(1)} %pad_clamp_fusion.1), kind=kCustom, calls=%fused_computation.1 | custom fusion | bytes 1048592 | tf_op jit(solution)/shard_map/jit(_take)/gather | solution.py:117
  13.8 1.2 %copy_select_fusion.1 = bf16[2,2,2,8,16,256]{5,4,3,1,0,2:T(8,128)(2,1)S(1)} fusion(bf16[2,2,2,8,16,256]{5,4,3,2,1,0:T(8,128)(2,1)} %bitcast.43, pred[2,2]{1,0:T(4,128)(4,1)S(1)} %copy.13), kind=kLoop, calls=%fused_computation.9 | loop fusion | flops 262144 | bytes 1048580 | tf_op jit(solution)/shard_map/jit(_take)/select_n | solution.py:117
  15.0 0.1 maximum_bitcast_fusion.1
  15.1 0.1 maximum_bitcast_fusion
  15.2 1.1 %copy.17 = bf16[2,8,2,2,16,2,256]{6,5,4,3,2,1,0:T(2,128)(2,1)S(1)} copy(bf16[2,8,2,2,16,2,256]{6,4,1,2,0,3,5:T(8,128)(2,1)S(1)} %maximum_bitcast_fusion) | data formatting | bytes 2097152 | tf_op jit(solution)/shard_map/transpose | solution.py:123
  16.3 1.5 %reshape.165.weight_ref = bf16[2,512,512]{2,1,0:T(8,128)(2,1)} reshape(bf16[2,8,2,2,16,2,256]{6,5,4,3,2,1,0:T(2,128)(2,1)S(1)} %copy.17) | data formatting | bytes 2097152 | tf_op jit(solution)/shard_map/reshape | solution.py:123
  17.8 0.1 copy.18
  17.9 0.1 copy.19
  18.0 0.1 reshape.166
  18.1 2.2 %gather_fusion.2 = bf16[4,2,256,256]{3,2,1,0:T(8,128)(2,1)S(1)} fusion(bf16[8,2,256,256]{3,2,1,0:T(8,128)(2,1)} %param.7, s32[1024]{0:T(1024)S(1)} %pad_clamp_fusion), kind=kCustom, calls=%fused_computation.2 | custom fusion | bytes 2097168 | tf_op jit(solution)/shard_map/jit(_take)/gather | solution.py:127
  20.3 1.2 %copy_select_fusion = bf16[2,2,2,16,16,256]{5,4,2,1,3,0:T(8,128)(2,1)} fusion(bf16[2,2,2,16,16,256]{5,4,3,2,1,0:T(8,128)(2,1)S(1)} %bitcast.41, pred[2,2]{1,0:T(4,128)(4,1)S(1)} %copy.18), kind=kLoop, calls=%fused_computation.6 | loop fusion | flops 524288 | bytes 2097156 | tf_op jit(solution)/shard_map/jit(_take)/select_n | solution.py:127
  21.5 4.4 %all-to-all-done = bf16[32,16,512]{2,1,0:T(8,128)(2,1)} async-done(((bf16[32,16,512]{2,1,0:T(8,128)(2,1)}), bf16[32,16,512]{2,1,0:T(8,128)(2,1)}, u32[]{:S(2)}, u32[]{:S(2)}) %all-to-all-start) | async-done | bytes 524320 | tf_op jit(solution)/shard_map/all_to_all | solution.py:177
  25.9 3.4 %shard_map.55 = f32[16,8,2,256]{3,2,1,0:T(2,128)} custom-call(bf16[2,256,512]{2,1,0:T(8,128)(2,1)} %bitcast.1.stem_ref, bf16[2,512,512]{2,1,0:T(8,128)(2,1)} %reshape.165.weight_ref, bf16[2048,256]{1,0:T(8,128)(2,1)} %bitcast.42), custom_call_target="tpu_custom_call" | custom-call | flops 536870912 | bytes 2883584 | tf_op jit(solution)/shard_map/pallas_call | solution.py:97
  (22 shorter events, 0.4 us)
Async XLA Ops:
  0.0 10.4 %copy-start = (bf16[8,2,256,256]{3,2,1,0:T(8,128)(2,1)S(1)}, bf16[8,2,256,256]{3,2,1,0:T(8,128)(2,1)}, u32[]{:S(2)}) copy-start(bf16[8,2,256,256]{3,2,1,0:T(8,128)(2,1)} %param.6) | copy-start | bytes 6291460
  0.0 10.0 %copy-start.1 = (s32[256]{0:T(256)S(1)}, s32[256]{0:T(256)}, u32[]{:S(2)}) copy-start(s32[256]{0:T(256)} %param.9) | copy-start | bytes 3076
  0.0 11.2 %collective-permute-start = (s32[2,2]{1,0:T(2,128)}, s32[2,2]{1,0:T(2,128)S(1)}, u32[]{:S(2)}, u32[]{:S(2)}) collective-permute-start(s32[2,2]{1,0:T(2,128)} %bitcast.46), channel_id=1, source_target_pairs={{0,16},{16,0},{1,17},{17,1},{2,18},{18,2},{3,19},{19,3},{4,20},{20... | collective-permute-start | bytes 56 | tf_op jit(solution)/shard_map/ppermute | solution.py:14
  4.9 6.3 %copy-start.2 = (s32[1,2,2]{2,1,0:T(2,128)S(1)}, s32[1,2,2]{2,1,0:T(2,128)}, u32[]{:S(2)}) copy-start(s32[1,2,2]{2,1,0:T(2,128)} %param.8) | copy-start | bytes 52
  4.9 20.9 %all-to-all-start = ((bf16[32,16,512]{2,1,0:T(8,128)(2,1)}), bf16[32,16,512]{2,1,0:T(8,128)(2,1)}, u32[]{:S(2)}, u32[]{:S(2)}) async-start(bf16[32,16,512]{2,1,0:T(8,128)(2,1)} %bitcast), calls=%async_computation | async-start | bytes 1048576 | tf_op jit(solution)/shard_map/all_to_all | solution.py:177

commit v23 on v22

--- a/solution.py
+++ b/solution.py
@@ -124,7 +124,11 @@
         block_count, q_local * group, 2 * width
     )
     if group == 64 and t_local == 16 and n_mode % 2 == 0 and q_local % 2 == 0:
-        second = jnp.take(w2_table, second_ids.reshape(-1), axis=0)
+        flat_ids = second_ids.reshape(-1)
+        second = jnp.stack(
+            [lax.dynamic_index_in_dim(w2_table, flat_ids[i], 0, keepdims=False)
+             for i in range(flat_ids.shape[0])]
+        )
         second = second.reshape(block_count, n_cuts, 2, n_mode, a_count, out_width)
         second_w = jnp.transpose(second, (0, 3, 1, 2, 4, 5)).reshape(
             block_count * n_mode * group, out_width

time: 29.6 us -> 32.6 us (1.10)
  between operations: 0.15 us -> 7.72 us
  waiting for transfers between devices: 4.38 us -> 0.01 us
  other arithmetic: 2.69 us -> 1.64 us
  local copies, waits for them, and re-layouts: 9.85 us -> 10.6 us
    all_to_all x1, waiting for transfers between devices: 4.38 us -> 0.01 us  [on_device(): stem_rows = lax.all_to_all(payload, ('cuts', 'mode'), 0, 0, tiled=True)]
    gather x1 -> x0, local copies, waits for them, and re-layouts: 2.2 us -> none  [stacked_part(): second = jnp.take(w2_table, second_ids.reshape(-1), axis=0)]
    dynamic_slice x0 -> x1, local copies, waits for them, and re-layouts: none -> 1.27 us  [stacked_part(): lax.dynamic_index_in_dim(w2_table, flat_ids[i], 0, keepdims=False)]
    select_n x2 -> x0, other arithmetic: 1.18 us -> none  [stacked_part(): second = jnp.take(w2_table, second_ids.reshape(-1), axis=0)]
    reshape x1 -> x2, local copies, waits for them, and re-layouts: 0.08 us -> 1.26 us  [the longest x1 1.18 us: stacked_part(): second = second.reshape(block_count, n_cuts, 2, n_mode, a_count, out_width)]
    slice x0 -> x1, local copies, waits for them, and re-layouts: none -> 0.66 us  [stacked_part(): flat_ids[i]]
  transfers between devices with their start and end apart: 2 -> 2, of which waited for: 1 -> 0; matrix products, arithmetic and copies ran while one was open for 46% -> 41% of each run, Pallas kernels for 0% -> 0%
where the time goes in v23:
time: 32.6 us; the launch traced here: 32.2 us
  local copies, waits for them, and re-layouts  10.6 us (33%)
  starting transfers between devices  8 us (25%)
  between operations  7.72 us (24%)
  Pallas kernels  3.42 us (10%)
  other arithmetic  1.64 us (5%)
  matrix products  0.81 us (2%)
    all_to_all x1, starting transfers between devices, on_device(): stem_rows = lax.all_to_all(payload, ('cuts', 'mode'), 0, 0, tiled=True)  5.06 us
    pallas_call x1, Pallas kernels, regroup(): pl.pallas_call(regroup_kernel, out_shape=out_shape, in_specs=[pl.BlockSpe...  3.42 us
    ppermute x1, starting transfers between devices, gather_over_cuts(): current = lax.ppermute(current, 'cuts', ring)  2.94 us
    broadcast_in_dim x2, local copies, waits for them, and re-layouts, on_device(): payload = jnp.broadcast_to(pieces, (n_cuts, n_mode, t_local, 2 * width))  1.98 us
    reshape x1, local copies, waits for them, and re-layouts, stacked_part(): jnp.transpose(first_w, (2, 4, 3, 1, 5, 0, 6))  1.49 us
    gather x1, local copies, waits for them, and re-layouts, stacked_part(): picked = jnp.take(first_t, first_ids.reshape(-1), axis=0)  1.36 us
    dynamic_slice x1, local copies, waits for them, and re-layouts, stacked_part(): lax.dynamic_index_in_dim(w2_table, flat_ids[i], 0, keepdims=False)  1.27 us
    reshape x1, local copies, waits for them, and re-layouts, stacked_part(): second = second.reshape(block_count, n_cuts, 2, n_mode, a_count, out_width)  1.18 us
  transfers between devices with their start and end apart: 2, of which 0 were waited for; matrix products, arithmetic and copies ran while one was open for 41% of the time, Pallas kernels for 0%

profile of v23, /device:TPU:0, one launch (start us, length us, event | category | flops | bytes accessed | tf_op | source)
XLA Modules:
  0.0 32.2 jit_solution(10916708846107113436)
XLA Ops:
  0.0 2.9 %collective-permute-start = (s32[2,2]{1,0:T(2,128)}, s32[2,2]{1,0:T(2,128)S(1)}, u32[]{:S(2)}, u32[]{:S(2)}) collective-permute-start(s32[2,2]{1,0:T(2,128)} %bitcast.47), channel_id=1, source_target_pairs={{0,16},{16,0},{1,17},{17,1},{2,18},{18,2},{3,19},{19,3},{4,20},{20... | collective-permute-start | bytes 56 | tf_op jit(solution)/shard_map/ppermute | solution.py:14
  2.9 1.1 %broadcast_in_dim.24 = bf16[16,16,512]{2,1,0:T(8,128)(2,1)S(1)} reshape(bf16[1,256,2,256]{3,2,1,0:T(2,128)(2,1)} %param.5) | data formatting | bytes 524288 | tf_op jit(solution)/shard_map/broadcast_in_dim | solution.py:179
  4.1 0.9 %broadcast_in_dim.25 = bf16[2,16,16,512]{3,2,1,0:T(8,128)(2,1)} broadcast(bf16[16,16,512]{2,1,0:T(8,128)(2,1)S(1)} %broadcast_in_dim.24), dimensions={1,2,3} | broadcast | bytes 786432 | tf_op jit(solution)/shard_map/broadcast_in_dim | solution.py:179
  4.9 5.1 %all-to-all-start = ((bf16[32,16,512]{2,1,0:T(8,128)(2,1)}), bf16[32,16,512]{2,1,0:T(8,128)(2,1)}, u32[]{:S(2)}, u32[]{:S(2)}) async-start(bf16[32,16,512]{2,1,0:T(8,128)(2,1)} %bitcast), calls=%async_computation | async-start | bytes 1048576 | tf_op jit(solution)/shard_map/all_to_all | solution.py:181
  10.3 0.1 eq.17
  10.4 0.8 %fusion = bf16[8,2,128,256]{3,2,1,0:T(8,128)(2,1)S(1)} fusion(bf16[8,2,256,256]{3,2,1,0:T(8,128)(2,1)S(1)} %copy-done, s32[128]{0:T(128)S(1)} %eq.17), kind=kOutput, calls=%fused_computation.3 | convolution fusion | flops 268992512 | bytes 3146240 | tf_op jit(solution)/shard_map/nj,spkj->spnk/dot_general | solution.py:202
  11.2 0.6 %gather_fusion = s32[2,2,2]{2,1,0:T(2,128)S(1)} fusion(s32[2,2,2]{2,1,0:T(2,128)S(1)} %pad_add_fusion, s32[1024]{0:T(1024)S(1)} %pad_clamp_fusion.1), kind=kCustom, calls=%fused_computation | custom fusion | bytes 72 | tf_op jit(solution)/shard_map/jit(_take)/gather | solution.py:19
  11.9 0.2 slice_reduce_fusion
  12.1 0.1 copy.17
  12.2 0.1 reshape.132
  12.3 0.7 %fusion.9 = (s32[1]{0:T(128)}, s32[1]{0:T(128)}, s32[1]{0:T(128)}, s32[1]{0:T(128)}) fusion(s32[4]{0:T(128)S(1)} %reshape.132), kind=kLoop, calls=%fused_computation.42 | loop fusion | bytes 32 | tf_op jit(solution)/shard_map/slice | solution.py:129
  18.0 0.1 copy.14
  18.1 0.1 reshape.130
  18.2 0.1 copy.12
  18.3 1.4 %gather_fusion.1 = bf16[4,2,128,256]{3,2,1,0:T(8,128)(2,1)} fusion(bf16[8,2,128,256]{3,2,1,0:T(8,128)(2,1)S(1)} %fusion, s32[1024]{0:T(1024)S(1)} %pad_clamp_fusion), kind=kCustom, calls=%fused_computation.1 | custom fusion | bytes 1048592 | tf_op jit(solution)/shard_map/jit(_take)/gather | solution.py:117
  19.7 1.2 %copy_select_fusion = bf16[2,2,2,8,16,256]{5,4,3,1,0,2:T(8,128)(2,1)S(1)} fusion(bf16[2,2,2,8,16,256]{5,4,3,2,1,0:T(8,128)(2,1)} %bitcast.44, pred[2,2]{1,0:T(4,128)(4,1)S(1)} %copy.12), kind=kLoop, calls=%fused_computation.8 | loop fusion | flops 262144 | bytes 1048580 | tf_op jit(solution)/shard_map/jit(_take)/select_n | solution.py:117
  20.9 0.1 maximum_bitcast_fusion.1
  21.0 0.1 maximum_bitcast_fusion
  21.1 1.1 %copy.16 = bf16[2,8,2,2,16,2,256]{6,5,4,3,2,1,0:T(2,128)(2,1)S(1)} copy(bf16[2,8,2,2,16,2,256]{6,4,1,2,0,3,5:T(8,128)(2,1)S(1)} %maximum_bitcast_fusion) | data formatting | bytes 2097152 | tf_op jit(solution)/shard_map/transpose | solution.py:123
  22.2 1.5 %reshape.131.weight_ref = bf16[2,512,512]{2,1,0:T(8,128)(2,1)} reshape(bf16[2,8,2,2,16,2,256]{6,5,4,3,2,1,0:T(2,128)(2,1)S(1)} %copy.16) | data formatting | bytes 2097152 | tf_op jit(solution)/shard_map/reshape | solution.py:123
  26.2 1.3 %constant_dynamic-slice_fusion.3 = (bf16[1,2,256,256]{3,2,1,0:T(8,128)(2,1)S(1)}, bf16[1,2,256,256]{3,2,1,0:T(8,128)(2,1)S(1)}, bf16[1,2,256,256]{3,2,1,0:T(8,128)(2,1)S(1)}, bf16[1,2,256,256]{3,2,1,0:T(8,128)(2,1)S(1)}) fusion(bf16[8,2,256,256]{3,2,1,0:T(8,128)(2,1)} %param.7, s32[]{:T(128)S(6)} %select_n.85, s32[]{:T(128)S(6)} %select_n.86, ...), kind=kLoop, calls=%fused_computation.36 | loop fusion | bytes 2097168 | tf_op jit(solution)/shard_map/jit(dynamic_index_in_dim)/dynamic_slice | solution.py:129
  27.5 0.1 pad_maximum_fusion
  27.6 1.2 %copy.18 = bf16[2,2,2,16,16,256]{5,4,2,1,3,0:T(8,128)(2,1)} copy(bf16[2,2,2,16,16,256]{5,4,3,2,1,0:T(8,128)(2,1)S(1)} %bitcast.42) | data formatting | bytes 2097152 | tf_op jit(solution)/shard_map/reshape | solution.py:132
  28.8 3.4 %shard_map.55 = f32[16,8,2,256]{3,2,1,0:T(2,128)} custom-call(bf16[2,256,512]{2,1,0:T(8,128)(2,1)} %bitcast.1.stem_ref, bf16[2,512,512]{2,1,0:T(8,128)(2,1)} %reshape.131.weight_ref, bf16[2048,256]{1,0:T(8,128)(2,1)} %bitcast.43), custom_call_target="tpu_custom_call" | custom-call | flops 536870912 | bytes 2883584 | tf_op jit(solution)/shard_map/pallas_call | solution.py:97
  (21 shorter events, 0.4 us)
Async XLA Ops:
  0.0 10.4 %copy-start = (bf16[8,2,256,256]{3,2,1,0:T(8,128)(2,1)S(1)}, bf16[8,2,256,256]{3,2,1,0:T(8,128)(2,1)}, u32[]{:S(2)}) copy-start(bf16[8,2,256,256]{3,2,1,0:T(8,128)(2,1)} %param.6) | copy-start | bytes 6291460
  0.0 10.0 %copy-start.1 = (s32[256]{0:T(256)S(1)}, s32[256]{0:T(256)}, u32[]{:S(2)}) copy-start(s32[256]{0:T(256)} %param.9) | copy-start | bytes 3076
  0.0 11.2 %collective-permute-start = (s32[2,2]{1,0:T(2,128)}, s32[2,2]{1,0:T(2,128)S(1)}, u32[]{:S(2)}, u32[]{:S(2)}) collective-permute-start(s32[2,2]{1,0:T(2,128)} %bitcast.47), channel_id=1, source_target_pairs={{0,16},{16,0},{1,17},{17,1},{2,18},{18,2},{3,19},{19,3},{4,20},{20... | collective-permute-start | bytes 56 | tf_op jit(solution)/shard_map/ppermute | solution.py:14
  4.9 6.3 %copy-start.2 = (s32[1,2,2]{2,1,0:T(2,128)S(1)}, s32[1,2,2]{2,1,0:T(2,128)}, u32[]{:S(2)}) copy-start(s32[1,2,2]{2,1,0:T(2,128)} %param.8) | copy-start | bytes 52
  4.9 23.9 %all-to-all-start = ((bf16[32,16,512]{2,1,0:T(8,128)(2,1)}), bf16[32,16,512]{2,1,0:T(8,128)(2,1)}, u32[]{:S(2)}, u32[]{:S(2)}) async-start(bf16[32,16,512]{2,1,0:T(8,128)(2,1)} %bitcast), calls=%async_computation | async-start | bytes 1048576 | tf_op jit(solution)/shard_map/all_to_all | solution.py:181

commit v24 on v22

--- a/solution.py
+++ b/solution.py
@@ -114,7 +114,7 @@
     width = first_t.shape[3]
     _, _, inner, out_width = w2_table.shape
     group = n_cuts * 2 * a_count
-    picked = jnp.take(first_t, first_ids.reshape(-1), axis=0)
+    picked = first_t if first_ids is None else jnp.take(first_t, first_ids.reshape(-1), axis=0)
     picked = picked.reshape(block_count, n_cuts, 2, q_local, a_count, width)
     real_part, imag_part = picked[:, :, 0], picked[:, :, 1]
     first_w = jnp.stack(
@@ -195,10 +195,11 @@
     if block_count * n_cuts <= 8:
         wanted_t = lax.dynamic_slice_in_dim(perm_grid, me * q_local, q_local, axis=1).T.reshape(-1)
         picker_t = (wanted_t[:, None] == jnp.arange(mid, dtype=jnp.int32)[None, :]).astype(w1_table.dtype)
+        used = jnp.take(w1_table, first_ids.reshape(-1), axis=0)
         first_t = jnp.einsum(
-            "nj,spkj->spnk", picker_t, w1_table, preferred_element_type=jnp.float32
+            "nj,spkj->spnk", picker_t, used, preferred_element_type=jnp.float32
         ).astype(w1_table.dtype)
-        return stacked_part(stem_rows, first_t, w2_table, first_ids, second_ids, sizes)
+        return stacked_part(stem_rows, first_t, w2_table, None, second_ids, sizes)
     else:
         def one_block(index, running):
             stem_one = lax.dynamic_slice_in_dim(stem_rows, index, 1, axis=0)

time: 29.6 us -> 29.7 us (level)
  waiting for transfers between devices: 4.38 us -> 6.6 us
  other arithmetic: 2.69 us -> 0.53 us
    all_to_all x1, waiting for transfers between devices: 4.38 us -> 6.6 us  [on_device(): stem_rows = lax.all_to_all(payload, ('cuts', 'mode'), 0, 0, tiled=True)]
    reshape x1 -> x2, local copies, waits for them, and re-layouts: 0.08 us -> 1.25 us  [the longest x1 1.17 us: stacked_part(): second = second.reshape(block_count, n_cuts, 2, n_mode, a_count, out_width)]
    select_n x2 -> x1, other arithmetic: 1.16 us -> 0.01 us  [on_device(): used = jnp.take(w1_table, first_ids.reshape(-1), axis=0)]
    select_n x2, other arithmetic: 1.18 us -> 0.17 us  [stacked_part(): second = jnp.take(w2_table, second_ids.reshape(-1), axis=0)]
    gather x1, local copies, waits for them, and re-layouts: 1.38 us -> 0.61 us  [on_device(): used = jnp.take(w1_table, first_ids.reshape(-1), axis=0)]
  transfers between devices with their start and end apart: 2 -> 2, of which waited for: 1 -> 1; matrix products, arithmetic and copies ran while one was open for 46% -> 38% of each run, Pallas kernels for 0% -> 0%
where the time goes in v24:
time: 29.7 us; the launch traced here: 29.4 us
  local copies, waits for them, and re-layouts  10 us (34%)
  starting transfers between devices  8.08 us (27%)
  waiting for transfers between devices  6.6 us (22%)
  Pallas kernels  3.42 us (12%)
  matrix products  0.55 us (2%)
  other arithmetic  0.53 us (2%)
    all_to_all x1, waiting for transfers between devices, on_device(): stem_rows = lax.all_to_all(payload, ('cuts', 'mode'), 0, 0, tiled=True)  6.6 us
    all_to_all x1, starting transfers between devices, on_device(): stem_rows = lax.all_to_all(payload, ('cuts', 'mode'), 0, 0, tiled=True)  5.07 us
    pallas_call x1, Pallas kernels, regroup(): pl.pallas_call(regroup_kernel, out_shape=out_shape, in_specs=[pl.BlockSpe...  3.42 us
    ppermute x1, starting transfers between devices, gather_over_cuts(): current = lax.ppermute(current, 'cuts', ring)  3.01 us
    gather x1, local copies, waits for them, and re-layouts, stacked_part(): second = jnp.take(w2_table, second_ids.reshape(-1), axis=0)  2.2 us
    broadcast_in_dim x2, local copies, waits for them, and re-layouts, on_device(): payload = jnp.broadcast_to(pieces, (n_cuts, n_mode, t_local, 2 * width))  1.99 us
    reshape x1, local copies, waits for them, and re-layouts, stacked_part(): jnp.transpose(first_w, (2, 4, 3, 1, 5, 0, 6))  1.48 us
    reshape x1, local copies, waits for them, and re-layouts, stacked_part(): second = second.reshape(block_count, n_cuts, 2, n_mode, a_count, out_width)  1.17 us
  transfers between devices with their start and end apart: 2, of which 1 were waited for; matrix products, arithmetic and copies ran while one was open for 38% of the time, Pallas kernels for 0%

profile of v24, /device:TPU:0, one launch (start us, length us, event | category | flops | bytes accessed | tf_op | source)
XLA Modules:
  0.0 29.4 jit_solution(5923764352373075656)
XLA Ops:
  0.0 3.0 %collective-permute-start = (s32[2,2]{1,0:T(2,128)}, s32[2,2]{1,0:T(2,128)S(1)}, u32[]{:S(2)}, u32[]{:S(2)}) collective-permute-start(s32[2,2]{1,0:T(2,128)} %bitcast.44), channel_id=1, source_target_pairs={{0,16},{16,0},{1,17},{17,1},{2,18},{18,2},{3,19},{19,3},{4,20},{20... | collective-permute-start | bytes 56 | tf_op jit(solution)/shard_map/ppermute | solution.py:14
  3.0 1.1 %broadcast_in_dim.23 = bf16[16,16,512]{2,1,0:T(8,128)(2,1)S(1)} reshape(bf16[1,256,2,256]{3,2,1,0:T(2,128)(2,1)} %param.7) | data formatting | bytes 524288 | tf_op jit(solution)/shard_map/broadcast_in_dim | solution.py:175
  4.1 0.9 %broadcast_in_dim.24 = bf16[2,16,16,512]{3,2,1,0:T(8,128)(2,1)} broadcast(bf16[16,16,512]{2,1,0:T(8,128)(2,1)S(1)} %broadcast_in_dim.23), dimensions={1,2,3} | broadcast | bytes 786432 | tf_op jit(solution)/shard_map/broadcast_in_dim | solution.py:175
  5.0 5.1 %all-to-all-start = ((bf16[32,16,512]{2,1,0:T(8,128)(2,1)}), bf16[32,16,512]{2,1,0:T(8,128)(2,1)}, u32[]{:S(2)}, u32[]{:S(2)}) async-start(bf16[32,16,512]{2,1,0:T(8,128)(2,1)} %bitcast), calls=%async_computation | async-start | bytes 1048576 | tf_op jit(solution)/shard_map/all_to_all | solution.py:177
  10.1 0.1 reshape.101
  10.2 0.1 dynamic-slice_bitcast_fusion
  10.4 0.1 eq.17
  10.5 0.6 %gather_fusion = s32[2,2,2]{2,1,0:T(2,128)S(1)} fusion(s32[2,2,2]{2,1,0:T(2,128)S(1)} %pad_add_fusion, s32[1024]{0:T(1024)S(1)} %pad_clamp_fusion.2), kind=kCustom, calls=%fused_computation.2 | custom fusion | bytes 72 | tf_op jit(solution)/shard_map/jit(_take)/gather | solution.py:19
  11.1 0.2 slice_reduce_fusion
  11.4 0.1 copy.12
  11.5 0.1 reshape.100
  11.6 0.6 %gather_fusion.1 = bf16[4,2,256,256]{3,2,1,0:T(8,128)(2,1)S(1)} fusion(bf16[8,2,256,256]{3,2,1,0:T(8,128)(2,1)S(1)} %copy-done, s32[1024]{0:T(1024)S(1)} %pad_clamp_fusion.1), kind=kCustom, calls=%fused_computation.clone | custom fusion | bytes 2097168 | tf_op jit(solution)/shard_map/jit(_take)/gather | solution.py:198
  12.2 0.5 %convolution_convert_fusion = bf16[4,2,256,128]{2,3,1,0:T(8,128)(2,1)S(1)} fusion(bf16[4,2,256,256]{3,2,1,0:T(8,128)(2,1)S(1)} %gather_fusion.1, pred[4]{0:T(512)(128)(4,1)S(1)} %compare_and_fusion.1, s32[128]{0:T(128)S(1)} %eq.17), kind=kOutput, calls=%fused_computation.3 | convolution fusion | flops 135036928 | bytes 1573380 | tf_op jit(solution)/shard_map/nj,spkj->spnk/dot_general | solution.py:199
  12.8 0.1 maximum_bitcast_fusion.1
  12.9 0.1 maximum_bitcast_fusion
  13.0 1.1 %copy.16 = bf16[2,8,2,2,16,2,256]{6,5,4,3,2,1,0:T(2,128)(2,1)S(1)} copy(bf16[2,8,2,2,16,2,256]{6,4,1,2,0,3,5:T(8,128)(2,1)S(1)} %maximum_bitcast_fusion) | data formatting | bytes 2097152 | tf_op jit(solution)/shard_map/transpose | solution.py:123
  14.1 1.5 %reshape.103.weight_ref = bf16[2,512,512]{2,1,0:T(8,128)(2,1)} reshape(bf16[2,8,2,2,16,2,256]{6,5,4,3,2,1,0:T(2,128)(2,1)S(1)} %copy.16) | data formatting | bytes 2097152 | tf_op jit(solution)/shard_map/reshape | solution.py:123
  15.6 0.1 copy.17
  15.7 0.1 reshape.104
  15.8 2.2 %gather_fusion.2 = bf16[4,2,256,256]{3,2,1,0:T(8,128)(2,1)S(1)} fusion(bf16[8,2,256,256]{3,2,1,0:T(8,128)(2,1)} %param.9, s32[1024]{0:T(1024)S(1)} %pad_clamp_fusion), kind=kCustom, calls=%fused_computation.1.clone | custom fusion | bytes 2097168 | tf_op jit(solution)/shard_map/jit(_take)/gather | solution.py:127
  18.0 0.2 broadcast_select_fusion
  18.2 1.2 %copy.18 = bf16[2,2,2,16,16,256]{5,4,2,1,3,0:T(8,128)(2,1)} copy(bf16[2,2,2,16,16,256]{5,4,3,2,1,0:T(8,128)(2,1)S(1)} %bitcast.38) | data formatting | bytes 2097152 | tf_op jit(solution)/shard_map/reshape | solution.py:128
  19.4 6.6 %all-to-all-done = bf16[32,16,512]{2,1,0:T(8,128)(2,1)} async-done(((bf16[32,16,512]{2,1,0:T(8,128)(2,1)}), bf16[32,16,512]{2,1,0:T(8,128)(2,1)}, u32[]{:S(2)}, u32[]{:S(2)}) %all-to-all-start) | async-done | bytes 524320 | tf_op jit(solution)/shard_map/all_to_all | solution.py:177
  26.0 3.4 %shard_map.55 = f32[16,8,2,256]{3,2,1,0:T(2,128)} custom-call(bf16[2,256,512]{2,1,0:T(8,128)(2,1)} %bitcast.1.stem_ref, bf16[2,512,512]{2,1,0:T(8,128)(2,1)} %reshape.103.weight_ref, bf16[2048,256]{1,0:T(8,128)(2,1)} %bitcast.39), custom_call_target="tpu_custom_call" | custom-call | flops 536870912 | bytes 2883584 | tf_op jit(solution)/shard_map/pallas_call | solution.py:97
  (21 shorter events, 0.3 us)
Async XLA Ops:
  0.0 11.6 %copy-start = (bf16[8,2,256,256]{3,2,1,0:T(8,128)(2,1)S(1)}, bf16[8,2,256,256]{3,2,1,0:T(8,128)(2,1)}, u32[]{:S(2)}) copy-start(bf16[8,2,256,256]{3,2,1,0:T(8,128)(2,1)} %param.8) | copy-start | bytes 6291460
  0.0 10.5 %copy-start.2 = (s32[1,2,2]{2,1,0:T(2,128)S(1)}, s32[1,2,2]{2,1,0:T(2,128)}, u32[]{:S(2)}) copy-start(s32[1,2,2]{2,1,0:T(2,128)} %param.10) | copy-start | bytes 52
  0.0 10.1 %copy-start.1 = (s32[256]{0:T(256)S(1)}, s32[256]{0:T(256)}, u32[]{:S(2)}) copy-start(s32[256]{0:T(256)} %param.11) | copy-start | bytes 3076
  0.0 10.5 %collective-permute-start = (s32[2,2]{1,0:T(2,128)}, s32[2,2]{1,0:T(2,128)S(1)}, u32[]{:S(2)}, u32[]{:S(2)}) collective-permute-start(s32[2,2]{1,0:T(2,128)} %bitcast.44), channel_id=1, source_target_pairs={{0,16},{16,0},{1,17},{17,1},{2,18},{18,2},{3,19},{19,3},{4,20},{20... | collective-permute-start | bytes 56 | tf_op jit(solution)/shard_map/ppermute | solution.py:14
  5.0 21.0 %all-to-all-start = ((bf16[32,16,512]{2,1,0:T(8,128)(2,1)}), bf16[32,16,512]{2,1,0:T(8,128)(2,1)}, u32[]{:S(2)}, u32[]{:S(2)}) async-start(bf16[32,16,512]{2,1,0:T(8,128)(2,1)} %bitcast), calls=%async_computation | async-start | bytes 1048576 | tf_op jit(solution)/shard_map/all_to_all | solution.py:177
